TPU v7x, 256 devices: a whole 4x4x8 slice. The times are simulated.
256 devices in a mesh: req: 64 (over y, z, core), grp: 4 (over x).
Axes of the slice: x: 4, y: 4, z: 8, core: 2. Of those that a mesh axis runs over, the one named last changes fastest.
Arguments:
- hidden_in: bfloat16 [131072, 1280], P(('req', 'grp')), may hold values from -28 to 28
- queries: bfloat16 [131072, 1280], P(('req', 'grp')), may hold values from -20 to 20
- projected_keys: bfloat16 [131072, 320], P(('req', 'grp')), may hold values from -20 to 20
- projected_values: bfloat16 [131072, 320], P(('req', 'grp')), may hold values from -6 to 6
- segment: int32 [64, 4, 512], P('req', 'grp'), may hold values from 0 to 511, as said below
- live_rows: int32 [64, 4], P('req', 'grp'), may hold values from 0 to 512, as said below
- out_weight: bfloat16 [1280, 1280], replicated, may hold values from -0.15625 to 0.15625
- norm_gain: float32 [1280], replicated, may hold values from 0.5 to 1.5
- gate_weight: bfloat16 [1280, 3584], P(None, 'grp'), may hold values from -0.15625 to 0.15625
- up_weight: bfloat16 [1280, 3584], P(None, 'grp'), may hold values from -0.15625 to 0.15625
- down_weight: bfloat16 [3584, 1280], P('grp'), may hold values from -0.09375 to 0.09375
Outputs:
- layer_out: bfloat16 [131072, 1280], P(('req', 'grp'))
Inputs may be any that keep to these rules, and one draw needn't show every extreme that they name: `live_rows`: in each group (one index of grp) the live rows of the 64 owners sum to exactly 8192, and one owner of each group has all 512 slots live. `segment`: within one owner the ids start at 0 at its first slot and rise by 0 or 1 from slot to slot.
All inputs are finite; a program needn't handle non-finite values.
Results may differ from a plain program's by a relative error of at most 0.008.
Values may be sent and summed in bfloat16 or wider, within the bound.
No kernel may reach another device: no remote copies, remote signals or barrier semaphores. Data moves between devices by JAX's collectives and lax.ppermute only.
A program may use at most 128 MiB of HBM per device.

v0:
```python
import math

import jax
import jax.numpy as jnp
from jax import lax
from jax.sharding import PartitionSpec as P

QUERY_HEADS = 20
KEY_VALUE_HEADS = 5
HEAD_SIZE = 64
WINDOW = 128
SINK = 4
BAL = 128


rope_base = 10000.0
norm_eps = 1e-05


def apply_rotary(table, token_position):
    half = table.shape[-1] // 2
    inverse = rope_base ** (-(2.0 * jnp.arange(half, dtype=jnp.float32)) / table.shape[-1])
    angle = token_position.astype(jnp.float32)[:, None] * inverse[None, :]
    cosine = jnp.concatenate([jnp.cos(angle), jnp.cos(angle)], axis=-1)[:, None, :]
    sine = jnp.concatenate([jnp.sin(angle), jnp.sin(angle)], axis=-1)[:, None, :]
    numbers = table.astype(jnp.float32)
    turned = jnp.concatenate([-numbers[..., half:], numbers[..., :half]], axis=-1)
    return numbers * cosine + turned * sine


def attend(queries, projected_keys, projected_values, segment):
    slot_capacity = queries.shape[0]
    slots = jnp.arange(slot_capacity, dtype=jnp.int32)
    begins = jnp.concatenate([jnp.ones((1,), dtype=jnp.bool_), segment[1:] != segment[:-1]])
    starts = lax.cummax(jnp.where(begins, slots, 0), axis=0)
    token_position = slots - starts
    head_group = QUERY_HEADS // KEY_VALUE_HEADS
    query_rotated = (
        apply_rotary(queries.reshape(slot_capacity, QUERY_HEADS, HEAD_SIZE), token_position)
        .astype(jnp.bfloat16)
        .reshape(slot_capacity, KEY_VALUE_HEADS, head_group, HEAD_SIZE)
    )
    key_rotated = apply_rotary(
        projected_keys.reshape(slot_capacity, KEY_VALUE_HEADS, HEAD_SIZE), token_position
    ).astype(jnp.bfloat16)
    scores = jnp.einsum(
        "qngd,knd->ngqk", query_rotated, key_rotated, preferred_element_type=jnp.float32
    ) / math.sqrt(HEAD_SIZE)
    allowed = (segment[:, None] == segment[None, :]) & (slots[None, :] <= slots[:, None])
    allowed = allowed & (
        (slots[:, None] - slots[None, :] < WINDOW) | (token_position[None, :] < SINK)
    )
    scores = jnp.where(allowed, scores, -jnp.inf)
    largest = jnp.max(scores, axis=-1, keepdims=True)
    raised = jnp.exp(scores - largest)
    layer_weights = (raised / jnp.sum(raised, axis=-1, keepdims=True)).astype(jnp.bfloat16)
    attended_context = jnp.einsum(
        "hemz,zhc->mhec",
        layer_weights,
        projected_values.reshape(slot_capacity, KEY_VALUE_HEADS, HEAD_SIZE),
        preferred_element_type=jnp.float32,
    )
    return attended_context.reshape(slot_capacity, QUERY_HEADS * HEAD_SIZE).astype(jnp.bfloat16)


def normalize(rows, norm_gain):
    numbers = rows.astype(jnp.float32)
    factor = lax.rsqrt(jnp.mean(numbers * numbers, axis=-1, keepdims=True) + norm_eps)
    return (numbers * factor * norm_gain[None, :]).astype(jnp.bfloat16)


def project(attended_context, hidden_in, out_weight):
    return (
        hidden_in.astype(jnp.float32)
        + jnp.dot(attended_context, out_weight, preferred_element_type=jnp.float32)
    ).astype(jnp.bfloat16)


def feed_forward(normed, gate_weight, up_weight, down_weight):
    gathered = lax.all_gather(normed, "grp", axis=0, tiled=True)
    gate = jnp.dot(gathered, gate_weight, preferred_element_type=jnp.float32)
    upward = jnp.dot(gathered, up_weight, preferred_element_type=jnp.float32)
    hidden = (jax.nn.silu(gate) * upward).astype(jnp.bfloat16)
    return lax.psum_scatter(
        jnp.dot(hidden, down_weight, preferred_element_type=jnp.float32).astype(jnp.bfloat16),
        "grp",
        scatter_dimension=0,
        tiled=True,
    ).astype(jnp.float32)


def on_device(
    hidden_in,
    queries,
    projected_keys,
    projected_values,
    segment,
    live_rows,
    out_weight,
    norm_gain,
    gate_weight,
    up_weight,
    down_weight,
):
    slot_capacity = hidden_in.shape[0]
    attended_context = attend(
        queries, projected_keys, projected_values, segment.reshape(slot_capacity)
    )
    slots = jnp.arange(slot_capacity, dtype=jnp.int32)
    own_count = live_rows.reshape(())
    request_owners = lax.axis_size("req")
    own_index = lax.axis_index("req")
    block_rows = slot_capacity // request_owners
    counts = lax.all_gather(live_rows.reshape(1), "req", axis=0, tiled=True)
    ends = jnp.cumsum(counts)
    firsts = ends - counts
    owner_ids = jnp.arange(request_owners, dtype=jnp.int32)
    own_first = jnp.sum(jnp.where(owner_ids == own_index, firsts, 0))
    own_shift = own_first % request_owners
    keep = slots < own_count
    stream = jnp.arange(BAL, dtype=jnp.int32) * request_owners + own_index
    source = jnp.sum((ends[None, :] <= stream[:, None]).astype(jnp.int32), axis=1)
    source_first = jnp.sum(
        jnp.where(source[:, None] == owner_ids[None, :], firsts[None, :], 0), axis=1
    )
    pick = (stream - source_first) // request_owners * request_owners + source
    rows = project(attended_context, hidden_in, out_weight)
    kept = jnp.where(keep[:, None], rows, jnp.zeros_like(rows))
    arrived = lax.all_to_all(
        jnp.roll(kept.reshape(block_rows, request_owners, rows.shape[1]), own_shift, axis=1),
        "req",
        split_axis=1,
        concat_axis=1,
        tiled=True,
    )
    mixed = arrived.reshape(slot_capacity, -1)[pick]
    normed = normalize(mixed, norm_gain)
    result = (
        mixed.astype(jnp.float32) + feed_forward(normed, gate_weight, up_weight, down_weight)
    ).astype(jnp.bfloat16)
    lanes = (own_index - firsts) % request_owners
    source_row = jnp.arange(block_rows, dtype=jnp.int32)[:, None] * request_owners + lanes[None, :]
    valid = source_row < counts[None, :]
    target = jnp.where(valid, (firsts[None, :] + source_row) // request_owners, 0)
    outgoing = jnp.where(valid[:, :, None], result[target], jnp.zeros((), jnp.bfloat16))
    returned = lax.all_to_all(outgoing, "req", split_axis=1, concat_axis=1, tiled=True)
    return jnp.roll(returned, -own_shift, axis=1).reshape(slot_capacity, -1)


def solution(mesh):
    placed = (
        P(("req", "grp"), None),
        P(("req", "grp"), None),
        P(("req", "grp"), None),
        P(("req", "grp"), None),
        P("req", "grp", None),
        P("req", "grp"),
        P(),
        P(),
        P(None, "grp"),
        P(None, "grp"),
        P("grp", None),
    )
    return jax.shard_map(
        on_device, mesh=mesh, in_specs=placed, out_specs=P(("req", "grp"), None), check_vma=False
    )
```

profile of v0, /device:TPU:1, one launch (start us, length us, event | category | flops | bytes accessed | tf_op | source)
XLA Modules:
  0.0 261.3 jit_solution(14430940369988425500)
XLA Ops:
  7.3 1.4 dynamic-slice
  8.8 0.7 bitcast_dynamic-update-slice_fusion
  9.5 21.0 %all-reduce = s32[64]{0:T(128)S(1)} all-reduce(s32[64]{0:T(128)S(1)} %bitcast_dynamic-update-slice_fusion), channel_id=2, replica_groups=mesh['req'=64,'grp'=4] {'req'}, use_global_device_ids=true, to_apply=%add | all-reduce | flops 64 | bytes 512 | tf_op jit(solution)/shard_map/all_gather | solution.py:114
  30.4 0.1 copy.45
  30.5 0.1 reduce-window.19
  30.6 0.1 reduce
  30.7 0.6 copy-done.6
  31.3 0.6 fusion.35
  33.9 0.5 multiply_power_fusion
  34.5 0.8 compare_reduce_fusion
  35.4 0.3 reduce-window.20
  35.8 0.1 slice_reduce_fusion
  35.9 0.7 fusion.34
  36.7 1.7 slice.40
  38.4 1.9 convert.3
  40.3 2.4 copy.47
  42.7 1.7 convert_element_type.96
  44.4 1.8 slice_negate_fusion
  46.2 0.6 copy-done.1
  46.8 0.8 slice_negate_fusion.1
  47.6 0.5 iota_compare_fusion.2
  48.1 0.3 fusion.16
  48.4 0.3 multiply_cosine_fusion
  48.7 0.7 pad_maximum_fusion
  49.4 13.7 %fusion.41 = (f32[5,4,512]{2,1,0:T(4,128)}, f32[5,4,512,512]{2,3,1,0:T(8,128)}) fusion(pred[512,512]{0,1:T(8,128)(4,1)S(1)} %fusion.16, f32[512,5,4,32]{0,3,2,1:T(8,128)} %bitcast.78, f32[512,5,4,32]{0,3,2,1:T(8,128)} %bitcast.77, f32[512,5,4,64]{0,3,2,1:T(8,128)} %bitcast.75, f32[512,64]{0,1:T(8,128)} %get-tuple-element.15, ...), kind=kOutput, calls=%fused_computation.101 | convolution fusion | flops 696320512 | bytes 27762688 | tf_op jit(solution)/shard_map/sub | solution.py:55
  63.2 9.0 %fusion.12 = bf16[5,4,512,64]{2,3,1,0:T(8,128)(2,1)S(1)} fusion(bf16[512,5,64,1]{0,2,3,1:T(8,128)(2,1)} %bitcast.85, f32[5,4,512,512]{2,3,1,0:T(8,128)} %get-tuple-element.13, f32[5,4,512]{2,1,0:T(4,128)} %get-tuple-element.12), kind=kOutput, calls=%fused_computation.24 | convolution fusion | flops 682229760 | bytes 22650880 | tf_op jit(solution)/shard_map/hemz,zhc->mhec/dot_general | solution.py:57
  72.2 2.0 fusion.7
  74.2 1.8 copy.49
  76.0 2.9 %fusion.14 = bf16[8,64,1280]{2,0,1:T(8,128)(2,1)} fusion(s32[]{:T(128)S(6)} %select_n.118, bf16[8,64,1280]{2,0,1:T(8,128)(2,1)} %copy.49), kind=kLoop, calls=%fused_computation.26 | loop fusion | flops 655360 | bytes 2621444 | tf_op jit(solution)/shard_map/jit(_roll_dynamic)/concatenate | solution.py:130
  78.9 9.6 %all-to-all-start = ((bf16[8,64,1280]{2,0,1:T(8,128)(2,1)}), bf16[8,64,1280]{2,0,1:T(8,128)(2,1)}, u32[]{:S(2)}, u32[]{:S(2)}) async-start(bf16[8,64,1280]{2,0,1:T(8,128)(2,1)} %fusion.14), calls=%async_computation | async-start | bytes 2621440 | tf_op jit(solution)/shard_map/all_to_all | solution.py:129
  88.5 0.2 all-gather.3.cloned.1.call-start
  88.9 33.7 %all-to-all-done = bf16[8,64,1280]{2,0,1:T(8,128)(2,1)} async-done(((bf16[8,64,1280]{2,0,1:T(8,128)(2,1)}), bf16[8,64,1280]{2,0,1:T(8,128)(2,1)}, u32[]{:S(2)}, u32[]{:S(2)}) %all-to-all-start) | async-done | bytes 1310752 | tf_op jit(solution)/shard_map/all_to_all | solution.py:129
  122.6 2.6 copy.51
  125.2 3.4 %gather_fusion = bf16[128,1280]{1,0:T(8,128)(2,1)} fusion(bf16[512,1280]{1,0:T(8,128)(2,1)} %bitcast.73, s32[1024]{0:T(1024)S(1)} %pad_clamp_fusion.1), kind=kCustom, calls=%fused_computation | custom fusion | bytes 655872 | tf_op jit(solution)/shard_map/gather | solution.py:136
  128.5 1.1 fusion.18
  129.7 1.8 fusion.20
  131.6 23.2 %all-gather.3.cloned.1.call-done = bf16[512,1280]{1,0:T(8,128)(2,1)} async-done(((bf16[128,1280]{1,0:T(8,128)(2,1)}), bf16[512,1280]{1,0:T(8,128)(2,1)}) %all-gather.3.cloned.1.call-update) | async-done | bytes 1310736 | tf_op jit(solution)/shard_map/all_gather | solution.py:80
  154.8 4.8 %fusion.48 = f32[512,896]{1,0:T(8,128)} fusion(bf16[512,1280]{1,0:T(8,128)(2,1)} %all-gather.3.cloned.1.call-done, bf16[1280,896]{1,0:T(8,128)(2,1)} %param.21), kind=kOutput, calls=%fused_computation.102 | convolution fusion | flops 1174405120 | bytes 5439488 | tf_op jit(solution)/shard_map/dot_general | solution.py:81
  159.6 7.3 %convolution_convert_fusion = bf16[512,1280]{1,0:T(8,128)(2,1)} fusion(bf16[896,1280]{1,0:T(8,128)(2,1)} %param.23, f32[512,896]{1,0:T(8,128)} %fusion.48, bf16[512,1280]{1,0:T(8,128)(2,1)} %all-gather.3.cloned.1.call-done, bf16[1280,896]{1,0:T(8,128)(2,1)} %param.22), kind=kOutput, calls=%fused_computation.13 | convolution fusion | flops 2352218112 | bytes 9043968 | tf_op jit(solution)/shard_map/dot_general | solution.py:85
  167.2 0.1 copy.46
  167.3 26.4 %reduce-scatter.2.cloned.1.call-done = bf16[128,1280]{1,0:T(8,128)(2,1)} async-done(((bf16[512,1280]{1,0:T(8,128)(2,1)}), bf16[128,1280]{1,0:T(8,128)(2,1)}) %reduce-scatter.2.cloned.1.call-update) | async-done | bytes 327696 | tf_op jit(solution)/shard_map/reduce_scatter | solution.py:84
  193.8 1.9 fusion.21
  195.7 4.9 %gather_fusion.1 = bf16[512,1280]{1,0:T(8,128)(2,1)} fusion(bf16[128,1280]{1,0:T(8,128)(2,1)} %fusion.21, s32[1024]{0:T(1024)S(1)} %pad_clamp_fusion), kind=kCustom, calls=%fused_computation.1 | custom fusion | bytes 2623488 | tf_op jit(solution)/shard_map/gather | solution.py:145
  200.6 3.2 %copy_select_fusion = bf16[8,64,1280]{2,0,1:T(8,128)(2,1)} fusion(bf16[8,64,1280]{2,1,0:T(8,128)(2,1)} %bitcast.76, pred[8,64]{0,1:T(8,128)(4,1)S(1)} %copy.46), kind=kLoop, calls=%fused_computation.28 | loop fusion | flops 655360 | bytes 2621952 | tf_op jit(solution)/shard_map/jit(_where)/select_n | solution.py:145
  203.8 13.2 %all-to-all-start.1 = ((bf16[8,64,1280]{2,0,1:T(8,128)(2,1)}), bf16[8,64,1280]{2,0,1:T(8,128)(2,1)}, u32[]{:S(2)}, u32[]{:S(2)}) async-start(bf16[8,64,1280]{2,0,1:T(8,128)(2,1)} %copy_select_fusion), calls=%async_computation.2 | async-start | bytes 2621440 | tf_op jit(solution)/shard_map/all_to_all | solution.py:146
  217.0 34.1 %all-to-all-done.1 = bf16[8,64,1280]{2,0,1:T(8,128)(2,1)} async-done(((bf16[8,64,1280]{2,0,1:T(8,128)(2,1)}), bf16[8,64,1280]{2,0,1:T(8,128)(2,1)}, u32[]{:S(2)}, u32[]{:S(2)}) %all-to-all-start.1) | async-done | bytes 1310752 | tf_op jit(solution)/shard_map/all_to_all | solution.py:146
  251.0 1.5 copy.53
  252.6 1.9 fusion.13
  (40 shorter events, 0.9 us)
Async XLA Ops:
  6.5 65.7 %copy-start = (bf16[1280,1280]{1,0:T(8,128)(2,1)S(1)}, bf16[1280,1280]{1,0:T(8,128)(2,1)}, u32[]{:S(2)}) copy-start(bf16[1280,1280]{1,0:T(8,128)(2,1)} %param.19) | copy-start | bytes 9830404
  30.7 0.6 copy-start.6
  44.4 2.4 copy-start.1
  44.4 2.4 copy-start.2
  44.4 3.7 %copy-start.3 = (s32[1,1,512]{2,1,0:T(1,128)S(1)}, s32[1,1,512]{2,1,0:T(1,128)}, u32[]{:S(2)}) copy-start(s32[1,1,512]{2,1,0:T(1,128)} %param.17) | copy-start | bytes 6148
  44.4 3.7 %copy-start.5 = (pred[512]{0:T(512)(128)(4,1)S(1)}, pred[512]{0:T(512)(128)(4,1)}, u32[]{:S(2)}) copy-start(pred[512]{0:T(512)(128)(4,1)} %fusion.34) | copy-start | bytes 1540
  44.4 4.0 %copy-start.8 = (f32[32]{0:T(128)S(1)}, f32[32]{0:T(128)}, u32[]{:S(2)}) copy-start(f32[32]{0:T(128)} %multiply_power_fusion) | copy-start | bytes 388
  63.2 9.0 %copy-start.9 = (bf16[512,1280]{1,0:T(8,128)(2,1)S(1)}, bf16[512,1280]{1,0:T(8,128)(2,1)}, u32[]{:S(2)}) copy-start(bf16[512,1280]{1,0:T(8,128)(2,1)} %param.13) | copy-start | bytes 3932164
  63.2 9.0 %copy-start.10 = (pred[512]{0:T(512)(128)(4,1)S(1)}, pred[512]{0:T(512)(128)(4,1)}, u32[]{:S(2)}) copy-start(pred[512]{0:T(512)(128)(4,1)} %iota_compare_fusion.2) | copy-start | bytes 1540
  78.9 9.9 %copy-start.7 = (s32[64]{0:T(128)S(1)}, s32[64]{0:T(128)}, u32[]{:S(2)}) copy-start(s32[64]{0:T(128)} %copy-done.6) | copy-start | bytes 772
  78.9 43.7 %all-to-all-start = ((bf16[8,64,1280]{2,0,1:T(8,128)(2,1)}), bf16[8,64,1280]{2,0,1:T(8,128)(2,1)}, u32[]{:S(2)}, u32[]{:S(2)}) async-start(bf16[8,64,1280]{2,0,1:T(8,128)(2,1)} %fusion.14), calls=%async_computation | async-start | bytes 2621440 | tf_op jit(solution)/shard_map/all_to_all | solution.py:129
  88.5 66.3 %all-gather.3.cloned.1.call-start = ((), (), s32[]{:S(2)}) async-start(), calls=%async_computation.3 | async-start | bytes 1638400 | tf_op jit(solution)/shard_map/all_gather | solution.py:80
  125.2 4.5 %copy-start.4 = (f32[1280]{0:T(1024)S(1)}, f32[1280]{0:T(1024)}, u32[]{:S(2)}) copy-start(f32[1280]{0:T(1024)} %param.20) | copy-start | bytes 15364
  131.5 62.2 %reduce-scatter.2.cloned.1.call-start = ((), (), s32[]{:S(2)}) async-start(), calls=%async_computation.4 | async-start | bytes 1638400 | tf_op jit(solution)/shard_map/reduce_scatter | solution.py:84
  203.8 47.3 %all-to-all-start.1 = ((bf16[8,64,1280]{2,0,1:T(8,128)(2,1)}), bf16[8,64,1280]{2,0,1:T(8,128)(2,1)}, u32[]{:S(2)}, u32[]{:S(2)}) async-start(bf16[8,64,1280]{2,0,1:T(8,128)(2,1)} %copy_select_fusion), calls=%async_computation.2 | async-start | bytes 2621440 | tf_op jit(solution)/shard_map/all_to_all | solution.py:146
Sparse Core Ops, SparseCore 0:
  131.7 23.0 all-gather.2
  167.1 26.6 reduce-scatter.1
where the time goes:
time: 262 us; the launch traced here: 261 us
  waiting for transfers between devices  117 us (45%)
  matrix products  36.9 us (14%)
  other arithmetic  24.6 us (9%)
  starting transfers between devices  23 us (9%)
  local copies, waits for them, and re-layouts  22.1 us (8%)
  blocking collectives  21 us (8%)
  between operations  16.4 us (6%)
    all_to_all x1, waiting for transfers between devices, on_device(): lax.all_to_all(outgoing, 'req', split_axis=1, concat_axis=1, tiled=True)  34.1 us
    all_to_all x1, waiting for transfers between devices, on_device(): lax.all_to_all(jnp.roll(kept.reshape(block_rows, request_owners, rows.sha...  33.7 us
    reduce_scatter x1, waiting for transfers between devices, feed_forward(): lax.psum_scatter(jnp.dot(hidden, down_weight, preferred_element_type=jnp....  26.4 us
    all_gather x1, waiting for transfers between devices, feed_forward(): gathered = lax.all_gather(normed, 'grp', axis=0, tiled=True)  23.2 us
    all_gather x1, blocking collectives, on_device(): counts = lax.all_gather(live_rows.reshape(1), 'req', axis=0, tiled=True)  21 us
    sub x1, matrix products, attend(): raised = jnp.exp(scores - largest)  13.7 us
    all_to_all x1, starting transfers between devices, on_device(): lax.all_to_all(outgoing, 'req', split_axis=1, concat_axis=1, tiled=True)  13.2 us
    all_to_all x1, starting transfers between devices, on_device(): lax.all_to_all(jnp.roll(kept.reshape(block_rows, request_owners, rows.sha...  9.55 us
  transfers between devices with their start and end apart: 4, of which 4 were waited for; matrix products, arithmetic and copies ran while one was open for 0% of the time, Pallas kernels for 0%

commit v1 on v0

--- a/solution.py
+++ b/solution.py
@@ -3,6 +3,8 @@
 import jax
 import jax.numpy as jnp
 from jax import lax
+from jax.experimental import pallas as pl
+from jax.experimental.pallas import tpu as pltpu
 from jax.sharding import PartitionSpec as P
 
 QUERY_HEADS = 20
@@ -15,17 +17,75 @@
 
 rope_base = 10000.0
 norm_eps = 1e-05
-
-
-def apply_rotary(table, token_position):
-    half = table.shape[-1] // 2
-    inverse = rope_base ** (-(2.0 * jnp.arange(half, dtype=jnp.float32)) / table.shape[-1])
+LANES = 128
+
+
+def rotation_tables(token_position):
+    half = HEAD_SIZE // 2
+    inverse = rope_base ** (-(2.0 * jnp.arange(half, dtype=jnp.float32)) / HEAD_SIZE)
     angle = token_position.astype(jnp.float32)[:, None] * inverse[None, :]
-    cosine = jnp.concatenate([jnp.cos(angle), jnp.cos(angle)], axis=-1)[:, None, :]
-    sine = jnp.concatenate([jnp.sin(angle), jnp.sin(angle)], axis=-1)[:, None, :]
-    numbers = table.astype(jnp.float32)
-    turned = jnp.concatenate([-numbers[..., half:], numbers[..., :half]], axis=-1)
-    return numbers * cosine + turned * sine
+    reps = LANES // half
+    return jnp.tile(jnp.cos(angle), (1, reps)), jnp.tile(jnp.sin(angle), (1, reps))
+
+
+def half_turn_matrix():
+    lane = jnp.arange(LANES, dtype=jnp.int32)
+    local = lane % HEAD_SIZE
+    half = HEAD_SIZE // 2
+    src = jnp.where(local < half, lane + half, lane - half)
+    sign = jnp.where(local < half, -1.0, 1.0)
+    turn = jnp.where(lane[:, None] == src[None, :], sign[None, :], 0.0)
+    return turn.astype(jnp.bfloat16)
+
+
+def attention_kernel(q_ref, k_ref, v_ref, cos_ref, sin_ref, turn_ref, segc_ref, segr_ref, posr_ref, out_ref, bias_ref):
+    slots = q_ref.shape[0]
+    block = LANES
+
+    @pl.when(pl.program_id(0) == 0)
+    def _():
+        qi = lax.broadcasted_iota(jnp.int32, (slots, slots), 0)
+        ki = lax.broadcasted_iota(jnp.int32, (slots, slots), 1)
+        allowed = (segc_ref[...] == segr_ref[...]) & (ki <= qi)
+        allowed = allowed & ((qi - ki < WINDOW) | (posr_ref[...] < SINK))
+        bias_ref[...] = jnp.where(allowed, 0.0, -jnp.inf).astype(jnp.float32)
+
+    cosine = cos_ref[...]
+    sine = sin_ref[...]
+    turn = turn_ref[...]
+
+    def rotate(x):
+        turned = jnp.dot(x, turn, preferred_element_type=jnp.float32)
+        return (x.astype(jnp.float32) * cosine + turned * sine).astype(jnp.bfloat16)
+
+    q_rot = rotate(q_ref[...])
+    k_rot = rotate(k_ref[...])
+    v = v_ref[...]
+    lane = lax.broadcasted_iota(jnp.int32, (1, LANES), 1)
+    low = lane < HEAD_SIZE
+    zero = jnp.zeros((), jnp.bfloat16)
+    q_low = jnp.where(low, q_rot, zero)
+    q_high = jnp.where(low, zero, q_rot)
+    scale = 1.0 / math.sqrt(HEAD_SIZE)
+    for i in range(slots // block):
+        keys = block * (i + 1)
+        k_part = k_rot[:keys]
+        v_part = v[:keys]
+        bias = bias_ref[i * block:(i + 1) * block, :keys]
+        parts = []
+        for qh in (q_low, q_high):
+            scores = lax.dot_general(
+                qh[i * block:(i + 1) * block], k_part, (((1,), (1,)), ((), ())),
+                preferred_element_type=jnp.float32,
+            )
+            scores = scores * scale + bias
+            largest = jnp.max(scores, axis=-1, keepdims=True)
+            raised = jnp.exp(scores - largest)
+            total = jnp.sum(raised, axis=-1, keepdims=True)
+            weights = (raised * (1.0 / total)).astype(jnp.bfloat16)
+            parts.append(jnp.dot(weights, v_part, preferred_element_type=jnp.float32))
+        context = jnp.where(low, parts[0], parts[1])
+        out_ref[i * block:(i + 1) * block, :] = context.astype(out_ref.dtype)
 
 
 def attend(queries, projected_keys, projected_values, segment):
@@ -34,33 +94,40 @@
     begins = jnp.concatenate([jnp.ones((1,), dtype=jnp.bool_), segment[1:] != segment[:-1]])
     starts = lax.cummax(jnp.where(begins, slots, 0), axis=0)
     token_position = slots - starts
-    head_group = QUERY_HEADS // KEY_VALUE_HEADS
-    query_rotated = (
-        apply_rotary(queries.reshape(slot_capacity, QUERY_HEADS, HEAD_SIZE), token_position)
-        .astype(jnp.bfloat16)
-        .reshape(slot_capacity, KEY_VALUE_HEADS, head_group, HEAD_SIZE)
-    )
-    key_rotated = apply_rotary(
-        projected_keys.reshape(slot_capacity, KEY_VALUE_HEADS, HEAD_SIZE), token_position
-    ).astype(jnp.bfloat16)
-    scores = jnp.einsum(
-        "qngd,knd->ngqk", query_rotated, key_rotated, preferred_element_type=jnp.float32
-    ) / math.sqrt(HEAD_SIZE)
-    allowed = (segment[:, None] == segment[None, :]) & (slots[None, :] <= slots[:, None])
-    allowed = allowed & (
-        (slots[:, None] - slots[None, :] < WINDOW) | (token_position[None, :] < SINK)
-    )
-    scores = jnp.where(allowed, scores, -jnp.inf)
-    largest = jnp.max(scores, axis=-1, keepdims=True)
-    raised = jnp.exp(scores - largest)
-    layer_weights = (raised / jnp.sum(raised, axis=-1, keepdims=True)).astype(jnp.bfloat16)
-    attended_context = jnp.einsum(
-        "hemz,zhc->mhec",
-        layer_weights,
-        projected_values.reshape(slot_capacity, KEY_VALUE_HEADS, HEAD_SIZE),
-        preferred_element_type=jnp.float32,
-    )
-    return attended_context.reshape(slot_capacity, QUERY_HEADS * HEAD_SIZE).astype(jnp.bfloat16)
+    cosine, sine = rotation_tables(token_position)
+    turn = half_turn_matrix()
+    def doubled(x):
+        x = x.reshape(slot_capacity, KEY_VALUE_HEADS, 1, HEAD_SIZE)
+        x = jnp.broadcast_to(x, (slot_capacity, KEY_VALUE_HEADS, 2, HEAD_SIZE))
+        return x.reshape(slot_capacity, KEY_VALUE_HEADS * 2 * HEAD_SIZE)
+    keys2 = doubled(projected_keys)
+    values2 = doubled(projected_values)
+    tiles = QUERY_HEADS * HEAD_SIZE // LANES
+    per_kv = tiles // KEY_VALUE_HEADS
+    full = lambda t: (0, 0)
+    return pl.pallas_call(
+        attention_kernel,
+        grid=(tiles,),
+        in_specs=[
+            pl.BlockSpec((slot_capacity, LANES), lambda t: (0, t)),
+            pl.BlockSpec((slot_capacity, LANES), lambda t: (0, t // per_kv)),
+            pl.BlockSpec((slot_capacity, LANES), lambda t: (0, t // per_kv)),
+            pl.BlockSpec((slot_capacity, LANES), full),
+            pl.BlockSpec((slot_capacity, LANES), full),
+            pl.BlockSpec((LANES, LANES), full),
+            pl.BlockSpec((slot_capacity, 1), full),
+            pl.BlockSpec((1, slot_capacity), full),
+            pl.BlockSpec((1, slot_capacity), full),
+        ],
+        out_specs=pl.BlockSpec((slot_capacity, LANES), lambda t: (0, t)),
+        out_shape=jax.ShapeDtypeStruct((slot_capacity, QUERY_HEADS * HEAD_SIZE), jnp.bfloat16),
+        scratch_shapes=[pltpu.VMEM((slot_capacity, slot_capacity), jnp.float32)],
+        compiler_params=pltpu.CompilerParams(dimension_semantics=("arbitrary",)),
+    )(
+        queries, keys2, values2, cosine, sine, turn,
+        segment.reshape(slot_capacity, 1), segment.reshape(1, slot_capacity),
+        token_position.reshape(1, slot_capacity),
+    )
 
 
 def normalize(rows, norm_gain):
@@ -111,7 +178,9 @@
     request_owners = lax.axis_size("req")
     own_index = lax.axis_index("req")
     block_rows = slot_capacity // request_owners
-    counts = lax.all_gather(live_rows.reshape(1), "req", axis=0, tiled=True)
+    counts = lax.all_to_all(
+        jnp.broadcast_to(live_rows.reshape(1, 1), (request_owners, LANES)), "req", 0, 0, tiled=True
+    )[:, 0]
     ends = jnp.cumsum(counts)
     firsts = ends - counts
     owner_ids = jnp.arange(request_owners, dtype=jnp.int32)

time: 262 us -> 264 us (level)
  Pallas kernels: 0 us -> 29.4 us
  blocking collectives: 21 us -> 0 us
  matrix products: 36.9 us -> 16.8 us
  starting transfers between devices: 23 us -> 37.3 us
  other arithmetic: 24.6 us -> 17 us
  local copies, waits for them, and re-layouts: 22.1 us -> 28.9 us
    pallas_call x0 -> x1, Pallas kernels: none -> 29.4 us  [attend(): pl.pallas_call(attention_kernel, grid=(tiles,), in_specs=[pl.BlockSpec((s...]
    all_gather x1 -> x0, blocking collectives: 21 us -> none  [on_device(): counts = lax.all_gather(live_rows.reshape(1), 'req', axis=0, tiled=True)]
    sub x1 -> x0, matrix products: 13.7 us -> none  [attend(): raised = jnp.exp(scores - largest)]
    all_to_all x0 -> x1, starting transfers between devices: none -> 13.3 us  [on_device(): lax.all_to_all(jnp.broadcast_to(live_rows.reshape(1, 1), (request_owners,...]
    dot_general x1 -> x0, matrix products: 9 us -> none  [attend(): jnp.einsum('hemz,zhc->mhec', layer_weights, projected_values.reshape(slot...]
    unnamed x27 -> x6, local copies, waits for them, and re-layouts: 5.83 us -> 0.01 us
    broadcast_in_dim x0 -> x3, local copies, waits for them, and re-layouts: none -> 4.37 us  [the longest x2 3.75 us: doubled(): x = jnp.broadcast_to(x, (slot_capacity, KEY_VALUE_HEADS, 2, HEAD_SIZE))]
    reshape x0 -> x2, local copies, waits for them, and re-layouts: none -> 4.34 us  [doubled(): return x.reshape(slot_capacity, KEY_VALUE_HEADS * 2 * HEAD_SIZE)]
  transfers between devices with their start and end apart: 4 -> 5, of which waited for: 4 -> 4; matrix products, arithmetic and copies ran while one was open for 0% -> 9% of each run, Pallas kernels for 0% -> 11%
where the time goes in v1:
time: 264 us; the launch traced here: 263 us
  waiting for transfers between devices  117 us (44%)
  starting transfers between devices  37.3 us (14%)
  Pallas kernels  29.4 us (11%)
  local copies, waits for them, and re-layouts  28.9 us (11%)
  other arithmetic  17 us (6%)
  matrix products  16.8 us (6%)
  between operations  16.5 us (6%)
    all_to_all x1, waiting for transfers between devices, on_device(): lax.all_to_all(outgoing, 'req', split_axis=1, concat_axis=1, tiled=True)  34.1 us
    all_to_all x1, waiting for transfers between devices, on_device(): lax.all_to_all(jnp.roll(kept.reshape(block_rows, request_owners, rows.sha...  33.8 us
    pallas_call x1, Pallas kernels, attend(): pl.pallas_call(attention_kernel, grid=(tiles,), in_specs=[pl.BlockSpec((s...  29.4 us
    reduce_scatter x1, waiting for transfers between devices, feed_forward(): lax.psum_scatter(jnp.dot(hidden, down_weight, preferred_element_type=jnp....  26.4 us
    all_gather x1, waiting for transfers between devices, feed_forward(): gathered = lax.all_gather(normed, 'grp', axis=0, tiled=True)  22.9 us
    all_to_all x1, starting transfers between devices, on_device(): lax.all_to_all(jnp.broadcast_to(live_rows.reshape(1, 1), (request_owners,...  13.3 us
    all_to_all x1, starting transfers between devices, on_device(): lax.all_to_all(outgoing, 'req', split_axis=1, concat_axis=1, tiled=True)  13.2 us
    all_to_all x1, starting transfers between devices, on_device(): lax.all_to_all(jnp.roll(kept.reshape(block_rows, request_owners, rows.sha...  10.5 us
  transfers between devices with their start and end apart: 5, of which 4 were waited for; matrix products, arithmetic and copies ran while one was open for 9% of the time, Pallas kernels for 11%

profile of v1, /device:TPU:1, one launch (start us, length us, event | category | flops | bytes accessed | tf_op | source)
XLA Modules:
  0.0 263.1 jit_solution(18181725226804988256)
XLA Ops:
  7.3 0.6 broadcast_in_dim.104
  8.0 13.3 %all-to-all-start = ((s32[64,1,128]{2,1,0:T(1,128)}), s32[64,1,128]{2,1,0:T(1,128)}, u32[]{:S(2)}, u32[]{:S(2)}) async-start(s32[64,1,128]{2,1,0:T(1,128)} %broadcast_in_dim.104), calls=%async_computation | async-start | bytes 65536 | tf_op jit(solution)/shard_map/all_to_all | solution.py:181
  21.3 1.9 broadcast_in_dim.108
  23.2 2.2 copy.53.k_ref
  25.4 1.9 broadcast_in_dim.110
  27.3 2.2 copy.54.v_ref
  29.4 0.1 compare_reduce_fusion
  29.5 0.1 add_select_fusion.1
  29.6 0.3 reduce-window.19
  30.0 0.1 slice_reduce_fusion
  30.2 0.9 multiply_sine_fusion
  31.2 0.9 copy.55.cos_ref
  32.1 0.9 tile.20
  32.9 0.8 copy.56.sin_ref
  33.8 0.9 copy.57.segc_ref
  34.6 0.6 iota_subtract_fusion.posr_ref
  35.2 0.6 select_convert_fusion.turn_ref
  35.8 29.4 %shard_map.109 = bf16[512,1280]{1,0:T(8,128)(2,1)} custom-call(bf16[512,1280]{1,0:T(8,128)(2,1)} %q_ref.1, bf16[512,640]{1,0:T(8,128)(2,1)} %copy.53.k_ref, bf16[512,640]{1,0:T(8,128)(2,1)} %copy.54.v_ref, f32[512,128]{1,0:T(8,128)} %copy.55.cos_ref, f32[512,128]{1,0:T(8,128)} %copy.56.sin_ref, bf16[128,128]{1,0:T(8,128)(2,1)} %select_convert_fusion.turn_ref, ...), custom_call_target="tpu_custom_call" | custom-call | tf_op jit(solution)/shard_map/pallas_call | solution.py:108
  65.3 4.6 %fusion.1 = bf16[512,1280]{1,0:T(8,128)(2,1)} fusion(bf16[512,1280]{1,0:T(8,128)(2,1)} %shard_map.109, bf16[1280,1280]{1,0:T(8,128)(2,1)S(1)} %copy-done, bf16[512,1280]{1,0:T(8,128)(2,1)} %param.13, pred[512]{0:T(512)(128)(4,1)S(1)} %iota_compare_fusion.2), kind=kOutput, calls=%fused_computation.5 | convolution fusion | flops 1680343040 | bytes 7209472 | tf_op jit(solution)/shard_map/dot_general | solution.py:142
  69.9 3.1 %copy.58 = bf16[8,64,1280]{2,0,1:T(8,128)(2,1)} copy(bf16[8,64,1280]{2,1,0:T(8,128)(2,1)} %bitcast.48) | data formatting | bytes 2621440 | tf_op jit(solution)/shard_map/reshape | solution.py:199
  73.0 0.9 slice_reduce_fusion.1
  73.9 0.1 reduce-window.18
  74.0 0.1 reduce
  74.1 0.7 fusion.17
  76.9 3.0 %fusion.3 = bf16[8,64,1280]{2,0,1:T(8,128)(2,1)} fusion(s32[]{:T(128)S(6)} %select_n.153, bf16[8,64,1280]{2,0,1:T(8,128)(2,1)} %copy.58), kind=kLoop, calls=%fused_computation.12 | loop fusion | flops 655360 | bytes 2621444 | tf_op jit(solution)/shard_map/jit(_roll_dynamic)/concatenate | solution.py:199
  79.9 10.5 %all-to-all-start.1 = ((bf16[8,64,1280]{2,0,1:T(8,128)(2,1)}), bf16[8,64,1280]{2,0,1:T(8,128)(2,1)}, u32[]{:S(2)}, u32[]{:S(2)}) async-start(bf16[8,64,1280]{2,0,1:T(8,128)(2,1)} %fusion.3), calls=%async_computation.1 | async-start | bytes 2621440 | tf_op jit(solution)/shard_map/all_to_all | solution.py:198
  90.4 0.1 convert_reduce_fusion
  90.5 0.1 select_reduce_fusion
  90.7 33.8 %all-to-all-done.1 = bf16[8,64,1280]{2,0,1:T(8,128)(2,1)} async-done(((bf16[8,64,1280]{2,0,1:T(8,128)(2,1)}), bf16[8,64,1280]{2,0,1:T(8,128)(2,1)}, u32[]{:S(2)}, u32[]{:S(2)}) %all-to-all-start.1) | async-done | bytes 1310752 | tf_op jit(solution)/shard_map/all_to_all | solution.py:198
  124.5 2.6 copy.60
  127.1 3.4 %gather_fusion = bf16[128,1280]{1,0:T(8,128)(2,1)} fusion(bf16[512,1280]{1,0:T(8,128)(2,1)} %bitcast.44, s32[1024]{0:T(1024)S(1)} %pad_clamp_fusion.1), kind=kCustom, calls=%fused_computation | custom fusion | bytes 655872 | tf_op jit(solution)/shard_map/gather | solution.py:205
  130.4 1.1 fusion.4
  131.6 1.8 fusion.6
  133.4 0.2 reduce-scatter.2.cloned.1.call-start
  133.7 22.9 %all-gather.2.cloned.1.call-done = bf16[512,1280]{1,0:T(8,128)(2,1)} async-done(((bf16[128,1280]{1,0:T(8,128)(2,1)}), bf16[512,1280]{1,0:T(8,128)(2,1)}) %all-gather.2.cloned.1.call-update) | async-done | bytes 1310736 | tf_op jit(solution)/shard_map/all_gather | solution.py:147
  156.5 4.8 %fusion.21 = f32[512,896]{1,0:T(8,128)} fusion(bf16[512,1280]{1,0:T(8,128)(2,1)} %all-gather.2.cloned.1.call-done, bf16[1280,896]{1,0:T(8,128)(2,1)} %param.21), kind=kOutput, calls=%fused_computation.81 | convolution fusion | flops 1174405120 | bytes 5439488 | tf_op jit(solution)/shard_map/dot_general | solution.py:148
  161.3 7.3 %convolution_convert_fusion = bf16[512,1280]{1,0:T(8,128)(2,1)} fusion(bf16[896,1280]{1,0:T(8,128)(2,1)} %param.23, f32[512,896]{1,0:T(8,128)} %fusion.21, bf16[512,1280]{1,0:T(8,128)(2,1)} %all-gather.2.cloned.1.call-done, bf16[1280,896]{1,0:T(8,128)(2,1)} %param.22), kind=kOutput, calls=%fused_computation.4 | convolution fusion | flops 2352218112 | bytes 9043968 | tf_op jit(solution)/shard_map/dot_general | solution.py:152
  168.7 0.1 compare_select_fusion
  168.8 0.1 reshape.514
  169.0 0.1 copy.52
  169.1 26.4 %reduce-scatter.2.cloned.1.call-done = bf16[128,1280]{1,0:T(8,128)(2,1)} async-done(((bf16[512,1280]{1,0:T(8,128)(2,1)}), bf16[128,1280]{1,0:T(8,128)(2,1)}) %reduce-scatter.2.cloned.1.call-update) | async-done | bytes 327696 | tf_op jit(solution)/shard_map/reduce_scatter | solution.py:151
  195.5 1.9 fusion.7
  197.4 4.9 %gather_fusion.1 = bf16[512,1280]{1,0:T(8,128)(2,1)} fusion(bf16[128,1280]{1,0:T(8,128)(2,1)} %fusion.7, s32[1024]{0:T(1024)S(1)} %pad_clamp_fusion), kind=kCustom, calls=%fused_computation.1 | custom fusion | bytes 2623488 | tf_op jit(solution)/shard_map/gather | solution.py:214
  202.3 3.2 %copy_select_fusion = bf16[8,64,1280]{2,0,1:T(8,128)(2,1)} fusion(bf16[8,64,1280]{2,1,0:T(8,128)(2,1)} %bitcast.45, pred[8,64]{0,1:T(8,128)(4,1)S(1)} %copy.52), kind=kLoop, calls=%fused_computation.13 | loop fusion | flops 655360 | bytes 2621952 | tf_op jit(solution)/shard_map/jit(_where)/select_n | solution.py:214
  205.5 13.2 %all-to-all-start.2 = ((bf16[8,64,1280]{2,0,1:T(8,128)(2,1)}), bf16[8,64,1280]{2,0,1:T(8,128)(2,1)}, u32[]{:S(2)}, u32[]{:S(2)}) async-start(bf16[8,64,1280]{2,0,1:T(8,128)(2,1)} %copy_select_fusion), calls=%async_computation.3 | async-start | bytes 2621440 | tf_op jit(solution)/shard_map/all_to_all | solution.py:215
  218.7 34.1 %all-to-all-done.2 = bf16[8,64,1280]{2,0,1:T(8,128)(2,1)} async-done(((bf16[8,64,1280]{2,0,1:T(8,128)(2,1)}), bf16[8,64,1280]{2,0,1:T(8,128)(2,1)}, u32[]{:S(2)}, u32[]{:S(2)}) %all-to-all-start.2) | async-done | bytes 1310752 | tf_op jit(solution)/shard_map/all_to_all | solution.py:215
  252.8 1.5 copy.62
  254.3 1.9 fusion.2
  (26 shorter events, 0.5 us)
Async XLA Ops:
  6.5 58.8 %copy-start = (bf16[1280,1280]{1,0:T(8,128)(2,1)S(1)}, bf16[1280,1280]{1,0:T(8,128)(2,1)}, u32[]{:S(2)}) copy-start(bf16[1280,1280]{1,0:T(8,128)(2,1)} %param.19) | copy-start | bytes 9830404
  8.0 65.1 %all-to-all-start = ((s32[64,1,128]{2,1,0:T(1,128)}), s32[64,1,128]{2,1,0:T(1,128)}, u32[]{:S(2)}, u32[]{:S(2)}) async-start(s32[64,1,128]{2,1,0:T(1,128)} %broadcast_in_dim.104), calls=%async_computation | async-start | bytes 65536 | tf_op jit(solution)/shard_map/all_to_all | solution.py:181
  25.4 4.1 %copy-start.1 = (s32[1,1,512]{2,1,0:T(1,128)S(1)}, s32[1,1,512]{2,1,0:T(1,128)}, u32[]{:S(2)}) copy-start(s32[1,1,512]{2,1,0:T(1,128)} %param.17) | copy-start | bytes 6148
  79.9 44.6 %all-to-all-start.1 = ((bf16[8,64,1280]{2,0,1:T(8,128)(2,1)}), bf16[8,64,1280]{2,0,1:T(8,128)(2,1)}, u32[]{:S(2)}, u32[]{:S(2)}) async-start(bf16[8,64,1280]{2,0,1:T(8,128)(2,1)} %fusion.3), calls=%async_computation.1 | async-start | bytes 2621440 | tf_op jit(solution)/shard_map/all_to_all | solution.py:198
  90.4 66.1 %all-gather.2.cloned.1.call-start = ((), (), s32[]{:S(2)}) async-start(), calls=%async_computation.4 | async-start | bytes 1638400 | tf_op jit(solution)/shard_map/all_gather | solution.py:147
  127.1 4.5 %copy-start.2 = (f32[1280]{0:T(1024)S(1)}, f32[1280]{0:T(1024)}, u32[]{:S(2)}) copy-start(f32[1280]{0:T(1024)} %param.20) | copy-start | bytes 15364
  133.4 62.1 %reduce-scatter.2.cloned.1.call-start = ((), (), s32[]{:S(2)}) async-start(), calls=%async_computation.5 | async-start | bytes 1638400 | tf_op jit(solution)/shard_map/reduce_scatter | solution.py:151
  205.5 47.3 %all-to-all-start.2 = ((bf16[8,64,1280]{2,0,1:T(8,128)(2,1)}), bf16[8,64,1280]{2,0,1:T(8,128)(2,1)}, u32[]{:S(2)}, u32[]{:S(2)}) async-start(bf16[8,64,1280]{2,0,1:T(8,128)(2,1)} %copy_select_fusion), calls=%async_computation.3 | async-start | bytes 2621440 | tf_op jit(solution)/shard_map/all_to_all | solution.py:215
Sparse Core Ops, SparseCore 0:
  133.5 22.9 all-gather.1
  168.8 26.6 reduce-scatter.1

commit v2 on v1

--- a/solution.py
+++ b/solution.py
@@ -144,16 +144,21 @@
 
 
 def feed_forward(normed, gate_weight, up_weight, down_weight):
-    gathered = lax.all_gather(normed, "grp", axis=0, tiled=True)
-    gate = jnp.dot(gathered, gate_weight, preferred_element_type=jnp.float32)
-    upward = jnp.dot(gathered, up_weight, preferred_element_type=jnp.float32)
-    hidden = (jax.nn.silu(gate) * upward).astype(jnp.bfloat16)
-    return lax.psum_scatter(
-        jnp.dot(hidden, down_weight, preferred_element_type=jnp.float32).astype(jnp.bfloat16),
-        "grp",
-        scatter_dimension=0,
-        tiled=True,
-    ).astype(jnp.float32)
+    groups = lax.axis_size("grp")
+    chunks = [normed]
+    for k in range(1, groups):
+        chunks.append(lax.ppermute(normed, "grp", [(j, (j + k) % groups) for j in range(groups)]))
+    total = None
+    for k, rows in enumerate(chunks):
+        gate = jnp.dot(rows, gate_weight, preferred_element_type=jnp.float32)
+        upward = jnp.dot(rows, up_weight, preferred_element_type=jnp.float32)
+        hidden = (jax.nn.silu(gate) * upward).astype(jnp.bfloat16)
+        part = jnp.dot(hidden, down_weight, preferred_element_type=jnp.float32).astype(jnp.bfloat16)
+        if k:
+            part = lax.ppermute(part, "grp", [(j, (j - k) % groups) for j in range(groups)])
+        part = part.astype(jnp.float32)
+        total = part if total is None else total + part
+    return total
 
 
 def on_device(

time: 264 us -> 239 us (0.905)
  waiting for transfers between devices: 117 us -> 86.2 us
  matrix products: 16.8 us -> 34.5 us
  between operations: 16.5 us -> 3.08 us
  starting transfers between devices: 37.3 us -> 40.2 us
    reduce_scatter x1 -> x0, waiting for transfers between devices: 26.4 us -> none  [feed_forward(): lax.psum_scatter(jnp.dot(hidden, down_weight, preferred_element_type=jnp....]
    all_gather x1 -> x0, waiting for transfers between devices: 22.9 us -> none  [feed_forward(): gathered = lax.all_gather(normed, 'grp', axis=0, tiled=True)]
    ppermute x0 -> x6, waiting for transfers between devices: none -> 18.3 us  [the longest x3 13.2 us: feed_forward(): lax.ppermute(normed, 'grp', [(j, (j + k) % groups) for j in range(groups)])]
    dot_general x1 -> x4, matrix products: 7.34 us -> 17.6 us  [feed_forward(): jnp.dot(hidden, down_weight, preferred_element_type=jnp.float32)]
    ppermute x0 -> x6, starting transfers between devices: none -> 8.35 us  [the longest x3 4.73 us: feed_forward(): lax.ppermute(part, 'grp', [(j, (j - k) % groups) for j in range(groups)])]
    dot_general x1 -> x4, matrix products: 4.82 us -> 12.2 us  [feed_forward(): gate = jnp.dot(rows, gate_weight, preferred_element_type=jnp.float32)]
    all_to_all x1, starting transfers between devices: 13.2 us -> 8.09 us  [on_device(): lax.all_to_all(outgoing, 'req', split_axis=1, concat_axis=1, tiled=True)]
  transfers between devices with their start and end apart: 5 -> 9, of which waited for: 4 -> 4; matrix products, arithmetic and copies ran while one was open for 9% -> 20% of each run, Pallas kernels for 11% -> 12%
where the time goes in v2:
time: 239 us; the launch traced here: 237 us
  waiting for transfers between devices  86.2 us (36%)
  starting transfers between devices  40.2 us (17%)
  matrix products  34.5 us (14%)
  Pallas kernels  29.4 us (12%)
  local copies, waits for them, and re-layouts  28.9 us (12%)
  other arithmetic  15.1 us (6%)
  between operations  3.08 us (1%)
    all_to_all x1, waiting for transfers between devices, on_device(): lax.all_to_all(outgoing, 'req', split_axis=1, concat_axis=1, tiled=True)  34.1 us
    all_to_all x1, waiting for transfers between devices, on_device(): lax.all_to_all(jnp.roll(kept.reshape(block_rows, request_owners, rows.sha...  33.8 us
    pallas_call x1, Pallas kernels, attend(): pl.pallas_call(attention_kernel, grid=(tiles,), in_specs=[pl.BlockSpec((s...  29.4 us
    dot_general x4, matrix products, feed_forward(): jnp.dot(hidden, down_weight, preferred_element_type=jnp.float32)  17.6 us
    all_to_all x1, starting transfers between devices, on_device(): lax.all_to_all(jnp.broadcast_to(live_rows.reshape(1, 1), (request_owners,...  13.3 us
    ppermute x3, waiting for transfers between devices, feed_forward(): lax.ppermute(normed, 'grp', [(j, (j + k) % groups) for j in range(groups)])  13.2 us
    dot_general x4, matrix products, feed_forward(): gate = jnp.dot(rows, gate_weight, preferred_element_type=jnp.float32)  12.2 us
    all_to_all x1, starting transfers between devices, on_device(): lax.all_to_all(jnp.roll(kept.reshape(block_rows, request_owners, rows.sha...  10.5 us
  transfers between devices with their start and end apart: 9, of which 4 were waited for; matrix products, arithmetic and copies ran while one was open for 20% of the time, Pallas kernels for 12%

profile of v2, /device:TPU:1, one launch (start us, length us, event | category | flops | bytes accessed | tf_op | source)
XLA Modules:
  0.0 237.4 jit_solution(5108018000860403684)
XLA Ops:
  0.8 0.6 broadcast_in_dim.104
  1.4 13.3 %all-to-all-start = ((s32[64,1,128]{2,1,0:T(1,128)}), s32[64,1,128]{2,1,0:T(1,128)}, u32[]{:S(2)}, u32[]{:S(2)}) async-start(s32[64,1,128]{2,1,0:T(1,128)} %broadcast_in_dim.104), calls=%async_computation | async-start | bytes 65536 | tf_op jit(solution)/shard_map/all_to_all | solution.py:186
  14.8 1.9 broadcast_in_dim.108
  16.7 2.2 copy.53.k_ref
  18.9 1.9 broadcast_in_dim.110
  20.7 2.2 copy.54.v_ref
  23.1 0.3 reduce-window.19
  23.5 0.1 slice_reduce_fusion
  23.7 0.9 multiply_sine_fusion
  24.7 0.9 copy.55.cos_ref
  25.5 0.9 tile.20
  26.4 0.8 copy.56.sin_ref
  27.2 0.9 copy.57.segc_ref
  28.1 0.6 iota_subtract_fusion.posr_ref
  28.7 0.6 select_convert_fusion.turn_ref
  29.3 29.4 %shard_map.109 = bf16[512,1280]{1,0:T(8,128)(2,1)} custom-call(bf16[512,1280]{1,0:T(8,128)(2,1)} %q_ref.1, bf16[512,640]{1,0:T(8,128)(2,1)} %copy.53.k_ref, bf16[512,640]{1,0:T(8,128)(2,1)} %copy.54.v_ref, f32[512,128]{1,0:T(8,128)} %copy.55.cos_ref, f32[512,128]{1,0:T(8,128)} %copy.56.sin_ref, bf16[128,128]{1,0:T(8,128)(2,1)} %select_convert_fusion.turn_ref, ...), custom_call_target="tpu_custom_call" | custom-call | tf_op jit(solution)/shard_map/pallas_call | solution.py:108
  58.8 4.6 %fusion.1 = bf16[512,1280]{1,0:T(8,128)(2,1)} fusion(bf16[512,1280]{1,0:T(8,128)(2,1)} %shard_map.109, bf16[1280,1280]{1,0:T(8,128)(2,1)S(1)} %copy-done, bf16[512,1280]{1,0:T(8,128)(2,1)} %param.13, pred[512]{0:T(512)(128)(4,1)S(1)} %iota_compare_fusion.2), kind=kOutput, calls=%fused_computation.4 | convolution fusion | flops 1680343040 | bytes 7209472 | tf_op jit(solution)/shard_map/dot_general | solution.py:142
  63.4 3.1 %copy.58 = bf16[8,64,1280]{2,0,1:T(8,128)(2,1)} copy(bf16[8,64,1280]{2,1,0:T(8,128)(2,1)} %bitcast.61) | data formatting | bytes 2621440 | tf_op jit(solution)/shard_map/reshape | solution.py:204
  66.5 0.9 slice_reduce_fusion.1
  67.4 0.1 reduce
  67.6 0.7 fusion.28
  70.4 2.9 %fusion.4 = bf16[8,64,1280]{2,0,1:T(8,128)(2,1)} fusion(s32[]{:T(128)S(6)} %select_n.153, bf16[8,64,1280]{2,0,1:T(8,128)(2,1)} %copy.58), kind=kLoop, calls=%fused_computation.15 | loop fusion | flops 655360 | bytes 2621444 | tf_op jit(solution)/shard_map/jit(_roll_dynamic)/concatenate | solution.py:204
  73.3 10.5 %all-to-all-start.1 = ((bf16[8,64,1280]{2,0,1:T(8,128)(2,1)}), bf16[8,64,1280]{2,0,1:T(8,128)(2,1)}, u32[]{:S(2)}, u32[]{:S(2)}) async-start(bf16[8,64,1280]{2,0,1:T(8,128)(2,1)} %fusion.4), calls=%async_computation.1 | async-start | bytes 2621440 | tf_op jit(solution)/shard_map/all_to_all | solution.py:203
  84.0 33.8 %all-to-all-done.1 = bf16[8,64,1280]{2,0,1:T(8,128)(2,1)} async-done(((bf16[8,64,1280]{2,0,1:T(8,128)(2,1)}), bf16[8,64,1280]{2,0,1:T(8,128)(2,1)}, u32[]{:S(2)}, u32[]{:S(2)}) %all-to-all-start.1) | async-done | bytes 1310752 | tf_op jit(solution)/shard_map/all_to_all | solution.py:203
  117.9 2.6 %copy.60 = bf16[8,64,1280]{2,1,0:T(8,128)(2,1)} copy(bf16[8,64,1280]{2,0,1:T(8,128)(2,1)} %all-to-all-done.1) | data formatting | bytes 2621440 | tf_op jit(solution)/shard_map/all_to_all | solution.py:203
  120.5 3.4 %gather_fusion = bf16[128,1280]{1,0:T(8,128)(2,1)} fusion(bf16[512,1280]{1,0:T(8,128)(2,1)} %bitcast.57, s32[1024]{0:T(1024)S(1)} %pad_clamp_fusion.1), kind=kCustom, calls=%fused_computation | custom fusion | bytes 655872 | tf_op jit(solution)/shard_map/gather | solution.py:210
  123.8 1.1 fusion.6
  124.9 1.9 fusion.8
  126.8 2.6 %collective-permute-start.4 = (bf16[128,1280]{1,0:T(8,128)(2,1)}, bf16[128,1280]{1,0:T(8,128)(2,1)}, u32[]{:S(2)}, u32[]{:S(2)}) collective-permute-start(bf16[128,1280]{1,0:T(8,128)(2,1)} %fusion.8), channel_id=1, source_target_pairs={{0,3},{1,0},{2,1},{3,2},{4,7},{5,4},{6,5},{7,6},{8,11},{9,8},{10,9... | collective-permute-start | bytes 983048 | tf_op jit(solution)/shard_map/ppermute | solution.py:150
  129.6 0.5 collective-permute-start.2
  130.0 0.6 collective-permute-start
  130.7 13.2 %collective-permute-done.4 = bf16[128,1280]{1,0:T(8,128)(2,1)} collective-permute-done((bf16[128,1280]{1,0:T(8,128)(2,1)}, bf16[128,1280]{1,0:T(8,128)(2,1)}, u32[]{:S(2)}, u32[]{:S(2)}) %collective-permute-start.4) | collective-permute-done | bytes 327712 | tf_op jit(solution)/shard_map/ppermute | solution.py:150
  143.8 3.1 %fusion.47 = f32[128,896]{1,0:T(8,128)} fusion(bf16[128,1280]{1,0:T(8,128)(2,1)} %collective-permute-done.4, bf16[1280,896]{1,0:T(8,128)(2,1)} %param.21), kind=kOutput, calls=%fused_computation.107 | convolution fusion | flops 293601280 | bytes 3080192 | tf_op jit(solution)/shard_map/dot_general | solution.py:153
  146.9 4.3 %convolution_convert_fusion = bf16[128,1280]{1,0:T(8,128)(2,1)} fusion(bf16[896,1280]{1,0:T(8,128)(2,1)} %param.23, f32[128,896]{1,0:T(8,128)} %fusion.47, bf16[128,1280]{1,0:T(8,128)(2,1)} %collective-permute-done.4, bf16[1280,896]{1,0:T(8,128)(2,1)} %param.22), kind=kOutput, calls=%fused_computation.9 | convolution fusion | flops 588054528 | bytes 5701632 | tf_op jit(solution)/shard_map/dot_general | solution.py:156
  151.2 3.0 %fusion.46 = f32[128,896]{1,0:T(8,128)} fusion(bf16[128,1280]{1,0:T(8,128)(2,1)} %collective-permute-done.2, bf16[1280,896]{1,0:T(8,128)(2,1)} %param.21), kind=kOutput, calls=%fused_computation.106 | convolution fusion | flops 293601280 | bytes 3080192 | tf_op jit(solution)/shard_map/dot_general | solution.py:153
  154.2 4.3 %convolution_convert_fusion.1 = bf16[128,1280]{1,0:T(8,128)(2,1)} fusion(bf16[896,1280]{1,0:T(8,128)(2,1)} %param.23, f32[128,896]{1,0:T(8,128)} %fusion.46, bf16[128,1280]{1,0:T(8,128)(2,1)} %collective-permute-done.2, bf16[1280,896]{1,0:T(8,128)(2,1)} %param.22), kind=kOutput, calls=%fused_computation.10 | convolution fusion | flops 588054528 | bytes 5701632 | tf_op jit(solution)/shard_map/dot_general | solution.py:156
  158.6 4.7 %collective-permute-start.3 = (bf16[128,1280]{1,0:T(8,128)(2,1)}, bf16[128,1280]{1,0:T(8,128)(2,1)}, u32[]{:S(2)}, u32[]{:S(2)}) collective-permute-start(bf16[128,1280]{1,0:T(8,128)(2,1)} %convolution_convert_fusion.1), channel_id=1, source_target_pairs={{0,2},{1,3},{2,0},{3,1},{4,6},{5,7},{6,4},{7,5},{8,10},{9,11},{10,... | collective-permute-start | bytes 983048 | tf_op jit(solution)/shard_map/ppermute | solution.py:158
  163.3 3.0 %fusion.45 = f32[128,896]{1,0:T(8,128)} fusion(bf16[128,1280]{1,0:T(8,128)(2,1)} %collective-permute-done, bf16[1280,896]{1,0:T(8,128)(2,1)} %param.21), kind=kOutput, calls=%fused_computation.105 | convolution fusion | flops 293601280 | bytes 3080192 | tf_op jit(solution)/shard_map/dot_general | solution.py:153
  166.3 4.3 %convolution_convert_fusion.2 = bf16[128,1280]{1,0:T(8,128)(2,1)} fusion(bf16[896,1280]{1,0:T(8,128)(2,1)} %param.23, f32[128,896]{1,0:T(8,128)} %fusion.45, bf16[128,1280]{1,0:T(8,128)(2,1)} %collective-permute-done, bf16[1280,896]{1,0:T(8,128)(2,1)} %param.22), kind=kOutput, calls=%fused_computation.11 | convolution fusion | flops 588054528 | bytes 5701632 | tf_op jit(solution)/shard_map/dot_general | solution.py:156
  170.8 3.1 %fusion.37 = f32[128,896]{1,0:T(8,128)} fusion(bf16[1280,896]{1,0:T(8,128)(2,1)} %param.21, bf16[128,1280]{1,0:T(8,128)(2,1)} %gather_fusion, f32[1280]{0:T(1024)S(1)} %copy-done.1, f32[128]{0:T(128)S(1)} %add_rsqrt_fusion), kind=kOutput, calls=%fused_computation.101 | convolution fusion | flops 294256640 | bytes 3085824 | tf_op jit(solution)/shard_map/dot_general | solution.py:153
  173.9 5.1 %collective-permute-done.1 = bf16[128,1280]{1,0:T(8,128)(2,1)} collective-permute-done((bf16[128,1280]{1,0:T(8,128)(2,1)}, bf16[128,1280]{1,0:T(8,128)(2,1)}, u32[]{:S(2)}, u32[]{:S(2)}) %collective-permute-start.1) | collective-permute-done | bytes 327712 | tf_op jit(solution)/shard_map/ppermute | solution.py:158
  179.0 4.7 %fusion.9 = bf16[128,1280]{1,0:T(8,128)(2,1)} fusion(bf16[128,1280]{1,0:T(8,128)(2,1)} %gather_fusion, bf16[128,1280]{1,0:T(8,128)(2,1)} %collective-permute-done.5, bf16[128,1280]{1,0:T(8,128)(2,1)} %collective-permute-done.3, bf16[128,1280]{1,0:T(8,128)(2,1)} %collective-permute-done.1, bf16[896,1280]{1,0:T(8,128)(2,1)} %param.23, ...), kind=kOutput, calls=%fused_computation.25 | convolution fusion | flops 590348288 | bytes 6690304 | tf_op jit(solution)/shard_map/dot_general | solution.py:156
  183.7 4.9 %gather_fusion.1 = bf16[512,1280]{1,0:T(8,128)(2,1)} fusion(bf16[128,1280]{1,0:T(8,128)(2,1)} %fusion.9, s32[1024]{0:T(1024)S(1)} %pad_clamp_fusion), kind=kCustom, calls=%fused_computation.1 | custom fusion | bytes 2623488 | tf_op jit(solution)/shard_map/gather | solution.py:219
  188.6 3.2 %copy_select_fusion = bf16[8,64,1280]{2,0,1:T(8,128)(2,1)} fusion(bf16[8,64,1280]{2,1,0:T(8,128)(2,1)} %bitcast.58, pred[8,64]{0,1:T(8,128)(4,1)S(1)} %copy.52), kind=kLoop, calls=%fused_computation.16 | loop fusion | flops 655360 | bytes 2621952 | tf_op jit(solution)/shard_map/jit(_where)/select_n | solution.py:219
  191.8 8.1 %all-to-all-start.2 = ((bf16[8,64,1280]{2,0,1:T(8,128)(2,1)}), bf16[8,64,1280]{2,0,1:T(8,128)(2,1)}, u32[]{:S(2)}, u32[]{:S(2)}) async-start(bf16[8,64,1280]{2,0,1:T(8,128)(2,1)} %copy_select_fusion), calls=%async_computation.2 | async-start | bytes 2621440 | tf_op jit(solution)/shard_map/all_to_all | solution.py:220
  199.9 34.1 %all-to-all-done.2 = bf16[8,64,1280]{2,0,1:T(8,128)(2,1)} async-done(((bf16[8,64,1280]{2,0,1:T(8,128)(2,1)}), bf16[8,64,1280]{2,0,1:T(8,128)(2,1)}, u32[]{:S(2)}, u32[]{:S(2)}) %all-to-all-start.2) | async-done | bytes 1310752 | tf_op jit(solution)/shard_map/all_to_all | solution.py:220
  234.0 1.5 copy.62
  235.5 1.9 fusion.3
  (37 shorter events, 1.1 us)
Async XLA Ops:
  0.0 58.8 %copy-start = (bf16[1280,1280]{1,0:T(8,128)(2,1)S(1)}, bf16[1280,1280]{1,0:T(8,128)(2,1)}, u32[]{:S(2)}) copy-start(bf16[1280,1280]{1,0:T(8,128)(2,1)} %param.19) | copy-start | bytes 9830404
  1.4 65.1 %all-to-all-start = ((s32[64,1,128]{2,1,0:T(1,128)}), s32[64,1,128]{2,1,0:T(1,128)}, u32[]{:S(2)}, u32[]{:S(2)}) async-start(s32[64,1,128]{2,1,0:T(1,128)} %broadcast_in_dim.104), calls=%async_computation | async-start | bytes 65536 | tf_op jit(solution)/shard_map/all_to_all | solution.py:186
  14.8 8.1 %copy-start.2 = (s32[1,1,512]{2,1,0:T(1,128)S(1)}, s32[1,1,512]{2,1,0:T(1,128)}, u32[]{:S(2)}) copy-start(s32[1,1,512]{2,1,0:T(1,128)} %param.17) | copy-start | bytes 6148
  73.3 44.6 %all-to-all-start.1 = ((bf16[8,64,1280]{2,0,1:T(8,128)(2,1)}), bf16[8,64,1280]{2,0,1:T(8,128)(2,1)}, u32[]{:S(2)}, u32[]{:S(2)}) async-start(bf16[8,64,1280]{2,0,1:T(8,128)(2,1)} %fusion.4), calls=%async_computation.1 | async-start | bytes 2621440 | tf_op jit(solution)/shard_map/all_to_all | solution.py:203
  120.4 4.5 %copy-start.1 = (f32[1280]{0:T(1024)S(1)}, f32[1280]{0:T(1024)}, u32[]{:S(2)}) copy-start(f32[1280]{0:T(1024)} %param.20) | copy-start | bytes 15364
  126.8 17.0 %collective-permute-start.4 = (bf16[128,1280]{1,0:T(8,128)(2,1)}, bf16[128,1280]{1,0:T(8,128)(2,1)}, u32[]{:S(2)}, u32[]{:S(2)}) collective-permute-start(bf16[128,1280]{1,0:T(8,128)(2,1)} %fusion.8), channel_id=1, source_target_pairs={{0,3},{1,0},{2,1},{3,2},{4,7},{5,4},{6,5},{7,6},{8,11},{9,8},{10,9... | collective-permute-start | bytes 983048 | tf_op jit(solution)/shard_map/ppermute | solution.py:150
  129.6 21.6 %collective-permute-start.2 = (bf16[128,1280]{1,0:T(8,128)(2,1)}, bf16[128,1280]{1,0:T(8,128)(2,1)}, u32[]{:S(2)}, u32[]{:S(2)}) collective-permute-start(bf16[128,1280]{1,0:T(8,128)(2,1)} %fusion.8), channel_id=1, source_target_pairs={{0,2},{1,3},{2,0},{3,1},{4,6},{5,7},{6,4},{7,5},{8,10},{9,11},{10,... | collective-permute-start | bytes 983048 | tf_op jit(solution)/shard_map/ppermute | solution.py:150
  130.0 33.2 %collective-permute-start = (bf16[128,1280]{1,0:T(8,128)(2,1)}, bf16[128,1280]{1,0:T(8,128)(2,1)}, u32[]{:S(2)}, u32[]{:S(2)}) collective-permute-start(bf16[128,1280]{1,0:T(8,128)(2,1)} %fusion.8), channel_id=1, source_target_pairs={{0,1},{1,2},{2,3},{3,0},{4,5},{5,6},{6,7},{7,4},{8,9},{9,10},{10,1... | collective-permute-start | bytes 983048 | tf_op jit(solution)/shard_map/ppermute | solution.py:150
  151.2 22.7 %collective-permute-start.5 = (bf16[128,1280]{1,0:T(8,128)(2,1)}, bf16[128,1280]{1,0:T(8,128)(2,1)}, u32[]{:S(2)}, u32[]{:S(2)}) collective-permute-start(bf16[128,1280]{1,0:T(8,128)(2,1)} %convolution_convert_fusion), channel_id=1, source_target_pairs={{0,1},{1,2},{2,3},{3,0},{4,5},{5,6},{6,7},{7,4},{8,9},{9,10},{10,1... | collective-permute-start | bytes 983048 | tf_op jit(solution)/shard_map/ppermute | solution.py:158
  158.6 15.3 %collective-permute-start.3 = (bf16[128,1280]{1,0:T(8,128)(2,1)}, bf16[128,1280]{1,0:T(8,128)(2,1)}, u32[]{:S(2)}, u32[]{:S(2)}) collective-permute-start(bf16[128,1280]{1,0:T(8,128)(2,1)} %convolution_convert_fusion.1), channel_id=1, source_target_pairs={{0,2},{1,3},{2,0},{3,1},{4,6},{5,7},{6,4},{7,5},{8,10},{9,11},{10,... | collective-permute-start | bytes 983048 | tf_op jit(solution)/shard_map/ppermute | solution.py:158
  170.6 8.3 %collective-permute-start.1 = (bf16[128,1280]{1,0:T(8,128)(2,1)}, bf16[128,1280]{1,0:T(8,128)(2,1)}, u32[]{:S(2)}, u32[]{:S(2)}) collective-permute-start(bf16[128,1280]{1,0:T(8,128)(2,1)} %convolution_convert_fusion.2), channel_id=1, source_target_pairs={{0,3},{1,0},{2,1},{3,2},{4,7},{5,4},{6,5},{7,6},{8,11},{9,8},{10,9... | collective-permute-start | bytes 983048 | tf_op jit(solution)/shard_map/ppermute | solution.py:158
  191.8 42.2 %all-to-all-start.2 = ((bf16[8,64,1280]{2,0,1:T(8,128)(2,1)}), bf16[8,64,1280]{2,0,1:T(8,128)(2,1)}, u32[]{:S(2)}, u32[]{:S(2)}) async-start(bf16[8,64,1280]{2,0,1:T(8,128)(2,1)} %copy_select_fusion), calls=%async_computation.2 | async-start | bytes 2621440 | tf_op jit(solution)/shard_map/all_to_all | solution.py:220

commit v3 on v2

--- a/solution.py
+++ b/solution.py
@@ -38,7 +38,7 @@
     return turn.astype(jnp.bfloat16)
 
 
-def attention_kernel(q_ref, k_ref, v_ref, cos_ref, sin_ref, turn_ref, segc_ref, segr_ref, posr_ref, out_ref, bias_ref):
+def attention_kernel(q_ref, k_ref, v_ref, cos_ref, sin_ref, turn_ref, segc_ref, segr_ref, posr_ref, w_ref, h_ref, out_ref, bias_ref, acc_ref):
     slots = q_ref.shape[0]
     block = LANES
 
@@ -49,6 +49,7 @@
         allowed = (segc_ref[...] == segr_ref[...]) & (ki <= qi)
         allowed = allowed & ((qi - ki < WINDOW) | (posr_ref[...] < SINK))
         bias_ref[...] = jnp.where(allowed, 0.0, -jnp.inf).astype(jnp.float32)
+        acc_ref[...] = h_ref[...].astype(jnp.float32)
 
     cosine = cos_ref[...]
     sine = sin_ref[...]
@@ -84,11 +85,17 @@
             total = jnp.sum(raised, axis=-1, keepdims=True)
             weights = (raised * (1.0 / total)).astype(jnp.bfloat16)
             parts.append(jnp.dot(weights, v_part, preferred_element_type=jnp.float32))
-        context = jnp.where(low, parts[0], parts[1])
-        out_ref[i * block:(i + 1) * block, :] = context.astype(out_ref.dtype)
-
-
-def attend(queries, projected_keys, projected_values, segment):
+        context = jnp.where(low, parts[0], parts[1]).astype(jnp.bfloat16)
+        acc_ref[i * block:(i + 1) * block, :] += jnp.dot(
+            context, w_ref[...], preferred_element_type=jnp.float32
+        )
+
+    @pl.when(pl.program_id(0) == pl.num_programs(0) - 1)
+    def _():
+        out_ref[...] = acc_ref[...].astype(out_ref.dtype)
+
+
+def attend(queries, projected_keys, projected_values, segment, out_weight, hidden_in):
     slot_capacity = queries.shape[0]
     slots = jnp.arange(slot_capacity, dtype=jnp.int32)
     begins = jnp.concatenate([jnp.ones((1,), dtype=jnp.bool_), segment[1:] != segment[:-1]])
@@ -105,6 +112,7 @@
     tiles = QUERY_HEADS * HEAD_SIZE // LANES
     per_kv = tiles // KEY_VALUE_HEADS
     full = lambda t: (0, 0)
+    width = out_weight.shape[1]
     return pl.pallas_call(
         attention_kernel,
         grid=(tiles,),
@@ -118,15 +126,20 @@
             pl.BlockSpec((slot_capacity, 1), full),
             pl.BlockSpec((1, slot_capacity), full),
             pl.BlockSpec((1, slot_capacity), full),
+            pl.BlockSpec((LANES, width), lambda t: (t, 0)),
+            pl.BlockSpec((slot_capacity, width), full),
         ],
-        out_specs=pl.BlockSpec((slot_capacity, LANES), lambda t: (0, t)),
-        out_shape=jax.ShapeDtypeStruct((slot_capacity, QUERY_HEADS * HEAD_SIZE), jnp.bfloat16),
-        scratch_shapes=[pltpu.VMEM((slot_capacity, slot_capacity), jnp.float32)],
+        out_specs=pl.BlockSpec((slot_capacity, width), full),
+        out_shape=jax.ShapeDtypeStruct((slot_capacity, width), jnp.bfloat16),
+        scratch_shapes=[
+            pltpu.VMEM((slot_capacity, slot_capacity), jnp.float32),
+            pltpu.VMEM((slot_capacity, width), jnp.float32),
+        ],
         compiler_params=pltpu.CompilerParams(dimension_semantics=("arbitrary",)),
     )(
         queries, keys2, values2, cosine, sine, turn,
         segment.reshape(slot_capacity, 1), segment.reshape(1, slot_capacity),
-        token_position.reshape(1, slot_capacity),
+        token_position.reshape(1, slot_capacity), out_weight, hidden_in,
     )
 
 
@@ -143,21 +156,27 @@
     ).astype(jnp.bfloat16)
 
 
+def ffn_rows(rows, gate_weight, up_weight, down_weight):
+    gate = jnp.dot(rows, gate_weight, preferred_element_type=jnp.float32)
+    upward = jnp.dot(rows, up_weight, preferred_element_type=jnp.float32)
+    hidden = (jax.nn.silu(gate) * upward).astype(jnp.bfloat16)
+    return jnp.dot(hidden, down_weight, preferred_element_type=jnp.float32).astype(jnp.bfloat16)
+
+
 def feed_forward(normed, gate_weight, up_weight, down_weight):
     groups = lax.axis_size("grp")
-    chunks = [normed]
+    rows = normed.shape[0]
+    arrived = [
+        lax.ppermute(normed, "grp", [(j, (j + k) % groups) for j in range(groups)])
+        for k in range(1, groups)
+    ]
+    own = ffn_rows(normed, gate_weight, up_weight, down_weight)
+    others = ffn_rows(jnp.concatenate(arrived, axis=0), gate_weight, up_weight, down_weight)
+    total = own.astype(jnp.float32)
     for k in range(1, groups):
-        chunks.append(lax.ppermute(normed, "grp", [(j, (j + k) % groups) for j in range(groups)]))
-    total = None
-    for k, rows in enumerate(chunks):
-        gate = jnp.dot(rows, gate_weight, preferred_element_type=jnp.float32)
-        upward = jnp.dot(rows, up_weight, preferred_element_type=jnp.float32)
-        hidden = (jax.nn.silu(gate) * upward).astype(jnp.bfloat16)
-        part = jnp.dot(hidden, down_weight, preferred_element_type=jnp.float32).astype(jnp.bfloat16)
-        if k:
-            part = lax.ppermute(part, "grp", [(j, (j - k) % groups) for j in range(groups)])
-        part = part.astype(jnp.float32)
-        total = part if total is None else total + part
+        part = others[(k - 1) * rows:k * rows]
+        part = lax.ppermute(part, "grp", [(j, (j - k) % groups) for j in range(groups)])
+        total = total + part.astype(jnp.float32)
     return total
 
 
@@ -175,8 +194,8 @@
     down_weight,
 ):
     slot_capacity = hidden_in.shape[0]
-    attended_context = attend(
-        queries, projected_keys, projected_values, segment.reshape(slot_capacity)
+    rows = attend(
+        queries, projected_keys, projected_values, segment.reshape(slot_capacity), out_weight, hidden_in
     )
     slots = jnp.arange(slot_capacity, dtype=jnp.int32)
     own_count = live_rows.reshape(())
@@ -198,7 +217,6 @@
         jnp.where(source[:, None] == owner_ids[None, :], firsts[None, :], 0), axis=1
     )
     pick = (stream - source_first) // request_owners * request_owners + source
-    rows = project(attended_context, hidden_in, out_weight)
     kept = jnp.where(keep[:, None], rows, jnp.zeros_like(rows))
     arrived = lax.all_to_all(
         jnp.roll(kept.reshape(block_rows, request_owners, rows.shape[1]), own_shift, axis=1),

time: 239 us -> 225 us (0.941)
  matrix products: 34.5 us -> 14.7 us
  waiting for transfers between devices: 86.2 us -> 93.5 us
  Pallas kernels: 29.4 us -> 35.8 us
  local copies, waits for them, and re-layouts: 28.9 us -> 23.7 us
    dot_general x9 -> x4, matrix products: 34.5 us -> 14.7 us  [the longest x2 8.55 us: ffn_rows(): jnp.dot(hidden, down_weight, preferred_element_type=jnp.float32)]
    ppermute x3, waiting for transfers between devices: 5.14 us -> 12.1 us  [feed_forward(): lax.ppermute(part, 'grp', [(j, (j - k) % groups) for j in range(groups)])]
    pallas_call x1, Pallas kernels: 29.4 us -> 35.8 us  [attend(): pl.pallas_call(attention_kernel, grid=(tiles,), in_specs=[pl.BlockSpec((s...]
    broadcast_in_dim x2, local copies, waits for them, and re-layouts: 3.74 us -> 1.08 us  [doubled(): x = jnp.broadcast_to(x, (slot_capacity, KEY_VALUE_HEADS, 2, HEAD_SIZE))]
    select_n x0 -> x1, other arithmetic: none -> 2.53 us  [on_device(): kept = jnp.where(keep[:, None], rows, jnp.zeros_like(rows))]
  transfers between devices with their start and end apart: 9 -> 9, of which waited for: 4 -> 7; matrix products, arithmetic and copies ran while one was open for 20% -> 8% of each run, Pallas kernels for 12% -> 16%
where the time goes in v3:
time: 225 us; the launch traced here: 224 us
  waiting for transfers between devices  93.5 us (42%)
  starting transfers between devices  39.6 us (18%)
  Pallas kernels  35.8 us (16%)
  local copies, waits for them, and re-layouts  23.7 us (11%)
  matrix products  14.7 us (7%)
  other arithmetic  14.3 us (6%)
  between operations  3.02 us (1%)
    pallas_call x1, Pallas kernels, attend(): pl.pallas_call(attention_kernel, grid=(tiles,), in_specs=[pl.BlockSpec((s...  35.8 us
    all_to_all x1, waiting for transfers between devices, on_device(): lax.all_to_all(outgoing, 'req', split_axis=1, concat_axis=1, tiled=True)  34.1 us
    all_to_all x1, waiting for transfers between devices, on_device(): lax.all_to_all(jnp.roll(kept.reshape(block_rows, request_owners, rows.sha...  33.8 us
    ppermute x3, waiting for transfers between devices, feed_forward(): lax.ppermute(normed, 'grp', [(j, (j + k) % groups) for j in range(groups)])  13.5 us
    all_to_all x1, starting transfers between devices, on_device(): lax.all_to_all(jnp.broadcast_to(live_rows.reshape(1, 1), (request_owners,...  13.1 us
    ppermute x3, waiting for transfers between devices, feed_forward(): lax.ppermute(part, 'grp', [(j, (j - k) % groups) for j in range(groups)])  12.1 us
    all_to_all x1, starting transfers between devices, on_device(): lax.all_to_all(jnp.roll(kept.reshape(block_rows, request_owners, rows.sha...  10.5 us
    dot_general x2, matrix products, ffn_rows(): jnp.dot(hidden, down_weight, preferred_element_type=jnp.float32)  8.55 us
  transfers between devices with their start and end apart: 9, of which 7 were waited for; matrix products, arithmetic and copies ran while one was open for 8% of the time, Pallas kernels for 16%

profile of v3, /device:TPU:1, one launch (start us, length us, event | category | flops | bytes accessed | tf_op | source)
XLA Modules:
  0.0 224.5 jit_solution(18343577036895229598)
XLA Ops:
  0.8 0.6 broadcast_in_dim.104
  1.4 13.1 %all-to-all-start = ((s32[64,1,128]{2,1,0:T(1,128)}), s32[64,1,128]{2,1,0:T(1,128)S(1)}, u32[]{:S(2)}, u32[]{:S(2)}) async-start(s32[64,1,128]{2,1,0:T(1,128)} %broadcast_in_dim.104), calls=%async_computation | async-start | bytes 65536 | tf_op jit(solution)/shard_map/all_to_all | solution.py:205
  14.6 1.0 broadcast_in_dim.108
  15.7 1.1 copy.53.k_ref
  16.8 1.1 copy.54.v_ref
  18.1 0.3 reduce-window.19
  18.5 0.1 slice_reduce_fusion
  18.7 0.3 multiply_sine_fusion
  19.0 0.9 copy.55.cos_ref
  19.9 0.8 copy.56.sin_ref
  20.7 0.9 copy.57.segc_ref
  21.6 0.6 iota_subtract_fusion.posr_ref
  22.2 0.6 select_convert_fusion.turn_ref
  22.8 35.8 %shard_map.109 = bf16[512,1280]{1,0:T(8,128)(2,1)} custom-call(bf16[512,1280]{1,0:T(8,128)(2,1)} %q_ref.1, bf16[512,640]{1,0:T(8,128)(2,1)} %copy.53.k_ref, bf16[512,640]{1,0:T(8,128)(2,1)} %copy.54.v_ref, f32[512,128]{1,0:T(8,128)} %copy.55.cos_ref, f32[512,128]{1,0:T(8,128)} %copy.56.sin_ref, bf16[128,128]{1,0:T(8,128)(2,1)} %select_convert_fusion.turn_ref, ...), custom_call_target="tpu_custom_call" | custom-call | tf_op jit(solution)/shard_map/pallas_call | solution.py:116
  58.6 2.5 %broadcast_select_fusion = bf16[512,1280]{1,0:T(8,128)(2,1)} fusion(bf16[512,1280]{1,0:T(8,128)(2,1)} %shard_map.109, pred[512]{0:T(512)(128)(4,1)S(1)} %iota_compare_fusion.2), kind=kLoop, calls=%fused_computation.13 | loop fusion | flops 655360 | bytes 2621952 | tf_op jit(solution)/shard_map/jit(_where)/select_n | solution.py:220
  61.1 3.1 %copy.58 = bf16[8,64,1280]{2,0,1:T(8,128)(2,1)} copy(bf16[8,64,1280]{2,1,0:T(8,128)(2,1)} %bitcast.46) | data formatting | bytes 2621440 | tf_op jit(solution)/shard_map/reshape | solution.py:222
  64.6 0.6 fusion.24
  67.2 2.9 %fusion.2 = bf16[8,64,1280]{2,0,1:T(8,128)(2,1)} fusion(s32[]{:T(128)S(6)} %select_n.153, bf16[8,64,1280]{2,0,1:T(8,128)(2,1)} %copy.58), kind=kLoop, calls=%fused_computation.11 | loop fusion | flops 655360 | bytes 2621444 | tf_op jit(solution)/shard_map/jit(_roll_dynamic)/concatenate | solution.py:222
  70.1 10.5 %all-to-all-start.1 = ((bf16[8,64,1280]{2,0,1:T(8,128)(2,1)}), bf16[8,64,1280]{2,0,1:T(8,128)(2,1)}, u32[]{:S(2)}, u32[]{:S(2)}) async-start(bf16[8,64,1280]{2,0,1:T(8,128)(2,1)} %fusion.2), calls=%async_computation.1 | async-start | bytes 2621440 | tf_op jit(solution)/shard_map/all_to_all | solution.py:221
  80.8 33.8 %all-to-all-done.1 = bf16[8,64,1280]{2,0,1:T(8,128)(2,1)} async-done(((bf16[8,64,1280]{2,0,1:T(8,128)(2,1)}), bf16[8,64,1280]{2,0,1:T(8,128)(2,1)}, u32[]{:S(2)}, u32[]{:S(2)}) %all-to-all-start.1) | async-done | bytes 1310752 | tf_op jit(solution)/shard_map/all_to_all | solution.py:221
  114.7 2.6 %copy.60 = bf16[8,64,1280]{2,1,0:T(8,128)(2,1)} copy(bf16[8,64,1280]{2,0,1:T(8,128)(2,1)} %all-to-all-done.1) | data formatting | bytes 2621440 | tf_op jit(solution)/shard_map/all_to_all | solution.py:221
  117.2 2.6 %gather_fusion = bf16[128,1280]{1,0:T(8,128)(2,1)S(1)} fusion(bf16[512,1280]{1,0:T(8,128)(2,1)} %bitcast.45, s32[1024]{0:T(1024)S(1)} %pad_clamp_fusion.1), kind=kCustom, calls=%fused_computation | custom fusion | bytes 655872 | tf_op jit(solution)/shard_map/gather | solution.py:228
  119.9 0.1 fusion.5
  120.1 0.1 fusion.7
  120.2 1.2 collective-permute-start
  121.5 2.6 %collective-permute-start.1 = (bf16[128,1280]{1,0:T(8,128)(2,1)S(1)}, bf16[128,1280]{1,0:T(8,128)(2,1)}, u32[]{:S(2)}, u32[]{:S(2)}) collective-permute-start(bf16[128,1280]{1,0:T(8,128)(2,1)S(1)} %fusion.7), channel_id=1, source_target_pairs={{0,2},{1,3},{2,0},{3,1},{4,6},{5,7},{6,4},{7,5},{8,10},{9,11},{10,... | collective-permute-start | bytes 983048 | tf_op jit(solution)/shard_map/ppermute | solution.py:170
  124.2 1.3 collective-permute-start.2
  125.5 5.4 %collective-permute-done = bf16[128,1280]{1,0:T(8,128)(2,1)S(1)} collective-permute-done((bf16[128,1280]{1,0:T(8,128)(2,1)S(1)}, bf16[128,1280]{1,0:T(8,128)(2,1)S(1)}, u32[]{:S(2)}, u32[]{:S(2)}) %collective-permute-start) | collective-permute-done | bytes 327712 | tf_op jit(solution)/shard_map/ppermute | solution.py:170
  131.0 8.1 %collective-permute-done.1 = bf16[128,1280]{1,0:T(8,128)(2,1)} collective-permute-done((bf16[128,1280]{1,0:T(8,128)(2,1)S(1)}, bf16[128,1280]{1,0:T(8,128)(2,1)}, u32[]{:S(2)}, u32[]{:S(2)}) %collective-permute-start.1) | collective-permute-done | bytes 327712 | tf_op jit(solution)/shard_map/ppermute | solution.py:170
  139.1 1.0 constant_dynamic-update-slice_fusion.1
  140.1 0.9 copy-done.2
  141.0 3.9 %fusion.36 = f32[384,896]{1,0:T(8,128)} fusion(bf16[384,1280]{1,0:T(8,128)(2,1)S(1)} %constant_dynamic-update-slice_fusion, bf16[1280,896]{1,0:T(8,128)(2,1)} %param.21), kind=kOutput, calls=%fused_computation.97 | convolution fusion | flops 880803840 | bytes 4653056 | tf_op jit(solution)/shard_map/dot_general | solution.py:160
  145.0 5.6 %convolution_convert_fusion = bf16[384,1280]{1,0:T(8,128)(2,1)} fusion(bf16[896,1280]{1,0:T(8,128)(2,1)S(1)} %copy-done, f32[384,896]{1,0:T(8,128)} %fusion.36, bf16[384,1280]{1,0:T(8,128)(2,1)} %copy-done.2, bf16[1280,896]{1,0:T(8,128)(2,1)} %param.22), kind=kOutput, calls=%fused_computation.2 | convolution fusion | flops 1764163584 | bytes 7929856 | tf_op jit(solution)/shard_map/dot_general | solution.py:163
  150.6 2.1 fusion.33
  152.6 0.2 collective-permute-start.5
  152.8 2.2 collective-permute-start.4
  155.0 0.8 collective-permute-start.3
  155.9 2.2 fusion.31
  158.2 4.7 %collective-permute-done.5 = bf16[128,1280]{1,0:T(8,128)(2,1)} collective-permute-done((bf16[128,1280]{1,0:T(8,128)(2,1)}, bf16[128,1280]{1,0:T(8,128)(2,1)}, u32[]{:S(2)}, u32[]{:S(2)}) %collective-permute-start.5) | collective-permute-done | bytes 327712 | tf_op jit(solution)/shard_map/ppermute | solution.py:178
  162.8 6.9 %collective-permute-done.4 = bf16[128,1280]{1,0:T(8,128)(2,1)} collective-permute-done((bf16[128,1280]{1,0:T(8,128)(2,1)}, bf16[128,1280]{1,0:T(8,128)(2,1)}, u32[]{:S(2)}, u32[]{:S(2)}) %collective-permute-start.4) | collective-permute-done | bytes 327712 | tf_op jit(solution)/shard_map/ppermute | solution.py:178
  169.7 0.5 collective-permute-done.3
  170.3 2.9 %fusion.8 = bf16[128,1280]{1,0:T(8,128)(2,1)S(1)} fusion(bf16[128,1280]{1,0:T(8,128)(2,1)S(1)} %gather_fusion, bf16[128,1280]{1,0:T(8,128)(2,1)} %collective-permute-done.5, bf16[128,1280]{1,0:T(8,128)(2,1)} %collective-permute-done.4, bf16[128,1280]{1,0:T(8,128)(2,1)} %collective-permute-done.3, bf16[896,1280]{1,0:T(8,128)(2,1)S(1)} %copy-done, ...), kind=kOutput, calls=%fused_computation.23 | convolution fusion | flops 590348288 | bytes 6690304 | tf_op jit(solution)/shard_map/dot_general | solution.py:163
  173.2 2.9 %gather_fusion.1 = bf16[512,1280]{1,0:T(8,128)(2,1)} fusion(bf16[128,1280]{1,0:T(8,128)(2,1)S(1)} %fusion.8, s32[1024]{0:T(1024)S(1)} %pad_clamp_fusion), kind=kCustom, calls=%fused_computation.1 | custom fusion | bytes 2623488 | tf_op jit(solution)/shard_map/gather | solution.py:237
  176.1 3.2 %copy_select_fusion = bf16[8,64,1280]{2,0,1:T(8,128)(2,1)} fusion(bf16[8,64,1280]{2,1,0:T(8,128)(2,1)} %bitcast.47, pred[8,64]{0,1:T(8,128)(4,1)S(1)} %copy.52), kind=kLoop, calls=%fused_computation.12 | loop fusion | flops 655360 | bytes 2621952 | tf_op jit(solution)/shard_map/jit(_where)/select_n | solution.py:237
  179.3 7.7 %all-to-all-start.2 = ((bf16[8,64,1280]{2,0,1:T(8,128)(2,1)}), bf16[8,64,1280]{2,0,1:T(8,128)(2,1)}, u32[]{:S(2)}, u32[]{:S(2)}) async-start(bf16[8,64,1280]{2,0,1:T(8,128)(2,1)} %copy_select_fusion), calls=%async_computation.2 | async-start | bytes 2621440 | tf_op jit(solution)/shard_map/all_to_all | solution.py:238
  186.9 34.1 %all-to-all-done.2 = bf16[8,64,1280]{2,0,1:T(8,128)(2,1)} async-done(((bf16[8,64,1280]{2,0,1:T(8,128)(2,1)}), bf16[8,64,1280]{2,0,1:T(8,128)(2,1)}, u32[]{:S(2)}, u32[]{:S(2)}) %all-to-all-start.2) | async-done | bytes 1310752 | tf_op jit(solution)/shard_map/all_to_all | solution.py:238
  221.0 1.5 copy.62
  222.5 1.9 fusion.1
  (41 shorter events, 1.4 us)
Async XLA Ops:
  0.0 144.9 %copy-start = (bf16[896,1280]{1,0:T(8,128)(2,1)S(1)}, bf16[896,1280]{1,0:T(8,128)(2,1)}, u32[]{:S(2)}) copy-start(bf16[896,1280]{1,0:T(8,128)(2,1)} %param.23) | copy-start | bytes 6881284
  0.0 16.7 %copy-start.1 = (bf16[512,320]{0,1:T(8,128)(2,1)S(1)}, bf16[512,320]{0,1:T(8,128)(2,1)}, u32[]{:S(2)}) copy-start(bf16[512,320]{0,1:T(8,128)(2,1)} %param.16) | copy-start | bytes 983044
  1.4 62.8 %all-to-all-start = ((s32[64,1,128]{2,1,0:T(1,128)}), s32[64,1,128]{2,1,0:T(1,128)S(1)}, u32[]{:S(2)}, u32[]{:S(2)}) async-start(s32[64,1,128]{2,1,0:T(1,128)} %broadcast_in_dim.104), calls=%async_computation | async-start | bytes 65536 | tf_op jit(solution)/shard_map/all_to_all | solution.py:205
  16.7 1.2 copy-start.4
  70.1 44.5 %all-to-all-start.1 = ((bf16[8,64,1280]{2,0,1:T(8,128)(2,1)}), bf16[8,64,1280]{2,0,1:T(8,128)(2,1)}, u32[]{:S(2)}, u32[]{:S(2)}) async-start(bf16[8,64,1280]{2,0,1:T(8,128)(2,1)} %fusion.2), calls=%async_computation.1 | async-start | bytes 2621440 | tf_op jit(solution)/shard_map/all_to_all | solution.py:221
  117.2 2.8 %copy-start.3 = (f32[1280]{0:T(1024)S(1)}, f32[1280]{0:T(1024)}, u32[]{:S(2)}) copy-start(f32[1280]{0:T(1024)} %param.20) | copy-start | bytes 15364
  120.2 10.7 %collective-permute-start = (bf16[128,1280]{1,0:T(8,128)(2,1)S(1)}, bf16[128,1280]{1,0:T(8,128)(2,1)S(1)}, u32[]{:S(2)}, u32[]{:S(2)}) collective-permute-start(bf16[128,1280]{1,0:T(8,128)(2,1)S(1)} %fusion.7), channel_id=1, source_target_pairs={{0,1},{1,2},{2,3},{3,0},{4,5},{5,6},{6,7},{7,4},{8,9},{9,10},{10,1... | collective-permute-start | bytes 983048 | tf_op jit(solution)/shard_map/ppermute | solution.py:170
  121.5 17.6 %collective-permute-start.1 = (bf16[128,1280]{1,0:T(8,128)(2,1)S(1)}, bf16[128,1280]{1,0:T(8,128)(2,1)}, u32[]{:S(2)}, u32[]{:S(2)}) collective-permute-start(bf16[128,1280]{1,0:T(8,128)(2,1)S(1)} %fusion.7), channel_id=1, source_target_pairs={{0,2},{1,3},{2,0},{3,1},{4,6},{5,7},{6,4},{7,5},{8,10},{9,11},{10,... | collective-permute-start | bytes 983048 | tf_op jit(solution)/shard_map/ppermute | solution.py:170
  124.2 15.8 %collective-permute-start.2 = (bf16[128,1280]{1,0:T(8,128)(2,1)S(1)}, bf16[128,1280]{1,0:T(8,128)(2,1)S(1)}, u32[]{:S(2)}, u32[]{:S(2)}) collective-permute-start(bf16[128,1280]{1,0:T(8,128)(2,1)S(1)} %fusion.7), channel_id=1, source_target_pairs={{0,3},{1,0},{2,1},{3,2},{4,7},{5,4},{6,5},{7,6},{8,11},{9,8},{10,9... | collective-permute-start | bytes 983048 | tf_op jit(solution)/shard_map/ppermute | solution.py:170
  140.1 0.9 copy-start.2
  152.6 10.2 %collective-permute-start.5 = (bf16[128,1280]{1,0:T(8,128)(2,1)}, bf16[128,1280]{1,0:T(8,128)(2,1)}, u32[]{:S(2)}, u32[]{:S(2)}) collective-permute-start(bf16[128,1280]{1,0:T(8,128)(2,1)} %get-tuple-element.11), channel_id=1, source_target_pairs={{0,1},{1,2},{2,3},{3,0},{4,5},{5,6},{6,7},{7,4},{8,9},{9,10},{10,1... | collective-permute-start | bytes 983048 | tf_op jit(solution)/shard_map/ppermute | solution.py:178
  152.8 16.9 %collective-permute-start.4 = (bf16[128,1280]{1,0:T(8,128)(2,1)}, bf16[128,1280]{1,0:T(8,128)(2,1)}, u32[]{:S(2)}, u32[]{:S(2)}) collective-permute-start(bf16[128,1280]{1,0:T(8,128)(2,1)} %get-tuple-element.12), channel_id=1, source_target_pairs={{0,2},{1,3},{2,0},{3,1},{4,6},{5,7},{6,4},{7,5},{8,10},{9,11},{10,... | collective-permute-start | bytes 983048 | tf_op jit(solution)/shard_map/ppermute | solution.py:178
  155.0 15.2 %collective-permute-start.3 = (bf16[128,1280]{1,0:T(8,128)(2,1)S(1)}, bf16[128,1280]{1,0:T(8,128)(2,1)}, u32[]{:S(2)}, u32[]{:S(2)}) collective-permute-start(bf16[128,1280]{1,0:T(8,128)(2,1)S(1)} %get-tuple-element.10), channel_id=1, source_target_pairs={{0,3},{1,0},{2,1},{3,2},{4,7},{5,4},{6,5},{7,6},{8,11},{9,8},{10,9... | collective-permute-start | bytes 983048 | tf_op jit(solution)/shard_map/ppermute | solution.py:178
  179.3 41.7 %all-to-all-start.2 = ((bf16[8,64,1280]{2,0,1:T(8,128)(2,1)}), bf16[8,64,1280]{2,0,1:T(8,128)(2,1)}, u32[]{:S(2)}, u32[]{:S(2)}) async-start(bf16[8,64,1280]{2,0,1:T(8,128)(2,1)} %copy_select_fusion), calls=%async_computation.2 | async-start | bytes 2621440 | tf_op jit(solution)/shard_map/all_to_all | solution.py:238

commit v4 on v3

--- a/solution.py
+++ b/solution.py
@@ -59,7 +59,7 @@
         turned = jnp.dot(x, turn, preferred_element_type=jnp.float32)
         return (x.astype(jnp.float32) * cosine + turned * sine).astype(jnp.bfloat16)
 
-    q_rot = rotate(q_ref[...])
+    q_rot = rotate(q_ref[...]) * jnp.bfloat16(1.0 / math.sqrt(HEAD_SIZE))
     k_rot = rotate(k_ref[...])
     v = v_ref[...]
     lane = lax.broadcasted_iota(jnp.int32, (1, LANES), 1)
@@ -67,7 +67,6 @@
     zero = jnp.zeros((), jnp.bfloat16)
     q_low = jnp.where(low, q_rot, zero)
     q_high = jnp.where(low, zero, q_rot)
-    scale = 1.0 / math.sqrt(HEAD_SIZE)
     for i in range(slots // block):
         keys = block * (i + 1)
         k_part = k_rot[:keys]
@@ -79,7 +78,7 @@
                 qh[i * block:(i + 1) * block], k_part, (((1,), (1,)), ((), ())),
                 preferred_element_type=jnp.float32,
             )
-            scores = scores * scale + bias
+            scores = scores + bias
             largest = jnp.max(scores, axis=-1, keepdims=True)
             raised = jnp.exp(scores - largest)
             total = jnp.sum(raised, axis=-1, keepdims=True)
@@ -171,6 +170,7 @@
         for k in range(1, groups)
     ]
     own = ffn_rows(normed, gate_weight, up_weight, down_weight)
+    own, *arrived = lax.optimization_barrier((own, *arrived))
     others = ffn_rows(jnp.concatenate(arrived, axis=0), gate_weight, up_weight, down_weight)
     total = own.astype(jnp.float32)
     for k in range(1, groups):
@@ -198,13 +198,11 @@
         queries, projected_keys, projected_values, segment.reshape(slot_capacity), out_weight, hidden_in
     )
     slots = jnp.arange(slot_capacity, dtype=jnp.int32)
-    own_count = live_rows.reshape(())
+    own_count = live_rows[lax.axis_index("req"), lax.axis_index("grp")]
     request_owners = lax.axis_size("req")
     own_index = lax.axis_index("req")
     block_rows = slot_capacity // request_owners
-    counts = lax.all_to_all(
-        jnp.broadcast_to(live_rows.reshape(1, 1), (request_owners, LANES)), "req", 0, 0, tiled=True
-    )[:, 0]
+    counts = live_rows[:, lax.axis_index("grp")]
     ends = jnp.cumsum(counts)
     firsts = ends - counts
     owner_ids = jnp.arange(request_owners, dtype=jnp.int32)
@@ -246,7 +244,7 @@
         P(("req", "grp"), None),
         P(("req", "grp"), None),
         P("req", "grp", None),
-        P("req", "grp"),
+        P(),
         P(),
         P(),
         P(None, "grp"),

time: 225 us -> 289 us (1.28)
  blocking collectives: 0 us -> 81.4 us
  starting transfers between devices: 39.6 us -> 20.8 us
    unnamed x0 -> x1, blocking collectives: none -> 81.4 us
    all_to_all x1 -> x0, starting transfers between devices: 13.1 us -> none  [on_device(): lax.all_to_all(jnp.broadcast_to(live_rows.reshape(1, 1), (request_owners,...]
    ppermute x3, waiting for transfers between devices: 13.5 us -> 9.59 us  [feed_forward(): lax.ppermute(normed, 'grp', [(j, (j + k) % groups) for j in range(groups)])]
    all_to_all x1, starting transfers between devices: 10.5 us -> 6.59 us  [on_device(): lax.all_to_all(jnp.roll(kept.reshape(block_rows, request_owners, rows.sha...]
  transfers between devices with their start and end apart: 9 -> 8, of which waited for: 7 -> 6; matrix products, arithmetic and copies ran while one was open for 8% -> 2% of each run, Pallas kernels for 16% -> 0%
where the time goes in v4:
time: 289 us; the launch traced here: 288 us
  waiting for transfers between devices  91.8 us (32%)
  blocking collectives  81.4 us (28%)
  Pallas kernels  35.7 us (12%)
  local copies, waits for them, and re-layouts  24.7 us (9%)
  starting transfers between devices  20.8 us (7%)
  other arithmetic  15.2 us (5%)
  matrix products  15.1 us (5%)
  between operations  3.05 us (1%)
    unnamed x1, blocking collectives  81.4 us
    pallas_call x1, Pallas kernels, attend(): pl.pallas_call(attention_kernel, grid=(tiles,), in_specs=[pl.BlockSpec((s...  35.7 us
    all_to_all x1, waiting for transfers between devices, on_device(): lax.all_to_all(outgoing, 'req', split_axis=1, concat_axis=1, tiled=True)  34.1 us
    all_to_all x1, waiting for transfers between devices, on_device(): lax.all_to_all(jnp.roll(kept.reshape(block_rows, request_owners, rows.sha...  33.7 us
    ppermute x3, waiting for transfers between devices, feed_forward(): lax.ppermute(part, 'grp', [(j, (j - k) % groups) for j in range(groups)])  14.5 us
    ppermute x3, waiting for transfers between devices, feed_forward(): lax.ppermute(normed, 'grp', [(j, (j + k) % groups) for j in range(groups)])  9.59 us
    dot_general x2, matrix products, ffn_rows(): jnp.dot(hidden, down_weight, preferred_element_type=jnp.float32)  8.99 us
    all_to_all x1, starting transfers between devices, on_device(): lax.all_to_all(outgoing, 'req', split_axis=1, concat_axis=1, tiled=True)  7.15 us
  transfers between devices with their start and end apart: 8, of which 6 were waited for; matrix products, arithmetic and copies ran while one was open for 2% of the time, Pallas kernels for 0%

profile of v4, /device:TPU:1, one launch (start us, length us, event | category | flops | bytes accessed | tf_op | source)
XLA Modules:
  0.0 287.8 jit_solution(16917579606349470145)
XLA Ops:
  0.9 81.4 %all-reduce = s32[256]{0:T(256)S(1)} all-reduce(s32[256]{0:T(256)S(1)} %bitcast_dynamic-update-slice_fusion), channel_id=3, replica_groups=mesh['req'=64,'grp'=4] {'req','grp'}, use_global_device_ids=true, to_apply=%add | all-reduce | flops 256 | bytes 2048
  82.4 0.2 dynamic-slice_reduce_fusion
  82.8 0.6 fusion.24
  85.6 1.0 broadcast_in_dim.99
  86.6 1.1 copy.63.k_ref
  87.7 1.1 copy.64.v_ref
  89.0 0.3 reduce-window.19
  89.6 0.3 multiply_sine_fusion
  90.0 0.9 copy.65.cos_ref
  90.8 0.8 copy.66.sin_ref
  91.7 0.9 copy.67.segc_ref
  92.5 0.6 iota_subtract_fusion.posr_ref
  93.1 0.6 dynamic_slice.10
  93.7 0.6 iota_compare_fusion.2
  94.4 0.6 select_convert_fusion.turn_ref
  95.0 35.7 %shard_map.109 = bf16[512,1280]{1,0:T(8,128)(2,1)} custom-call(bf16[512,1280]{1,0:T(8,128)(2,1)} %q_ref.1, bf16[512,640]{1,0:T(8,128)(2,1)} %copy.63.k_ref, bf16[512,640]{1,0:T(8,128)(2,1)} %copy.64.v_ref, f32[512,128]{1,0:T(8,128)} %copy.65.cos_ref, f32[512,128]{1,0:T(8,128)} %copy.66.sin_ref, bf16[128,128]{1,0:T(8,128)(2,1)} %select_convert_fusion.turn_ref, ...), custom_call_target="tpu_custom_call" | custom-call | tf_op jit(solution)/shard_map/pallas_call | solution.py:115
  130.7 1.5 broadcast_select_fusion
  132.2 1.8 copy.68
  134.0 2.9 fusion.2
  136.8 6.6 %all-to-all-start = ((bf16[8,64,1280]{2,0,1:T(8,128)(2,1)}), bf16[8,64,1280]{2,0,1:T(8,128)(2,1)}, u32[]{:S(2)}, u32[]{:S(2)}) async-start(bf16[8,64,1280]{2,0,1:T(8,128)(2,1)} %fusion.2), calls=%async_computation | async-start | bytes 2621440 | tf_op jit(solution)/shard_map/all_to_all | solution.py:219
  143.8 33.7 %all-to-all-done = bf16[8,64,1280]{2,0,1:T(8,128)(2,1)} async-done(((bf16[8,64,1280]{2,0,1:T(8,128)(2,1)}), bf16[8,64,1280]{2,0,1:T(8,128)(2,1)}, u32[]{:S(2)}, u32[]{:S(2)}) %all-to-all-start) | async-done | bytes 1310752 | tf_op jit(solution)/shard_map/all_to_all | solution.py:219
  177.5 2.6 copy.70
  180.1 2.6 gather_fusion
  183.1 0.6 collective-permute-start
  183.7 1.2 collective-permute-start.1
  184.8 1.3 collective-permute-start.2
  186.1 2.2 fusion.30
  188.3 3.4 %convolution_convert_fusion.1 = bf16[128,1280]{1,0:T(8,128)(2,1)} fusion(bf16[896,1280]{1,0:T(8,128)(2,1)S(1)} %copy-done, bf16[128,1280]{1,0:T(8,128)(2,1)S(1)} %fusion.7, bf16[1280,896]{1,0:T(8,128)(2,1)} %param.22, f32[128,896]{1,0:T(8,128)S(1)} %fusion.30), kind=kOutput, calls=%fused_computation.7 | convolution fusion | flops 588054528 | bytes 5701632 | tf_op jit(solution)/shard_map/dot_general | solution.py:162
  191.7 9.2 %collective-permute-done = bf16[128,1280]{1,0:T(8,128)(2,1)} collective-permute-done((bf16[128,1280]{1,0:T(8,128)(2,1)S(1)}, bf16[128,1280]{1,0:T(8,128)(2,1)}, u32[]{:S(2)}, u32[]{:S(2)}) %collective-permute-start) | collective-permute-done | bytes 327712 | tf_op jit(solution)/shard_map/ppermute | solution.py:169
  200.9 0.3 collective-permute-done.2
  201.3 1.0 constant_dynamic-update-slice_fusion.2
  202.3 1.0 constant_dynamic-update-slice_fusion.1
  203.3 1.0 constant_dynamic-update-slice_fusion
  204.3 0.9 copy-done.4
  205.2 3.9 %fusion.31 = f32[384,896]{1,0:T(8,128)} fusion(bf16[384,1280]{1,0:T(8,128)(2,1)S(1)} %constant_dynamic-update-slice_fusion, bf16[1280,896]{1,0:T(8,128)(2,1)} %param.21), kind=kOutput, calls=%fused_computation.98 | convolution fusion | flops 880803840 | bytes 4653056 | tf_op jit(solution)/shard_map/dot_general | solution.py:159
  209.1 5.6 %convolution_convert_fusion = bf16[384,1280]{1,0:T(8,128)(2,1)} fusion(bf16[896,1280]{1,0:T(8,128)(2,1)S(1)} %copy-done, bf16[384,1280]{1,0:T(8,128)(2,1)} %copy-done.4, bf16[1280,896]{1,0:T(8,128)(2,1)} %param.22, f32[384,896]{1,0:T(8,128)} %fusion.31), kind=kOutput, calls=%fused_computation.2 | convolution fusion | flops 1764163584 | bytes 7929856 | tf_op jit(solution)/shard_map/dot_general | solution.py:162
  214.8 2.2 fusion.29
  216.9 0.7 collective-permute-start.5
  217.7 3.3 %collective-permute-start.4 = (bf16[128,1280]{1,0:T(8,128)(2,1)}, bf16[128,1280]{1,0:T(8,128)(2,1)}, u32[]{:S(2)}, u32[]{:S(2)}) collective-permute-start(bf16[128,1280]{1,0:T(8,128)(2,1)} %get-tuple-element.20), channel_id=1, source_target_pairs={{0,2},{1,3},{2,0},{3,1},{4,6},{5,7},{6,4},{7,5},{8,10},{9,11},{10,... | collective-permute-start | bytes 983048 | tf_op jit(solution)/shard_map/ppermute | solution.py:178
  221.1 5.8 %collective-permute-done.5 = bf16[128,1280]{1,0:T(8,128)(2,1)S(1)} collective-permute-done((bf16[128,1280]{1,0:T(8,128)(2,1)}, bf16[128,1280]{1,0:T(8,128)(2,1)S(1)}, u32[]{:S(2)}, u32[]{:S(2)}) %collective-permute-start.5) | collective-permute-done | bytes 327712 | tf_op jit(solution)/shard_map/ppermute | solution.py:178
  227.0 8.6 %collective-permute-done.4 = bf16[128,1280]{1,0:T(8,128)(2,1)} collective-permute-done((bf16[128,1280]{1,0:T(8,128)(2,1)}, bf16[128,1280]{1,0:T(8,128)(2,1)}, u32[]{:S(2)}, u32[]{:S(2)}) %collective-permute-start.4) | collective-permute-done | bytes 327712 | tf_op jit(solution)/shard_map/ppermute | solution.py:178
  235.6 1.4 fusion.8
  237.0 2.9 gather_fusion.1
  239.9 3.2 %copy_select_fusion = bf16[8,64,1280]{2,0,1:T(8,128)(2,1)} fusion(bf16[8,64,1280]{2,1,0:T(8,128)(2,1)} %bitcast.50, pred[8,64]{0,1:T(8,128)(4,1)S(1)} %copy.62), kind=kLoop, calls=%fused_computation.12 | loop fusion | flops 655360 | bytes 2621952 | tf_op jit(solution)/shard_map/jit(_where)/select_n | solution.py:235
  243.1 7.2 %all-to-all-start.1 = ((bf16[8,64,1280]{2,0,1:T(8,128)(2,1)}), bf16[8,64,1280]{2,0,1:T(8,128)(2,1)}, u32[]{:S(2)}, u32[]{:S(2)}) async-start(bf16[8,64,1280]{2,0,1:T(8,128)(2,1)} %copy_select_fusion), calls=%async_computation.1 | async-start | bytes 2621440 | tf_op jit(solution)/shard_map/all_to_all | solution.py:236
  250.2 34.1 %all-to-all-done.1 = bf16[8,64,1280]{2,0,1:T(8,128)(2,1)} async-done(((bf16[8,64,1280]{2,0,1:T(8,128)(2,1)}), bf16[8,64,1280]{2,0,1:T(8,128)(2,1)}, u32[]{:S(2)}, u32[]{:S(2)}) %all-to-all-start.1) | async-done | bytes 1310752 | tf_op jit(solution)/shard_map/all_to_all | solution.py:236
  284.3 1.5 copy.72
  285.8 1.9 fusion.1
  (49 shorter events, 1.9 us)
Async XLA Ops:
  0.0 188.3 %copy-start = (bf16[896,1280]{1,0:T(8,128)(2,1)S(1)}, bf16[896,1280]{1,0:T(8,128)(2,1)}, u32[]{:S(2)}) copy-start(bf16[896,1280]{1,0:T(8,128)(2,1)} %param.23) | copy-start | bytes 6881284
  0.0 87.7 %copy-start.1 = (bf16[512,320]{0,1:T(8,128)(2,1)S(1)}, bf16[512,320]{0,1:T(8,128)(2,1)}, u32[]{:S(2)}) copy-start(bf16[512,320]{0,1:T(8,128)(2,1)} %param.16) | copy-start | bytes 983044
  87.7 1.2 copy-start.5
  136.8 40.7 %all-to-all-start = ((bf16[8,64,1280]{2,0,1:T(8,128)(2,1)}), bf16[8,64,1280]{2,0,1:T(8,128)(2,1)}, u32[]{:S(2)}, u32[]{:S(2)}) async-start(bf16[8,64,1280]{2,0,1:T(8,128)(2,1)} %fusion.2), calls=%async_computation | async-start | bytes 2621440 | tf_op jit(solution)/shard_map/all_to_all | solution.py:219
  180.1 2.8 copy-start.6
  183.1 17.9 %collective-permute-start = (bf16[128,1280]{1,0:T(8,128)(2,1)S(1)}, bf16[128,1280]{1,0:T(8,128)(2,1)}, u32[]{:S(2)}, u32[]{:S(2)}) collective-permute-start(bf16[128,1280]{1,0:T(8,128)(2,1)S(1)} %fusion.7), channel_id=1, source_target_pairs={{0,1},{1,2},{2,3},{3,0},{4,5},{5,6},{6,7},{7,4},{8,9},{9,10},{10,1... | collective-permute-start | bytes 983048 | tf_op jit(solution)/shard_map/ppermute | solution.py:169
  183.7 17.3 %collective-permute-start.1 = (bf16[128,1280]{1,0:T(8,128)(2,1)S(1)}, bf16[128,1280]{1,0:T(8,128)(2,1)}, u32[]{:S(2)}, u32[]{:S(2)}) collective-permute-start(bf16[128,1280]{1,0:T(8,128)(2,1)S(1)} %fusion.7), channel_id=1, source_target_pairs={{0,2},{1,3},{2,0},{3,1},{4,6},{5,7},{6,4},{7,5},{8,10},{9,11},{10,... | collective-permute-start | bytes 983048 | tf_op jit(solution)/shard_map/ppermute | solution.py:169
  184.8 16.5 %collective-permute-start.2 = (bf16[128,1280]{1,0:T(8,128)(2,1)S(1)}, bf16[128,1280]{1,0:T(8,128)(2,1)}, u32[]{:S(2)}, u32[]{:S(2)}) collective-permute-start(bf16[128,1280]{1,0:T(8,128)(2,1)S(1)} %fusion.7), channel_id=1, source_target_pairs={{0,3},{1,0},{2,1},{3,2},{4,7},{5,4},{6,5},{7,6},{8,11},{9,8},{10,9... | collective-permute-start | bytes 983048 | tf_op jit(solution)/shard_map/ppermute | solution.py:169
  204.3 0.9 copy-start.4
  214.8 20.9 %copy-start.2 = (bf16[128,1280]{1,0:T(8,128)(2,1)S(1)}, bf16[128,1280]{1,0:T(8,128)(2,1)}, u32[]{:S(2)}) copy-start(bf16[128,1280]{1,0:T(8,128)(2,1)} %convolution_convert_fusion.1) | copy-start | bytes 983044
  216.9 10.0 %collective-permute-start.5 = (bf16[128,1280]{1,0:T(8,128)(2,1)}, bf16[128,1280]{1,0:T(8,128)(2,1)S(1)}, u32[]{:S(2)}, u32[]{:S(2)}) collective-permute-start(bf16[128,1280]{1,0:T(8,128)(2,1)} %get-tuple-element.19), channel_id=1, source_target_pairs={{0,1},{1,2},{2,3},{3,0},{4,5},{5,6},{6,7},{7,4},{8,9},{9,10},{10,1... | collective-permute-start | bytes 983048 | tf_op jit(solution)/shard_map/ppermute | solution.py:178
  217.7 17.9 %collective-permute-start.4 = (bf16[128,1280]{1,0:T(8,128)(2,1)}, bf16[128,1280]{1,0:T(8,128)(2,1)}, u32[]{:S(2)}, u32[]{:S(2)}) collective-permute-start(bf16[128,1280]{1,0:T(8,128)(2,1)} %get-tuple-element.20), channel_id=1, source_target_pairs={{0,2},{1,3},{2,0},{3,1},{4,6},{5,7},{6,4},{7,5},{8,10},{9,11},{10,... | collective-permute-start | bytes 983048 | tf_op jit(solution)/shard_map/ppermute | solution.py:178
  220.9 14.7 %collective-permute-start.3 = (bf16[128,1280]{1,0:T(8,128)(2,1)}, bf16[128,1280]{1,0:T(8,128)(2,1)}, u32[]{:S(2)}, u32[]{:S(2)}) collective-permute-start(bf16[128,1280]{1,0:T(8,128)(2,1)} %get-tuple-element.18), channel_id=1, source_target_pairs={{0,3},{1,0},{2,1},{3,2},{4,7},{5,4},{6,5},{7,6},{8,11},{9,8},{10,9... | collective-permute-start | bytes 983048 | tf_op jit(solution)/shard_map/ppermute | solution.py:178
  227.0 8.6 %copy-start.3 = (bf16[128,1280]{1,0:T(8,128)(2,1)}, bf16[128,1280]{1,0:T(8,128)(2,1)S(1)}, u32[]{:S(2)}) copy-start(bf16[128,1280]{1,0:T(8,128)(2,1)S(1)} %collective-permute-done.5) | copy-start | bytes 983044
  243.1 41.2 %all-to-all-start.1 = ((bf16[8,64,1280]{2,0,1:T(8,128)(2,1)}), bf16[8,64,1280]{2,0,1:T(8,128)(2,1)}, u32[]{:S(2)}, u32[]{:S(2)}) async-start(bf16[8,64,1280]{2,0,1:T(8,128)(2,1)} %copy_select_fusion), calls=%async_computation.1 | async-start | bytes 2621440 | tf_op jit(solution)/shard_map/all_to_all | solution.py:236

commit v5 on v3

--- a/solution.py
+++ b/solution.py
@@ -59,7 +59,7 @@
         turned = jnp.dot(x, turn, preferred_element_type=jnp.float32)
         return (x.astype(jnp.float32) * cosine + turned * sine).astype(jnp.bfloat16)
 
-    q_rot = rotate(q_ref[...])
+    q_rot = rotate(q_ref[...]) * jnp.bfloat16(1.0 / math.sqrt(HEAD_SIZE))
     k_rot = rotate(k_ref[...])
     v = v_ref[...]
     lane = lax.broadcasted_iota(jnp.int32, (1, LANES), 1)
@@ -67,7 +67,6 @@
     zero = jnp.zeros((), jnp.bfloat16)
     q_low = jnp.where(low, q_rot, zero)
     q_high = jnp.where(low, zero, q_rot)
-    scale = 1.0 / math.sqrt(HEAD_SIZE)
     for i in range(slots // block):
         keys = block * (i + 1)
         k_part = k_rot[:keys]
@@ -79,7 +78,7 @@
                 qh[i * block:(i + 1) * block], k_part, (((1,), (1,)), ((), ())),
                 preferred_element_type=jnp.float32,
             )
-            scores = scores * scale + bias
+            scores = scores + bias
             largest = jnp.max(scores, axis=-1, keepdims=True)
             raised = jnp.exp(scores - largest)
             total = jnp.sum(raised, axis=-1, keepdims=True)
@@ -171,6 +170,7 @@
         for k in range(1, groups)
     ]
     own = ffn_rows(normed, gate_weight, up_weight, down_weight)
+    own, *arrived = lax.optimization_barrier((own, *arrived))
     others = ffn_rows(jnp.concatenate(arrived, axis=0), gate_weight, up_weight, down_weight)
     total = own.astype(jnp.float32)
     for k in range(1, groups):

time: 225 us -> 226 us (level)
  waiting for transfers between devices: 93.5 us -> 89.8 us
    ppermute x3, waiting for transfers between devices: 13.5 us -> 8.36 us  [feed_forward(): lax.ppermute(normed, 'grp', [(j, (j + k) % groups) for j in range(groups)])]
  transfers between devices with their start and end apart: 9 -> 9, of which waited for: 7 -> 6; matrix products, arithmetic and copies ran while one was open for 8% -> 9% of each run, Pallas kernels for 16% -> 16%
where the time goes in v5:
time: 226 us; the launch traced here: 225 us
  waiting for transfers between devices  89.8 us (40%)
  starting transfers between devices  39.9 us (18%)
  Pallas kernels  35.7 us (16%)
  local copies, waits for them, and re-layouts  25.8 us (11%)
  other arithmetic  15.6 us (7%)
  matrix products  15.1 us (7%)
  between operations  3.01 us (1%)
    pallas_call x1, Pallas kernels, attend(): pl.pallas_call(attention_kernel, grid=(tiles,), in_specs=[pl.BlockSpec((s...  35.7 us
    all_to_all x1, waiting for transfers between devices, on_device(): lax.all_to_all(outgoing, 'req', split_axis=1, concat_axis=1, tiled=True)  34.1 us
    all_to_all x1, waiting for transfers between devices, on_device(): lax.all_to_all(jnp.roll(kept.reshape(block_rows, request_owners, rows.sha...  33.7 us
    ppermute x3, waiting for transfers between devices, feed_forward(): lax.ppermute(part, 'grp', [(j, (j - k) % groups) for j in range(groups)])  13.7 us
    all_to_all x1, starting transfers between devices, on_device(): lax.all_to_all(jnp.broadcast_to(live_rows.reshape(1, 1), (request_owners,...  13.1 us
    all_to_all x1, starting transfers between devices, on_device(): lax.all_to_all(jnp.roll(kept.reshape(block_rows, request_owners, rows.sha...  10.4 us
    dot_general x2, matrix products, ffn_rows(): jnp.dot(hidden, down_weight, preferred_element_type=jnp.float32)  8.99 us
    ppermute x3, waiting for transfers between devices, feed_forward(): lax.ppermute(normed, 'grp', [(j, (j + k) % groups) for j in range(groups)])  8.36 us
  transfers between devices with their start and end apart: 9, of which 6 were waited for; matrix products, arithmetic and copies ran while one was open for 9% of the time, Pallas kernels for 16%

profile of v5, /device:TPU:1, one launch (start us, length us, event | category | flops | bytes accessed | tf_op | source)
XLA Modules:
  0.0 224.9 jit_solution(12832279003977858071)
XLA Ops:
  0.8 0.6 broadcast_in_dim.104
  1.4 13.1 %all-to-all-start = ((s32[64,1,128]{2,1,0:T(1,128)}), s32[64,1,128]{2,1,0:T(1,128)S(1)}, u32[]{:S(2)}, u32[]{:S(2)}) async-start(s32[64,1,128]{2,1,0:T(1,128)} %broadcast_in_dim.104), calls=%async_computation | async-start | bytes 65536 | tf_op jit(solution)/shard_map/all_to_all | solution.py:205
  14.6 1.0 broadcast_in_dim.108
  15.7 1.1 copy.53.k_ref
  16.8 1.1 copy.54.v_ref
  18.1 0.3 reduce-window.19
  18.7 0.3 multiply_sine_fusion
  19.0 0.9 copy.55.cos_ref
  19.9 0.8 copy.56.sin_ref
  20.7 0.9 copy.57.segc_ref
  21.6 0.6 iota_subtract_fusion.posr_ref
  22.2 0.6 select_convert_fusion.turn_ref
  22.8 35.7 %shard_map.109 = bf16[512,1280]{1,0:T(8,128)(2,1)} custom-call(bf16[512,1280]{1,0:T(8,128)(2,1)} %q_ref.1, bf16[512,640]{1,0:T(8,128)(2,1)} %copy.53.k_ref, bf16[512,640]{1,0:T(8,128)(2,1)} %copy.54.v_ref, f32[512,128]{1,0:T(8,128)} %copy.55.cos_ref, f32[512,128]{1,0:T(8,128)} %copy.56.sin_ref, bf16[128,128]{1,0:T(8,128)(2,1)} %select_convert_fusion.turn_ref, ...), custom_call_target="tpu_custom_call" | custom-call | tf_op jit(solution)/shard_map/pallas_call | solution.py:115
  58.5 2.5 %broadcast_select_fusion = bf16[512,1280]{1,0:T(8,128)(2,1)} fusion(bf16[512,1280]{1,0:T(8,128)(2,1)} %shard_map.109, pred[512]{0:T(512)(128)(4,1)S(1)} %iota_compare_fusion.2), kind=kLoop, calls=%fused_computation.13 | loop fusion | flops 655360 | bytes 2621952 | tf_op jit(solution)/shard_map/jit(_where)/select_n | solution.py:220
  61.1 3.1 %copy.58 = bf16[8,64,1280]{2,0,1:T(8,128)(2,1)} copy(bf16[8,64,1280]{2,1,0:T(8,128)(2,1)} %bitcast.48) | data formatting | bytes 2621440 | tf_op jit(solution)/shard_map/reshape | solution.py:222
  64.5 0.6 fusion.24
  67.1 2.9 %fusion.2 = bf16[8,64,1280]{2,0,1:T(8,128)(2,1)} fusion(s32[]{:T(128)S(6)} %select_n.153, bf16[8,64,1280]{2,0,1:T(8,128)(2,1)} %copy.58), kind=kLoop, calls=%fused_computation.11 | loop fusion | flops 655360 | bytes 2621444 | tf_op jit(solution)/shard_map/jit(_roll_dynamic)/concatenate | solution.py:222
  70.0 10.4 %all-to-all-start.1 = ((bf16[8,64,1280]{2,0,1:T(8,128)(2,1)}), bf16[8,64,1280]{2,0,1:T(8,128)(2,1)}, u32[]{:S(2)}, u32[]{:S(2)}) async-start(bf16[8,64,1280]{2,0,1:T(8,128)(2,1)} %fusion.2), calls=%async_computation.1 | async-start | bytes 2621440 | tf_op jit(solution)/shard_map/all_to_all | solution.py:221
  80.9 33.7 %all-to-all-done.1 = bf16[8,64,1280]{2,0,1:T(8,128)(2,1)} async-done(((bf16[8,64,1280]{2,0,1:T(8,128)(2,1)}), bf16[8,64,1280]{2,0,1:T(8,128)(2,1)}, u32[]{:S(2)}, u32[]{:S(2)}) %all-to-all-start.1) | async-done | bytes 1310752 | tf_op jit(solution)/shard_map/all_to_all | solution.py:221
  114.6 2.6 %copy.60 = bf16[8,64,1280]{2,1,0:T(8,128)(2,1)} copy(bf16[8,64,1280]{2,0,1:T(8,128)(2,1)} %all-to-all-done.1) | data formatting | bytes 2621440 | tf_op jit(solution)/shard_map/all_to_all | solution.py:221
  117.2 2.6 %gather_fusion = bf16[128,1280]{1,0:T(8,128)(2,1)S(1)} fusion(bf16[512,1280]{1,0:T(8,128)(2,1)} %bitcast.47, s32[1024]{0:T(1024)S(1)} %pad_clamp_fusion.1), kind=kCustom, calls=%fused_computation | custom fusion | bytes 655872 | tf_op jit(solution)/shard_map/gather | solution.py:228
  119.8 0.1 fusion.5
  120.1 1.2 collective-permute-start
  121.4 2.4 %collective-permute-start.1 = (bf16[128,1280]{1,0:T(8,128)(2,1)S(1)}, bf16[128,1280]{1,0:T(8,128)(2,1)}, u32[]{:S(2)}, u32[]{:S(2)}) collective-permute-start(bf16[128,1280]{1,0:T(8,128)(2,1)S(1)} %fusion.7), channel_id=1, source_target_pairs={{0,2},{1,3},{2,0},{3,1},{4,6},{5,7},{6,4},{7,5},{8,10},{9,11},{10,... | collective-permute-start | bytes 983048 | tf_op jit(solution)/shard_map/ppermute | solution.py:169
  123.8 1.2 collective-permute-start.2
  125.0 2.2 fusion.30
  127.2 3.4 %convolution_convert_fusion.1 = bf16[128,1280]{1,0:T(8,128)(2,1)} fusion(bf16[896,1280]{1,0:T(8,128)(2,1)S(1)} %copy-done, bf16[128,1280]{1,0:T(8,128)(2,1)S(1)} %fusion.7, bf16[1280,896]{1,0:T(8,128)(2,1)} %param.22, f32[128,896]{1,0:T(8,128)S(1)} %fusion.30), kind=kOutput, calls=%fused_computation.7 | convolution fusion | flops 588054528 | bytes 5701632 | tf_op jit(solution)/shard_map/dot_general | solution.py:162
  130.6 0.4 collective-permute-done
  131.0 7.9 %collective-permute-done.1 = bf16[128,1280]{1,0:T(8,128)(2,1)} collective-permute-done((bf16[128,1280]{1,0:T(8,128)(2,1)S(1)}, bf16[128,1280]{1,0:T(8,128)(2,1)}, u32[]{:S(2)}, u32[]{:S(2)}) %collective-permute-start.1) | collective-permute-done | bytes 327712 | tf_op jit(solution)/shard_map/ppermute | solution.py:169
  138.9 1.0 constant_dynamic-update-slice_fusion.2
  139.9 1.0 constant_dynamic-update-slice_fusion.1
  140.9 1.0 constant_dynamic-update-slice_fusion
  142.0 0.9 copy-done.4
  142.9 3.9 %fusion.31 = f32[384,896]{1,0:T(8,128)} fusion(bf16[384,1280]{1,0:T(8,128)(2,1)S(1)} %constant_dynamic-update-slice_fusion, bf16[1280,896]{1,0:T(8,128)(2,1)} %param.21), kind=kOutput, calls=%fused_computation.96 | convolution fusion | flops 880803840 | bytes 4653056 | tf_op jit(solution)/shard_map/dot_general | solution.py:159
  146.8 5.6 %convolution_convert_fusion = bf16[384,1280]{1,0:T(8,128)(2,1)} fusion(bf16[896,1280]{1,0:T(8,128)(2,1)S(1)} %copy-done, bf16[384,1280]{1,0:T(8,128)(2,1)} %copy-done.4, bf16[1280,896]{1,0:T(8,128)(2,1)} %param.22, f32[384,896]{1,0:T(8,128)} %fusion.31), kind=kOutput, calls=%fused_computation.2 | convolution fusion | flops 1764163584 | bytes 7929856 | tf_op jit(solution)/shard_map/dot_general | solution.py:162
  152.4 2.2 fusion.29
  154.6 0.6 collective-permute-start.5
  155.2 2.8 %collective-permute-start.4 = (bf16[128,1280]{1,0:T(8,128)(2,1)}, bf16[128,1280]{1,0:T(8,128)(2,1)}, u32[]{:S(2)}, u32[]{:S(2)}) collective-permute-start(bf16[128,1280]{1,0:T(8,128)(2,1)} %get-tuple-element.20), channel_id=1, source_target_pairs={{0,2},{1,3},{2,0},{3,1},{4,6},{5,7},{6,4},{7,5},{8,10},{9,11},{10,... | collective-permute-start | bytes 983048 | tf_op jit(solution)/shard_map/ppermute | solution.py:178
  158.0 0.8 collective-permute-start.3
  159.0 5.6 %collective-permute-done.5 = bf16[128,1280]{1,0:T(8,128)(2,1)S(1)} collective-permute-done((bf16[128,1280]{1,0:T(8,128)(2,1)}, bf16[128,1280]{1,0:T(8,128)(2,1)S(1)}, u32[]{:S(2)}, u32[]{:S(2)}) %collective-permute-start.5) | collective-permute-done | bytes 327712 | tf_op jit(solution)/shard_map/ppermute | solution.py:178
  164.6 8.1 %collective-permute-done.4 = bf16[128,1280]{1,0:T(8,128)(2,1)} collective-permute-done((bf16[128,1280]{1,0:T(8,128)(2,1)}, bf16[128,1280]{1,0:T(8,128)(2,1)}, u32[]{:S(2)}, u32[]{:S(2)}) %collective-permute-start.4) | collective-permute-done | bytes 327712 | tf_op jit(solution)/shard_map/ppermute | solution.py:178
  172.7 1.4 fusion.8
  174.0 2.9 %gather_fusion.1 = bf16[512,1280]{1,0:T(8,128)(2,1)} fusion(bf16[128,1280]{1,0:T(8,128)(2,1)S(1)} %fusion.8, s32[1024]{0:T(1024)S(1)} %pad_clamp_fusion), kind=kCustom, calls=%fused_computation.1 | custom fusion | bytes 2623488 | tf_op jit(solution)/shard_map/gather | solution.py:237
  176.9 3.2 %copy_select_fusion = bf16[8,64,1280]{2,0,1:T(8,128)(2,1)} fusion(bf16[8,64,1280]{2,1,0:T(8,128)(2,1)} %bitcast.49, pred[8,64]{0,1:T(8,128)(4,1)S(1)} %copy.52), kind=kLoop, calls=%fused_computation.12 | loop fusion | flops 655360 | bytes 2621952 | tf_op jit(solution)/shard_map/jit(_where)/select_n | solution.py:237
  180.1 7.2 %all-to-all-start.2 = ((bf16[8,64,1280]{2,0,1:T(8,128)(2,1)}), bf16[8,64,1280]{2,0,1:T(8,128)(2,1)}, u32[]{:S(2)}, u32[]{:S(2)}) async-start(bf16[8,64,1280]{2,0,1:T(8,128)(2,1)} %copy_select_fusion), calls=%async_computation.2 | async-start | bytes 2621440 | tf_op jit(solution)/shard_map/all_to_all | solution.py:238
  187.3 34.1 %all-to-all-done.2 = bf16[8,64,1280]{2,0,1:T(8,128)(2,1)} async-done(((bf16[8,64,1280]{2,0,1:T(8,128)(2,1)}), bf16[8,64,1280]{2,0,1:T(8,128)(2,1)}, u32[]{:S(2)}, u32[]{:S(2)}) %all-to-all-start.2) | async-done | bytes 1310752 | tf_op jit(solution)/shard_map/all_to_all | solution.py:238
  221.4 1.5 copy.62
  222.9 1.9 fusion.1
  (46 shorter events, 1.7 us)
Async XLA Ops:
  0.0 127.2 %copy-start = (bf16[896,1280]{1,0:T(8,128)(2,1)S(1)}, bf16[896,1280]{1,0:T(8,128)(2,1)}, u32[]{:S(2)}) copy-start(bf16[896,1280]{1,0:T(8,128)(2,1)} %param.23) | copy-start | bytes 6881284
  0.0 16.7 %copy-start.1 = (bf16[512,320]{0,1:T(8,128)(2,1)S(1)}, bf16[512,320]{0,1:T(8,128)(2,1)}, u32[]{:S(2)}) copy-start(bf16[512,320]{0,1:T(8,128)(2,1)} %param.16) | copy-start | bytes 983044
  1.4 62.7 %all-to-all-start = ((s32[64,1,128]{2,1,0:T(1,128)}), s32[64,1,128]{2,1,0:T(1,128)S(1)}, u32[]{:S(2)}, u32[]{:S(2)}) async-start(s32[64,1,128]{2,1,0:T(1,128)} %broadcast_in_dim.104), calls=%async_computation | async-start | bytes 65536 | tf_op jit(solution)/shard_map/all_to_all | solution.py:205
  16.7 1.2 copy-start.5
  70.0 44.5 %all-to-all-start.1 = ((bf16[8,64,1280]{2,0,1:T(8,128)(2,1)}), bf16[8,64,1280]{2,0,1:T(8,128)(2,1)}, u32[]{:S(2)}, u32[]{:S(2)}) async-start(bf16[8,64,1280]{2,0,1:T(8,128)(2,1)} %fusion.2), calls=%async_computation.1 | async-start | bytes 2621440 | tf_op jit(solution)/shard_map/all_to_all | solution.py:221
  117.2 2.8 %copy-start.6 = (f32[1280]{0:T(1024)S(1)}, f32[1280]{0:T(1024)}, u32[]{:S(2)}) copy-start(f32[1280]{0:T(1024)} %param.20) | copy-start | bytes 15364
  120.1 10.8 %collective-permute-start = (bf16[128,1280]{1,0:T(8,128)(2,1)S(1)}, bf16[128,1280]{1,0:T(8,128)(2,1)}, u32[]{:S(2)}, u32[]{:S(2)}) collective-permute-start(bf16[128,1280]{1,0:T(8,128)(2,1)S(1)} %fusion.7), channel_id=1, source_target_pairs={{0,1},{1,2},{2,3},{3,0},{4,5},{5,6},{6,7},{7,4},{8,9},{9,10},{10,1... | collective-permute-start | bytes 983048 | tf_op jit(solution)/shard_map/ppermute | solution.py:169
  121.4 17.6 %collective-permute-start.1 = (bf16[128,1280]{1,0:T(8,128)(2,1)S(1)}, bf16[128,1280]{1,0:T(8,128)(2,1)}, u32[]{:S(2)}, u32[]{:S(2)}) collective-permute-start(bf16[128,1280]{1,0:T(8,128)(2,1)S(1)} %fusion.7), channel_id=1, source_target_pairs={{0,2},{1,3},{2,0},{3,1},{4,6},{5,7},{6,4},{7,5},{8,10},{9,11},{10,... | collective-permute-start | bytes 983048 | tf_op jit(solution)/shard_map/ppermute | solution.py:169
  123.8 15.1 %collective-permute-start.2 = (bf16[128,1280]{1,0:T(8,128)(2,1)S(1)}, bf16[128,1280]{1,0:T(8,128)(2,1)}, u32[]{:S(2)}, u32[]{:S(2)}) collective-permute-start(bf16[128,1280]{1,0:T(8,128)(2,1)S(1)} %fusion.7), channel_id=1, source_target_pairs={{0,3},{1,0},{2,1},{3,2},{4,7},{5,4},{6,5},{7,6},{8,11},{9,8},{10,9... | collective-permute-start | bytes 983048 | tf_op jit(solution)/shard_map/ppermute | solution.py:169
  141.9 0.9 copy-start.4
  152.4 20.3 %copy-start.2 = (bf16[128,1280]{1,0:T(8,128)(2,1)S(1)}, bf16[128,1280]{1,0:T(8,128)(2,1)}, u32[]{:S(2)}) copy-start(bf16[128,1280]{1,0:T(8,128)(2,1)} %convolution_convert_fusion.1) | copy-start | bytes 983044
  154.6 10.0 %collective-permute-start.5 = (bf16[128,1280]{1,0:T(8,128)(2,1)}, bf16[128,1280]{1,0:T(8,128)(2,1)S(1)}, u32[]{:S(2)}, u32[]{:S(2)}) collective-permute-start(bf16[128,1280]{1,0:T(8,128)(2,1)} %get-tuple-element.19), channel_id=1, source_target_pairs={{0,1},{1,2},{2,3},{3,0},{4,5},{5,6},{6,7},{7,4},{8,9},{9,10},{10,1... | collective-permute-start | bytes 983048 | tf_op jit(solution)/shard_map/ppermute | solution.py:178
  155.2 17.5 %collective-permute-start.4 = (bf16[128,1280]{1,0:T(8,128)(2,1)}, bf16[128,1280]{1,0:T(8,128)(2,1)}, u32[]{:S(2)}, u32[]{:S(2)}) collective-permute-start(bf16[128,1280]{1,0:T(8,128)(2,1)} %get-tuple-element.20), channel_id=1, source_target_pairs={{0,2},{1,3},{2,0},{3,1},{4,6},{5,7},{6,4},{7,5},{8,10},{9,11},{10,... | collective-permute-start | bytes 983048 | tf_op jit(solution)/shard_map/ppermute | solution.py:178
  158.0 14.7 %collective-permute-start.3 = (bf16[128,1280]{1,0:T(8,128)(2,1)}, bf16[128,1280]{1,0:T(8,128)(2,1)}, u32[]{:S(2)}, u32[]{:S(2)}) collective-permute-start(bf16[128,1280]{1,0:T(8,128)(2,1)} %get-tuple-element.18), channel_id=1, source_target_pairs={{0,3},{1,0},{2,1},{3,2},{4,7},{5,4},{6,5},{7,6},{8,11},{9,8},{10,9... | collective-permute-start | bytes 983048 | tf_op jit(solution)/shard_map/ppermute | solution.py:178
  164.6 8.1 %copy-start.3 = (bf16[128,1280]{1,0:T(8,128)(2,1)}, bf16[128,1280]{1,0:T(8,128)(2,1)S(1)}, u32[]{:S(2)}) copy-start(bf16[128,1280]{1,0:T(8,128)(2,1)S(1)} %collective-permute-done.5) | copy-start | bytes 983044
  180.1 41.3 %all-to-all-start.2 = ((bf16[8,64,1280]{2,0,1:T(8,128)(2,1)}), bf16[8,64,1280]{2,0,1:T(8,128)(2,1)}, u32[]{:S(2)}, u32[]{:S(2)}) async-start(bf16[8,64,1280]{2,0,1:T(8,128)(2,1)} %copy_select_fusion), calls=%async_computation.2 | async-start | bytes 2621440 | tf_op jit(solution)/shard_map/all_to_all | solution.py:238

commit v6 on v5

--- a/solution.py
+++ b/solution.py
@@ -210,21 +210,17 @@
     owner_ids = jnp.arange(request_owners, dtype=jnp.int32)
     own_first = jnp.sum(jnp.where(owner_ids == own_index, firsts, 0))
     own_shift = own_first % request_owners
-    keep = slots < own_count
     stream = jnp.arange(BAL, dtype=jnp.int32) * request_owners + own_index
     source = jnp.sum((ends[None, :] <= stream[:, None]).astype(jnp.int32), axis=1)
     source_first = jnp.sum(
         jnp.where(source[:, None] == owner_ids[None, :], firsts[None, :], 0), axis=1
     )
-    pick = (stream - source_first) // request_owners * request_owners + source
-    kept = jnp.where(keep[:, None], rows, jnp.zeros_like(rows))
-    arrived = lax.all_to_all(
-        jnp.roll(kept.reshape(block_rows, request_owners, rows.shape[1]), own_shift, axis=1),
-        "req",
-        split_axis=1,
-        concat_axis=1,
-        tiled=True,
-    )
+    pick = source * block_rows + (stream - source_first) // request_owners
+    dest = jnp.arange(request_owners, dtype=jnp.int32)[:, None]
+    blocks = jnp.arange(block_rows, dtype=jnp.int32)[None, :]
+    send_row = blocks * request_owners + (dest - own_shift) % request_owners
+    outbound = jnp.where((send_row < own_count)[:, :, None], rows[send_row], jnp.zeros((), rows.dtype))
+    arrived = lax.all_to_all(outbound, "req", 0, 0, tiled=True)
     mixed = arrived.reshape(slot_capacity, -1)[pick]
     normed = normalize(mixed, norm_gain)
     result = (
@@ -234,9 +230,10 @@
     source_row = jnp.arange(block_rows, dtype=jnp.int32)[:, None] * request_owners + lanes[None, :]
     valid = source_row < counts[None, :]
     target = jnp.where(valid, (firsts[None, :] + source_row) // request_owners, 0)
-    outgoing = jnp.where(valid[:, :, None], result[target], jnp.zeros((), jnp.bfloat16))
-    returned = lax.all_to_all(outgoing, "req", split_axis=1, concat_axis=1, tiled=True)
-    return jnp.roll(returned, -own_shift, axis=1).reshape(slot_capacity, -1)
+    outgoing = jnp.where(valid.T[:, :, None], result[target.T], jnp.zeros((), jnp.bfloat16))
+    returned = lax.all_to_all(outgoing, "req", 0, 0, tiled=True).reshape(slot_capacity, -1)
+    back_row = ((slots % request_owners + own_shift) % request_owners) * block_rows + slots // request_owners
+    return returned[back_row]
 
 
 def solution(mesh):

time: 226 us -> 227 us (level)
  other arithmetic: 15.6 us -> 11 us
  waiting for transfers between devices: 89.8 us -> 93.7 us
  local copies, waits for them, and re-layouts: 25.8 us -> 29.6 us
  starting transfers between devices: 39.9 us -> 37.6 us
    gather x1 -> x3, local copies, waits for them, and re-layouts: 2.87 us -> 13.7 us  [the longest x1 5.42 us: on_device(): rows[send_row]]
    concatenate x2 -> x0, other arithmetic: 4.86 us -> none  [the longest x1 2.92 us: on_device(): jnp.roll(kept.reshape(block_rows, request_owners, rows.shape[1]), own_shi...]
    all_to_all x2 -> x0, local copies, waits for them, and re-layouts: 4.13 us -> none  [the longest x1 2.59 us: on_device(): lax.all_to_all(jnp.roll(kept.reshape(block_rows, request_owners, rows.sha...]
    ppermute x3, waiting for transfers between devices: 8.36 us -> 11.6 us  [feed_forward(): lax.ppermute(normed, 'grp', [(j, (j + k) % groups) for j in range(groups)])]
    reshape x1 -> x0, local copies, waits for them, and re-layouts: 3.1 us -> none  [on_device(): kept.reshape(block_rows, request_owners, rows.shape[1])]
    select_n x3 -> x5, other arithmetic: 5.81 us -> 5.23 us  [the longest x1 2.56 us: on_device(): jnp.where(valid.T[:, :, None], result[target.T], jnp.zeros((), jnp.bfloat...]
  transfers between devices with their start and end apart: 9 -> 9, of which waited for: 6 -> 7; matrix products, arithmetic and copies ran while one was open for 9% -> 7% of each run, Pallas kernels for 16% -> 16%
where the time goes in v6:
time: 227 us; the launch traced here: 226 us
  waiting for transfers between devices  93.7 us (41%)
  starting transfers between devices  37.6 us (17%)
  Pallas kernels  35.7 us (16%)
  local copies, waits for them, and re-layouts  29.6 us (13%)
  matrix products  15.1 us (7%)
  other arithmetic  11 us (5%)
  between operations  3.12 us (1%)
    pallas_call x1, Pallas kernels, attend(): pl.pallas_call(attention_kernel, grid=(tiles,), in_specs=[pl.BlockSpec((s...  35.7 us
    all_to_all x1, waiting for transfers between devices, on_device(): lax.all_to_all(outgoing, 'req', 0, 0, tiled=True).reshape(slot_capacity, -1)  34 us
    all_to_all x1, waiting for transfers between devices, on_device(): arrived = lax.all_to_all(outbound, 'req', 0, 0, tiled=True)  33.8 us
    ppermute x3, waiting for transfers between devices, feed_forward(): lax.ppermute(part, 'grp', [(j, (j - k) % groups) for j in range(groups)])  14.2 us
    all_to_all x1, starting transfers between devices, on_device(): lax.all_to_all(jnp.broadcast_to(live_rows.reshape(1, 1), (request_owners,...  13.1 us
    ppermute x3, waiting for transfers between devices, feed_forward(): lax.ppermute(normed, 'grp', [(j, (j + k) % groups) for j in range(groups)])  11.6 us
    all_to_all x1, starting transfers between devices, on_device(): arrived = lax.all_to_all(outbound, 'req', 0, 0, tiled=True)  10.5 us
    dot_general x2, matrix products, ffn_rows(): jnp.dot(hidden, down_weight, preferred_element_type=jnp.float32)  8.99 us
  transfers between devices with their start and end apart: 9, of which 7 were waited for; matrix products, arithmetic and copies ran while one was open for 7% of the time, Pallas kernels for 16%

profile of v6, /device:TPU:1, one launch (start us, length us, event | category | flops | bytes accessed | tf_op | source)
XLA Modules:
  0.0 225.8 jit_solution(3499001107586481882)
XLA Ops:
  0.8 0.6 broadcast_in_dim.105
  1.4 13.1 %all-to-all-start = ((s32[64,1,128]{2,1,0:T(1,128)}), s32[64,1,128]{2,1,0:T(1,128)S(1)}, u32[]{:S(2)}, u32[]{:S(2)}) async-start(s32[64,1,128]{2,1,0:T(1,128)} %broadcast_in_dim.105), calls=%async_computation | async-start | bytes 65536 | tf_op jit(solution)/shard_map/all_to_all | solution.py:205
  14.6 0.8 compare_reduce_fusion
  15.6 0.3 reduce-window.19
  16.0 0.1 slice_reduce_fusion
  16.2 0.6 iota_subtract_fusion.posr_ref
  16.8 0.3 multiply_sine_fusion
  17.1 0.8 copy.41.sin_ref
  18.0 0.9 copy.40.cos_ref
  18.8 0.9 copy.42.segc_ref
  19.7 1.1 copy.38.k_ref
  20.8 1.0 broadcast_in_dim.111
  21.8 1.1 copy.39.v_ref
  22.9 0.6 select_convert_fusion.turn_ref
  23.6 35.7 %shard_map.109 = bf16[512,1280]{1,0:T(8,128)(2,1)} custom-call(bf16[512,1280]{1,0:T(8,128)(2,1)} %q_ref.1, bf16[512,640]{1,0:T(8,128)(2,1)} %copy.38.k_ref, bf16[512,640]{1,0:T(8,128)(2,1)} %copy.39.v_ref, f32[512,128]{1,0:T(8,128)} %copy.40.cos_ref, f32[512,128]{1,0:T(8,128)} %copy.41.sin_ref, bf16[128,128]{1,0:T(8,128)(2,1)} %select_convert_fusion.turn_ref, ...), custom_call_target="tpu_custom_call" | custom-call | tf_op jit(solution)/shard_map/pallas_call | solution.py:115
  59.6 0.7 fusion.26
  62.8 5.4 %gather_fusion = bf16[512,1280]{1,0:T(8,128)(2,1)} fusion(bf16[512,1280]{1,0:T(8,128)(2,1)} %shard_map.109, s32[1024]{0:T(1024)S(1)} %pad_clamp_fusion.3), kind=kCustom, calls=%fused_computation | custom fusion | bytes 2623488 | tf_op jit(solution)/shard_map/gather | solution.py:222
  68.3 2.5 %bitcast_select_fusion.1 = bf16[64,8,1280]{2,1,0:T(8,128)(2,1)} fusion(bf16[512,1280]{1,0:T(8,128)(2,1)} %gather_fusion, pred[64,8]{1,0:T(8,128)(4,1)S(1)} %copy.37), kind=kLoop, calls=%fused_computation.9 | loop fusion | flops 655360 | bytes 2621952 | tf_op jit(solution)/shard_map/jit(_where)/select_n | solution.py:222
  70.8 10.5 %all-to-all-start.1 = ((bf16[64,8,1280]{2,1,0:T(8,128)(2,1)}), bf16[64,8,1280]{2,1,0:T(8,128)(2,1)}, u32[]{:S(2)}, u32[]{:S(2)}) async-start(bf16[64,8,1280]{2,1,0:T(8,128)(2,1)} %bitcast_select_fusion.1), calls=%async_computation.1 | async-start | bytes 2621440 | tf_op jit(solution)/shard_map/all_to_all | solution.py:223
  81.5 33.8 %all-to-all-done.1 = bf16[64,8,1280]{2,1,0:T(8,128)(2,1)} async-done(((bf16[64,8,1280]{2,1,0:T(8,128)(2,1)}), bf16[64,8,1280]{2,1,0:T(8,128)(2,1)}, u32[]{:S(2)}, u32[]{:S(2)}) %all-to-all-start.1) | async-done | bytes 1310752 | tf_op jit(solution)/shard_map/all_to_all | solution.py:223
  115.4 2.6 %gather_fusion.1 = bf16[128,1280]{1,0:T(8,128)(2,1)S(1)} fusion(bf16[512,1280]{1,0:T(8,128)(2,1)} %bitcast.14, s32[1024]{0:T(1024)S(1)} %pad_clamp_fusion.2), kind=kCustom, calls=%fused_computation.1 | custom fusion | bytes 655872 | tf_op jit(solution)/shard_map/gather | solution.py:224
  118.0 0.1 fusion.3
  118.2 0.1 fusion.5
  118.3 2.5 %collective-permute-start.2 = (bf16[128,1280]{1,0:T(8,128)(2,1)S(1)}, bf16[128,1280]{1,0:T(8,128)(2,1)}, u32[]{:S(2)}, u32[]{:S(2)}) collective-permute-start(bf16[128,1280]{1,0:T(8,128)(2,1)S(1)} %fusion.5), channel_id=1, source_target_pairs={{0,3},{1,0},{2,1},{3,2},{4,7},{5,4},{6,5},{7,6},{8,11},{9,8},{10,9... | collective-permute-start | bytes 983048 | tf_op jit(solution)/shard_map/ppermute | solution.py:169
  120.9 0.5 collective-permute-start.1
  121.4 0.6 collective-permute-start
  122.0 2.2 fusion.33
  124.2 3.4 %convolution_convert_fusion.1 = bf16[128,1280]{1,0:T(8,128)(2,1)} fusion(bf16[896,1280]{1,0:T(8,128)(2,1)S(1)} %copy-done, bf16[128,1280]{1,0:T(8,128)(2,1)S(1)} %fusion.5, bf16[1280,896]{1,0:T(8,128)(2,1)} %param.20, f32[128,896]{1,0:T(8,128)S(1)} %fusion.33), kind=kOutput, calls=%fused_computation.5 | convolution fusion | flops 588054528 | bytes 5701632 | tf_op jit(solution)/shard_map/dot_general | solution.py:162
  127.6 7.5 %collective-permute-done.2 = bf16[128,1280]{1,0:T(8,128)(2,1)} collective-permute-done((bf16[128,1280]{1,0:T(8,128)(2,1)S(1)}, bf16[128,1280]{1,0:T(8,128)(2,1)}, u32[]{:S(2)}, u32[]{:S(2)}) %collective-permute-start.2) | collective-permute-done | bytes 327712 | tf_op jit(solution)/shard_map/ppermute | solution.py:169
  135.0 4.1 %collective-permute-done = bf16[128,1280]{1,0:T(8,128)(2,1)} collective-permute-done((bf16[128,1280]{1,0:T(8,128)(2,1)S(1)}, bf16[128,1280]{1,0:T(8,128)(2,1)}, u32[]{:S(2)}, u32[]{:S(2)}) %collective-permute-start) | collective-permute-done | bytes 327712 | tf_op jit(solution)/shard_map/ppermute | solution.py:169
  139.2 1.0 constant_dynamic-update-slice_fusion.2
  140.2 1.0 constant_dynamic-update-slice_fusion.1
  141.2 1.0 constant_dynamic-update-slice_fusion
  142.2 0.9 copy-done.4
  143.1 3.9 %fusion.34 = f32[384,896]{1,0:T(8,128)} fusion(bf16[384,1280]{1,0:T(8,128)(2,1)S(1)} %constant_dynamic-update-slice_fusion, bf16[1280,896]{1,0:T(8,128)(2,1)} %param.19), kind=kOutput, calls=%fused_computation.111 | convolution fusion | flops 880803840 | bytes 4653056 | tf_op jit(solution)/shard_map/dot_general | solution.py:159
  147.0 5.6 %convolution_convert_fusion = bf16[384,1280]{1,0:T(8,128)(2,1)} fusion(bf16[896,1280]{1,0:T(8,128)(2,1)S(1)} %copy-done, bf16[384,1280]{1,0:T(8,128)(2,1)} %copy-done.4, bf16[1280,896]{1,0:T(8,128)(2,1)} %param.20, f32[384,896]{1,0:T(8,128)} %fusion.34), kind=kOutput, calls=%fused_computation.4 | convolution fusion | flops 1764163584 | bytes 7929856 | tf_op jit(solution)/shard_map/dot_general | solution.py:162
  152.6 2.2 fusion.32
  154.8 1.5 collective-permute-start.5
  156.3 0.5 collective-permute-start.4
  157.0 6.9 %collective-permute-done.3 = bf16[128,1280]{1,0:T(8,128)(2,1)S(1)} collective-permute-done((bf16[128,1280]{1,0:T(8,128)(2,1)}, bf16[128,1280]{1,0:T(8,128)(2,1)S(1)}, u32[]{:S(2)}, u32[]{:S(2)}) %collective-permute-start.3) | collective-permute-done | bytes 327712 | tf_op jit(solution)/shard_map/ppermute | solution.py:178
  163.9 1.0 collective-permute-done.5
  164.9 6.3 %collective-permute-done.4 = bf16[128,1280]{1,0:T(8,128)(2,1)} collective-permute-done((bf16[128,1280]{1,0:T(8,128)(2,1)}, bf16[128,1280]{1,0:T(8,128)(2,1)}, u32[]{:S(2)}, u32[]{:S(2)}) %collective-permute-start.4) | collective-permute-done | bytes 327712 | tf_op jit(solution)/shard_map/ppermute | solution.py:178
  171.2 1.4 fusion.6
  172.6 2.9 %gather_fusion.2 = bf16[512,1280]{1,0:T(8,128)(2,1)} fusion(bf16[128,1280]{1,0:T(8,128)(2,1)S(1)} %fusion.6, s32[1024]{0:T(1024)S(1)} %pad_clamp_fusion.1), kind=kCustom, calls=%fused_computation.2 | custom fusion | bytes 2623488 | tf_op jit(solution)/shard_map/gather | solution.py:233
  175.5 2.6 %bitcast_select_fusion = bf16[64,8,1280]{2,1,0:T(8,128)(2,1)} fusion(bf16[512,1280]{1,0:T(8,128)(2,1)} %gather_fusion.2, pred[64,8]{1,0:T(8,128)(4,1)S(1)} %copy.36), kind=kLoop, calls=%fused_computation.8 | loop fusion | flops 655360 | bytes 2621952 | tf_op jit(solution)/shard_map/jit(_where)/select_n | solution.py:233
  178.0 8.3 %all-to-all-start.2 = ((bf16[64,8,1280]{2,1,0:T(8,128)(2,1)}), bf16[64,8,1280]{2,1,0:T(8,128)(2,1)}, u32[]{:S(2)}, u32[]{:S(2)}) async-start(bf16[64,8,1280]{2,1,0:T(8,128)(2,1)} %bitcast_select_fusion), calls=%async_computation.2 | async-start | bytes 2621440 | tf_op jit(solution)/shard_map/all_to_all | solution.py:234
  186.4 34.0 %all-to-all-done.2 = bf16[64,8,1280]{2,1,0:T(8,128)(2,1)} async-done(((bf16[64,8,1280]{2,1,0:T(8,128)(2,1)}), bf16[64,8,1280]{2,1,0:T(8,128)(2,1)}, u32[]{:S(2)}, u32[]{:S(2)}) %all-to-all-start.2) | async-done | bytes 1310752 | tf_op jit(solution)/shard_map/all_to_all | solution.py:234
  220.4 5.4 %gather_fusion.3 = bf16[512,1280]{1,0:T(8,128)(2,1)} fusion(bf16[512,1280]{1,0:T(8,128)(2,1)} %bitcast.19, s32[1024]{0:T(1024)S(1)} %pad_clamp_fusion), kind=kCustom, calls=%fused_computation.3 | custom fusion | bytes 2623488 | tf_op jit(solution)/shard_map/gather | solution.py:236
  (48 shorter events, 1.6 us)
Async XLA Ops:
  0.0 124.2 %copy-start = (bf16[896,1280]{1,0:T(8,128)(2,1)S(1)}, bf16[896,1280]{1,0:T(8,128)(2,1)}, u32[]{:S(2)}) copy-start(bf16[896,1280]{1,0:T(8,128)(2,1)} %param.21) | copy-start | bytes 6881284
  0.0 18.8 %copy-start.5 = (s32[1,1,512]{2,1,0:T(1,128)S(1)}, s32[1,1,512]{2,1,0:T(1,128)}, u32[]{:S(2)}) copy-start(s32[1,1,512]{2,1,0:T(1,128)} %param.15) | copy-start | bytes 6148
  0.0 19.7 %copy-start.1 = (bf16[512,320]{0,1:T(8,128)(2,1)S(1)}, bf16[512,320]{0,1:T(8,128)(2,1)}, u32[]{:S(2)}) copy-start(bf16[512,320]{0,1:T(8,128)(2,1)} %param.13) | copy-start | bytes 983044
  1.4 57.9 %all-to-all-start = ((s32[64,1,128]{2,1,0:T(1,128)}), s32[64,1,128]{2,1,0:T(1,128)S(1)}, u32[]{:S(2)}, u32[]{:S(2)}) async-start(s32[64,1,128]{2,1,0:T(1,128)} %broadcast_in_dim.105), calls=%async_computation | async-start | bytes 65536 | tf_op jit(solution)/shard_map/all_to_all | solution.py:205
  70.8 44.6 %all-to-all-start.1 = ((bf16[64,8,1280]{2,1,0:T(8,128)(2,1)}), bf16[64,8,1280]{2,1,0:T(8,128)(2,1)}, u32[]{:S(2)}, u32[]{:S(2)}) async-start(bf16[64,8,1280]{2,1,0:T(8,128)(2,1)} %bitcast_select_fusion.1), calls=%async_computation.1 | async-start | bytes 2621440 | tf_op jit(solution)/shard_map/all_to_all | solution.py:223
  115.4 2.8 %copy-start.6 = (f32[1280]{0:T(1024)S(1)}, f32[1280]{0:T(1024)}, u32[]{:S(2)}) copy-start(f32[1280]{0:T(1024)} %param.18) | copy-start | bytes 15364
  118.3 16.7 %collective-permute-start.2 = (bf16[128,1280]{1,0:T(8,128)(2,1)S(1)}, bf16[128,1280]{1,0:T(8,128)(2,1)}, u32[]{:S(2)}, u32[]{:S(2)}) collective-permute-start(bf16[128,1280]{1,0:T(8,128)(2,1)S(1)} %fusion.5), channel_id=1, source_target_pairs={{0,3},{1,0},{2,1},{3,2},{4,7},{5,4},{6,5},{7,6},{8,11},{9,8},{10,9... | collective-permute-start | bytes 983048 | tf_op jit(solution)/shard_map/ppermute | solution.py:169
  120.9 14.1 %collective-permute-start.1 = (bf16[128,1280]{1,0:T(8,128)(2,1)S(1)}, bf16[128,1280]{1,0:T(8,128)(2,1)}, u32[]{:S(2)}, u32[]{:S(2)}) collective-permute-start(bf16[128,1280]{1,0:T(8,128)(2,1)S(1)} %fusion.5), channel_id=1, source_target_pairs={{0,2},{1,3},{2,0},{3,1},{4,6},{5,7},{6,4},{7,5},{8,10},{9,11},{10,... | collective-permute-start | bytes 983048 | tf_op jit(solution)/shard_map/ppermute | solution.py:169
  121.4 17.8 %collective-permute-start = (bf16[128,1280]{1,0:T(8,128)(2,1)S(1)}, bf16[128,1280]{1,0:T(8,128)(2,1)}, u32[]{:S(2)}, u32[]{:S(2)}) collective-permute-start(bf16[128,1280]{1,0:T(8,128)(2,1)S(1)} %fusion.5), channel_id=1, source_target_pairs={{0,1},{1,2},{2,3},{3,0},{4,5},{5,6},{6,7},{7,4},{8,9},{9,10},{10,1... | collective-permute-start | bytes 983048 | tf_op jit(solution)/shard_map/ppermute | solution.py:169
  142.2 0.9 copy-start.4
  152.6 18.6 %copy-start.2 = (bf16[128,1280]{1,0:T(8,128)(2,1)S(1)}, bf16[128,1280]{1,0:T(8,128)(2,1)}, u32[]{:S(2)}) copy-start(bf16[128,1280]{1,0:T(8,128)(2,1)} %convolution_convert_fusion.1) | copy-start | bytes 983044
  154.8 9.1 %collective-permute-start.3 = (bf16[128,1280]{1,0:T(8,128)(2,1)}, bf16[128,1280]{1,0:T(8,128)(2,1)S(1)}, u32[]{:S(2)}, u32[]{:S(2)}) collective-permute-start(bf16[128,1280]{1,0:T(8,128)(2,1)} %get-tuple-element.17), channel_id=1, source_target_pairs={{0,3},{1,0},{2,1},{3,2},{4,7},{5,4},{6,5},{7,6},{8,11},{9,8},{10,9... | collective-permute-start | bytes 983048 | tf_op jit(solution)/shard_map/ppermute | solution.py:178
  154.8 10.1 %collective-permute-start.5 = (bf16[128,1280]{1,0:T(8,128)(2,1)}, bf16[128,1280]{1,0:T(8,128)(2,1)}, u32[]{:S(2)}, u32[]{:S(2)}) collective-permute-start(bf16[128,1280]{1,0:T(8,128)(2,1)} %get-tuple-element.18), channel_id=1, source_target_pairs={{0,1},{1,2},{2,3},{3,0},{4,5},{5,6},{6,7},{7,4},{8,9},{9,10},{10,1... | collective-permute-start | bytes 983048 | tf_op jit(solution)/shard_map/ppermute | solution.py:178
  156.3 14.9 %collective-permute-start.4 = (bf16[128,1280]{1,0:T(8,128)(2,1)}, bf16[128,1280]{1,0:T(8,128)(2,1)}, u32[]{:S(2)}, u32[]{:S(2)}) collective-permute-start(bf16[128,1280]{1,0:T(8,128)(2,1)} %get-tuple-element.19), channel_id=1, source_target_pairs={{0,2},{1,3},{2,0},{3,1},{4,6},{5,7},{6,4},{7,5},{8,10},{9,11},{10,... | collective-permute-start | bytes 983048 | tf_op jit(solution)/shard_map/ppermute | solution.py:178
  163.9 1.0 copy-start.3
  178.0 42.4 %all-to-all-start.2 = ((bf16[64,8,1280]{2,1,0:T(8,128)(2,1)}), bf16[64,8,1280]{2,1,0:T(8,128)(2,1)}, u32[]{:S(2)}, u32[]{:S(2)}) async-start(bf16[64,8,1280]{2,1,0:T(8,128)(2,1)} %bitcast_select_fusion), calls=%async_computation.2 | async-start | bytes 2621440 | tf_op jit(solution)/shard_map/all_to_all | solution.py:234

commit v7 on v6

--- a/solution.py
+++ b/solution.py
@@ -180,6 +180,14 @@
     return total
 
 
+def take_rows(table, index, valid):
+    columns = jnp.arange(table.shape[0], dtype=jnp.int32)
+    chosen = (index[:, None] == columns[None, :]) & valid[:, None]
+    return jnp.dot(
+        chosen.astype(table.dtype), table, preferred_element_type=jnp.float32
+    ).astype(table.dtype)
+
+
 def on_device(
     hidden_in,
     queries,
@@ -219,9 +227,12 @@
     dest = jnp.arange(request_owners, dtype=jnp.int32)[:, None]
     blocks = jnp.arange(block_rows, dtype=jnp.int32)[None, :]
     send_row = blocks * request_owners + (dest - own_shift) % request_owners
-    outbound = jnp.where((send_row < own_count)[:, :, None], rows[send_row], jnp.zeros((), rows.dtype))
-    arrived = lax.all_to_all(outbound, "req", 0, 0, tiled=True)
-    mixed = arrived.reshape(slot_capacity, -1)[pick]
+    send_row = send_row.reshape(slot_capacity)
+    outbound = take_rows(rows, send_row, send_row < own_count)
+    arrived = lax.all_to_all(
+        outbound.reshape(request_owners, block_rows, -1), "req", 0, 0, tiled=True
+    )
+    mixed = take_rows(arrived.reshape(slot_capacity, -1), pick, pick >= 0)
     normed = normalize(mixed, norm_gain)
     result = (
         mixed.astype(jnp.float32) + feed_forward(normed, gate_weight, up_weight, down_weight)
@@ -230,10 +241,12 @@
     source_row = jnp.arange(block_rows, dtype=jnp.int32)[:, None] * request_owners + lanes[None, :]
     valid = source_row < counts[None, :]
     target = jnp.where(valid, (firsts[None, :] + source_row) // request_owners, 0)
-    outgoing = jnp.where(valid.T[:, :, None], result[target.T], jnp.zeros((), jnp.bfloat16))
-    returned = lax.all_to_all(outgoing, "req", 0, 0, tiled=True).reshape(slot_capacity, -1)
+    outgoing = take_rows(result, target.T.reshape(slot_capacity), valid.T.reshape(slot_capacity))
+    returned = lax.all_to_all(
+        outgoing.reshape(request_owners, block_rows, -1), "req", 0, 0, tiled=True
+    ).reshape(slot_capacity, -1)
     back_row = ((slots % request_owners + own_shift) % request_owners) * block_rows + slots // request_owners
-    return returned[back_row]
+    return take_rows(returned, back_row, back_row >= 0)
 
 
 def solution(mesh):

time: 227 us -> 215 us (0.947)
  local copies, waits for them, and re-layouts: 29.6 us -> 13.2 us
  matrix products: 15.1 us -> 25.6 us
  other arithmetic: 11 us -> 4.39 us
    gather x4 -> x0, local copies, waits for them, and re-layouts: 16.3 us -> none  [the longest x1 5.42 us: on_device(): rows[send_row]]
    dot_general x0 -> x4, matrix products: none -> 11.4 us  [take_rows(): jnp.dot(chosen.astype(table.dtype), table, preferred_element_type=jnp.flo...]
    select_n x5 -> x1, other arithmetic: 5.24 us -> 0.01 us  [on_device(): jnp.where(valid, (firsts[None, :] + source_row) // request_owners, 0)]
  transfers between devices with their start and end apart: 9 -> 9, of which waited for: 7 -> 7; matrix products, arithmetic and copies ran while one was open for 7% -> 7% of each run, Pallas kernels for 16% -> 17%
where the time goes in v7:
time: 215 us; the launch traced here: 214 us
  waiting for transfers between devices  94.5 us (44%)
  starting transfers between devices  37.6 us (17%)
  Pallas kernels  35.7 us (17%)
  matrix products  25.6 us (12%)
  local copies, waits for them, and re-layouts  13.2 us (6%)
  other arithmetic  4.39 us (2%)
  between operations  3.11 us (1%)
    pallas_call x1, Pallas kernels, attend(): pl.pallas_call(attention_kernel, grid=(tiles,), in_specs=[pl.BlockSpec((s...  35.7 us
    all_to_all x1, waiting for transfers between devices, on_device(): lax.all_to_all(outgoing.reshape(request_owners, block_rows, -1), 'req', 0...  34 us
    all_to_all x1, waiting for transfers between devices, on_device(): lax.all_to_all(outbound.reshape(request_owners, block_rows, -1), 'req', 0...  33.8 us
    ppermute x3, waiting for transfers between devices, feed_forward(): lax.ppermute(part, 'grp', [(j, (j - k) % groups) for j in range(groups)])  14.1 us
    all_to_all x1, starting transfers between devices, on_device(): lax.all_to_all(jnp.broadcast_to(live_rows.reshape(1, 1), (request_owners,...  13.1 us
    ppermute x3, waiting for transfers between devices, feed_forward(): lax.ppermute(normed, 'grp', [(j, (j + k) % groups) for j in range(groups)])  12.4 us
    dot_general x4, matrix products, take_rows(): jnp.dot(chosen.astype(table.dtype), table, preferred_element_type=jnp.flo...  11.4 us
    all_to_all x1, starting transfers between devices, on_device(): lax.all_to_all(outbound.reshape(request_owners, block_rows, -1), 'req', 0...  10.5 us
  transfers between devices with their start and end apart: 9, of which 7 were waited for; matrix products, arithmetic and copies ran while one was open for 7% of the time, Pallas kernels for 17%

profile of v7, /device:TPU:1, one launch (start us, length us, event | category | flops | bytes accessed | tf_op | source)
XLA Modules:
  0.0 214.1 jit_solution(12914552461074116681)
XLA Ops:
  0.8 0.6 broadcast_in_dim.52
  1.4 13.1 %all-to-all-start = ((s32[64,1,128]{2,1,0:T(1,128)}), s32[64,1,128]{2,1,0:T(1,128)S(1)}, u32[]{:S(2)}, u32[]{:S(2)}) async-start(s32[64,1,128]{2,1,0:T(1,128)} %broadcast_in_dim.52), calls=%async_computation | async-start | bytes 65536 | tf_op jit(solution)/shard_map/all_to_all | solution.py:213
  14.6 0.8 compare_reduce_fusion
  15.6 0.3 reduce-window.19
  16.0 0.1 slice_reduce_fusion
  16.2 0.6 iota_subtract_fusion.posr_ref
  16.8 0.3 multiply_sine_fusion
  17.1 0.8 copy.34.sin_ref
  18.0 0.9 copy.33.cos_ref
  18.8 0.9 copy.35.segc_ref
  19.7 1.1 copy.31.k_ref
  20.8 1.0 broadcast_in_dim.60
  21.8 1.1 copy.32.v_ref
  22.9 0.6 select_convert_fusion.turn_ref
  23.6 35.7 %shard_map.109 = bf16[512,1280]{1,0:T(8,128)(2,1)} custom-call(bf16[512,1280]{1,0:T(8,128)(2,1)} %q_ref.1, bf16[512,640]{1,0:T(8,128)(2,1)} %copy.31.k_ref, bf16[512,640]{1,0:T(8,128)(2,1)} %copy.32.v_ref, f32[512,128]{1,0:T(8,128)} %copy.33.cos_ref, f32[512,128]{1,0:T(8,128)} %copy.34.sin_ref, bf16[128,128]{1,0:T(8,128)(2,1)} %select_convert_fusion.turn_ref, ...), custom_call_target="tpu_custom_call" | custom-call | tf_op jit(solution)/shard_map/pallas_call | solution.py:115
  59.3 0.1 slice_reduce_fusion.1
  59.4 0.1 reduce-window.18
  59.5 0.1 reduce
  59.6 0.7 fusion.43
  62.6 3.3 %fusion = bf16[64,8,1280]{2,1,0:T(8,128)(2,1)} fusion(bf16[512,1280]{1,0:T(8,128)(2,1)} %shard_map.109, s32[512]{0:T(512)S(1)} %add.259, pred[512]{0:T(512)(128)(4,1)S(1)} %broadcast_compare_fusion), kind=kOutput, calls=%fused_computation.4 | convolution fusion | flops 672268288 | bytes 2624000 | tf_op jit(solution)/shard_map/dot_general | solution.py:186
  66.0 10.5 %all-to-all-start.1 = ((bf16[64,8,1280]{2,1,0:T(8,128)(2,1)}), bf16[64,8,1280]{2,1,0:T(8,128)(2,1)}, u32[]{:S(2)}, u32[]{:S(2)}) async-start(bf16[64,8,1280]{2,1,0:T(8,128)(2,1)} %fusion), calls=%async_computation.1 | async-start | bytes 2621440 | tf_op jit(solution)/shard_map/all_to_all | solution.py:232
  76.7 33.8 %all-to-all-done.1 = bf16[64,8,1280]{2,1,0:T(8,128)(2,1)} async-done(((bf16[64,8,1280]{2,1,0:T(8,128)(2,1)}), bf16[64,8,1280]{2,1,0:T(8,128)(2,1)}, u32[]{:S(2)}, u32[]{:S(2)}) %all-to-all-start.1) | async-done | bytes 1310752 | tf_op jit(solution)/shard_map/all_to_all | solution.py:232
  110.6 1.9 multiply_reduce_fusion
  112.5 0.1 multiply_convert_fusion
  112.6 2.5 %collective-permute-start.2 = (bf16[128,1280]{1,0:T(8,128)(2,1)S(1)}, bf16[128,1280]{1,0:T(8,128)(2,1)}, u32[]{:S(2)}, u32[]{:S(2)}) collective-permute-start(bf16[128,1280]{1,0:T(8,128)(2,1)S(1)} %multiply_convert_fusion), channel_id=1, source_target_pairs={{0,3},{1,0},{2,1},{3,2},{4,7},{5,4},{6,5},{7,6},{8,11},{9,8},{10,9... | collective-permute-start | bytes 983048 | tf_op jit(solution)/shard_map/ppermute | solution.py:169
  115.2 0.5 collective-permute-start.1
  115.7 0.6 collective-permute-start
  116.3 1.3 fusion.51
  117.6 3.4 %convolution_convert_fusion.4 = bf16[128,1280]{1,0:T(8,128)(2,1)} fusion(bf16[896,1280]{1,0:T(8,128)(2,1)S(1)} %copy-done, bf16[128,1280]{1,0:T(8,128)(2,1)S(1)} %multiply_convert_fusion, bf16[1280,896]{1,0:T(8,128)(2,1)} %param.20, f32[128,896]{1,0:T(8,128)} %fusion.51), kind=kOutput, calls=%fused_computation.6 | convolution fusion | flops 588054528 | bytes 5701632 | tf_op jit(solution)/shard_map/dot_general | solution.py:162
  121.0 8.3 %collective-permute-done.2 = bf16[128,1280]{1,0:T(8,128)(2,1)} collective-permute-done((bf16[128,1280]{1,0:T(8,128)(2,1)S(1)}, bf16[128,1280]{1,0:T(8,128)(2,1)}, u32[]{:S(2)}, u32[]{:S(2)}) %collective-permute-start.2) | collective-permute-done | bytes 327712 | tf_op jit(solution)/shard_map/ppermute | solution.py:169
  129.3 4.1 %collective-permute-done = bf16[128,1280]{1,0:T(8,128)(2,1)} collective-permute-done((bf16[128,1280]{1,0:T(8,128)(2,1)S(1)}, bf16[128,1280]{1,0:T(8,128)(2,1)}, u32[]{:S(2)}, u32[]{:S(2)}) %collective-permute-start) | collective-permute-done | bytes 327712 | tf_op jit(solution)/shard_map/ppermute | solution.py:169
  133.5 1.0 constant_dynamic-update-slice_fusion.2
  134.5 1.0 constant_dynamic-update-slice_fusion.1
  135.5 1.0 constant_dynamic-update-slice_fusion
  136.5 0.9 copy-done.4
  137.4 3.9 %fusion.52 = f32[384,896]{1,0:T(8,128)} fusion(bf16[384,1280]{1,0:T(8,128)(2,1)S(1)} %constant_dynamic-update-slice_fusion, bf16[1280,896]{1,0:T(8,128)(2,1)} %param.19), kind=kOutput, calls=%fused_computation.120 | convolution fusion | flops 880803840 | bytes 4653056 | tf_op jit(solution)/shard_map/dot_general | solution.py:159
  141.3 5.6 %convolution_convert_fusion.3 = bf16[384,1280]{1,0:T(8,128)(2,1)} fusion(bf16[896,1280]{1,0:T(8,128)(2,1)S(1)} %copy-done, bf16[384,1280]{1,0:T(8,128)(2,1)} %copy-done.4, bf16[1280,896]{1,0:T(8,128)(2,1)} %param.20, f32[384,896]{1,0:T(8,128)} %fusion.52), kind=kOutput, calls=%fused_computation.3 | convolution fusion | flops 1764163584 | bytes 7929856 | tf_op jit(solution)/shard_map/dot_general | solution.py:162
  146.9 2.2 %fusion.50 = (bf16[128,1280]{1,0:T(8,128)(2,1)}, bf16[128,1280]{1,0:T(8,128)(2,1)}, bf16[128,1280]{1,0:T(8,128)(2,1)}) fusion(bf16[384,1280]{1,0:T(8,128)(2,1)} %convolution_convert_fusion.3), kind=kLoop, calls=%fused_computation.118 | loop fusion | bytes 1966080 | tf_op jit(solution)/shard_map/slice | solution.py:177
  149.1 1.5 collective-permute-start.5
  150.6 0.5 collective-permute-start.4
  151.2 0.1 lt.81
  151.4 6.8 %collective-permute-done.3 = bf16[128,1280]{1,0:T(8,128)(2,1)} collective-permute-done((bf16[128,1280]{1,0:T(8,128)(2,1)}, bf16[128,1280]{1,0:T(8,128)(2,1)}, u32[]{:S(2)}, u32[]{:S(2)}) %collective-permute-start.3) | collective-permute-done | bytes 327712 | tf_op jit(solution)/shard_map/ppermute | solution.py:178
  158.2 1.0 collective-permute-done.5
  159.2 6.4 %collective-permute-done.4 = bf16[128,1280]{1,0:T(8,128)(2,1)} collective-permute-done((bf16[128,1280]{1,0:T(8,128)(2,1)}, bf16[128,1280]{1,0:T(8,128)(2,1)}, u32[]{:S(2)}, u32[]{:S(2)}) %collective-permute-start.4) | collective-permute-done | bytes 327712 | tf_op jit(solution)/shard_map/ppermute | solution.py:178
  165.6 2.8 %fusion.1 = bf16[64,8,1280]{2,1,0:T(8,128)(2,1)} fusion(f32[128,1280]{1,0:T(8,128)S(1)} %get-tuple-element.29, bf16[128,1280]{1,0:T(8,128)(2,1)} %collective-permute-done.5, bf16[128,1280]{1,0:T(8,128)(2,1)} %collective-permute-done.4, bf16[128,1280]{1,0:T(8,128)(2,1)} %collective-permute-done.3, bf16[128,1280]{1,0:T(8,128)(2,1)S(1)} %copy-done.2, ...), kind=kOutput, calls=%fused_computation.5 | convolution fusion | flops 170033152 | bytes 3279360 | tf_op jit(solution)/shard_map/dot_general | solution.py:186
  168.4 8.3 %all-to-all-start.2 = ((bf16[64,8,1280]{2,1,0:T(8,128)(2,1)}), bf16[64,8,1280]{2,1,0:T(8,128)(2,1)}, u32[]{:S(2)}, u32[]{:S(2)}) async-start(bf16[64,8,1280]{2,1,0:T(8,128)(2,1)} %fusion.1), calls=%async_computation.2 | async-start | bytes 2621440 | tf_op jit(solution)/shard_map/all_to_all | solution.py:245
  176.7 34.0 %all-to-all-done.2 = bf16[64,8,1280]{2,1,0:T(8,128)(2,1)} async-done(((bf16[64,8,1280]{2,1,0:T(8,128)(2,1)}), bf16[64,8,1280]{2,1,0:T(8,128)(2,1)}, u32[]{:S(2)}, u32[]{:S(2)}) %all-to-all-start.2) | async-done | bytes 1310752 | tf_op jit(solution)/shard_map/all_to_all | solution.py:245
  210.8 3.3 %convolution_convert_fusion = bf16[512,1280]{1,0:T(8,128)(2,1)} fusion(bf16[64,8,1280]{2,1,0:T(8,128)(2,1)} %all-to-all-done.2, s32[512]{0:T(512)S(1)} %fusion.33, pred[512]{0:T(512)(128)(4,1)S(1)} %broadcast_compare_fusion.1), kind=kOutput, calls=%fused_computation | convolution fusion | flops 672268288 | bytes 2624000 | tf_op jit(solution)/shard_map/dot_general | solution.py:186
  (42 shorter events, 1.1 us)
Async XLA Ops:
  0.0 117.6 %copy-start = (bf16[896,1280]{1,0:T(8,128)(2,1)S(1)}, bf16[896,1280]{1,0:T(8,128)(2,1)}, u32[]{:S(2)}) copy-start(bf16[896,1280]{1,0:T(8,128)(2,1)} %param.21) | copy-start | bytes 6881284
  0.0 18.8 %copy-start.5 = (s32[1,1,512]{2,1,0:T(1,128)S(1)}, s32[1,1,512]{2,1,0:T(1,128)}, u32[]{:S(2)}) copy-start(s32[1,1,512]{2,1,0:T(1,128)} %param.15) | copy-start | bytes 6148
  0.0 19.7 %copy-start.3 = (bf16[512,320]{0,1:T(8,128)(2,1)S(1)}, bf16[512,320]{0,1:T(8,128)(2,1)}, u32[]{:S(2)}) copy-start(bf16[512,320]{0,1:T(8,128)(2,1)} %param.13) | copy-start | bytes 983044
  1.4 57.9 %all-to-all-start = ((s32[64,1,128]{2,1,0:T(1,128)}), s32[64,1,128]{2,1,0:T(1,128)S(1)}, u32[]{:S(2)}, u32[]{:S(2)}) async-start(s32[64,1,128]{2,1,0:T(1,128)} %broadcast_in_dim.52), calls=%async_computation | async-start | bytes 65536 | tf_op jit(solution)/shard_map/all_to_all | solution.py:213
  66.0 44.6 %all-to-all-start.1 = ((bf16[64,8,1280]{2,1,0:T(8,128)(2,1)}), bf16[64,8,1280]{2,1,0:T(8,128)(2,1)}, u32[]{:S(2)}, u32[]{:S(2)}) async-start(bf16[64,8,1280]{2,1,0:T(8,128)(2,1)} %fusion), calls=%async_computation.1 | async-start | bytes 2621440 | tf_op jit(solution)/shard_map/all_to_all | solution.py:232
  76.5 36.0 %copy-start.6 = (f32[1280]{0:T(1024)S(1)}, f32[1280]{0:T(1024)}, u32[]{:S(2)}) copy-start(f32[1280]{0:T(1024)} %param.18) | copy-start | bytes 15364
  110.6 5.8 %copy-start.1 = (bf16[1280,896]{1,0:T(8,128)(2,1)S(1)}, bf16[1280,896]{1,0:T(8,128)(2,1)}, u32[]{:S(2)}) copy-start(bf16[1280,896]{1,0:T(8,128)(2,1)} %param.19) | copy-start | bytes 6881284
  112.6 16.7 %collective-permute-start.2 = (bf16[128,1280]{1,0:T(8,128)(2,1)S(1)}, bf16[128,1280]{1,0:T(8,128)(2,1)}, u32[]{:S(2)}, u32[]{:S(2)}) collective-permute-start(bf16[128,1280]{1,0:T(8,128)(2,1)S(1)} %multiply_convert_fusion), channel_id=1, source_target_pairs={{0,3},{1,0},{2,1},{3,2},{4,7},{5,4},{6,5},{7,6},{8,11},{9,8},{10,9... | collective-permute-start | bytes 983048 | tf_op jit(solution)/shard_map/ppermute | solution.py:169
  115.2 14.1 %collective-permute-start.1 = (bf16[128,1280]{1,0:T(8,128)(2,1)S(1)}, bf16[128,1280]{1,0:T(8,128)(2,1)}, u32[]{:S(2)}, u32[]{:S(2)}) collective-permute-start(bf16[128,1280]{1,0:T(8,128)(2,1)S(1)} %multiply_convert_fusion), channel_id=1, source_target_pairs={{0,2},{1,3},{2,0},{3,1},{4,6},{5,7},{6,4},{7,5},{8,10},{9,11},{10,... | collective-permute-start | bytes 983048 | tf_op jit(solution)/shard_map/ppermute | solution.py:169
  115.7 17.8 %collective-permute-start = (bf16[128,1280]{1,0:T(8,128)(2,1)S(1)}, bf16[128,1280]{1,0:T(8,128)(2,1)}, u32[]{:S(2)}, u32[]{:S(2)}) collective-permute-start(bf16[128,1280]{1,0:T(8,128)(2,1)S(1)} %multiply_convert_fusion), channel_id=1, source_target_pairs={{0,1},{1,2},{2,3},{3,0},{4,5},{5,6},{6,7},{7,4},{8,9},{9,10},{10,1... | collective-permute-start | bytes 983048 | tf_op jit(solution)/shard_map/ppermute | solution.py:169
  136.5 0.9 copy-start.4
  146.9 18.6 %copy-start.2 = (bf16[128,1280]{1,0:T(8,128)(2,1)S(1)}, bf16[128,1280]{1,0:T(8,128)(2,1)}, u32[]{:S(2)}) copy-start(bf16[128,1280]{1,0:T(8,128)(2,1)} %convolution_convert_fusion.4) | copy-start | bytes 983044
  149.1 9.1 %collective-permute-start.3 = (bf16[128,1280]{1,0:T(8,128)(2,1)}, bf16[128,1280]{1,0:T(8,128)(2,1)}, u32[]{:S(2)}, u32[]{:S(2)}) collective-permute-start(bf16[128,1280]{1,0:T(8,128)(2,1)} %get-tuple-element.19), channel_id=1, source_target_pairs={{0,3},{1,0},{2,1},{3,2},{4,7},{5,4},{6,5},{7,6},{8,11},{9,8},{10,9... | collective-permute-start | bytes 983048 | tf_op jit(solution)/shard_map/ppermute | solution.py:178
  149.1 10.1 %collective-permute-start.5 = (bf16[128,1280]{1,0:T(8,128)(2,1)}, bf16[128,1280]{1,0:T(8,128)(2,1)}, u32[]{:S(2)}, u32[]{:S(2)}) collective-permute-start(bf16[128,1280]{1,0:T(8,128)(2,1)} %get-tuple-element.20), channel_id=1, source_target_pairs={{0,1},{1,2},{2,3},{3,0},{4,5},{5,6},{6,7},{7,4},{8,9},{9,10},{10,1... | collective-permute-start | bytes 983048 | tf_op jit(solution)/shard_map/ppermute | solution.py:178
  150.6 15.0 %collective-permute-start.4 = (bf16[128,1280]{1,0:T(8,128)(2,1)}, bf16[128,1280]{1,0:T(8,128)(2,1)}, u32[]{:S(2)}, u32[]{:S(2)}) collective-permute-start(bf16[128,1280]{1,0:T(8,128)(2,1)} %get-tuple-element.21), channel_id=1, source_target_pairs={{0,2},{1,3},{2,0},{3,1},{4,6},{5,7},{6,4},{7,5},{8,10},{9,11},{10,... | collective-permute-start | bytes 983048 | tf_op jit(solution)/shard_map/ppermute | solution.py:178
  168.4 42.4 %all-to-all-start.2 = ((bf16[64,8,1280]{2,1,0:T(8,128)(2,1)}), bf16[64,8,1280]{2,1,0:T(8,128)(2,1)}, u32[]{:S(2)}, u32[]{:S(2)}) async-start(bf16[64,8,1280]{2,1,0:T(8,128)(2,1)} %fusion.1), calls=%async_computation.2 | async-start | bytes 2621440 | tf_op jit(solution)/shard_map/all_to_all | solution.py:245

commit v8 on v7

--- a/solution.py
+++ b/solution.py
@@ -162,7 +162,7 @@
     return jnp.dot(hidden, down_weight, preferred_element_type=jnp.float32).astype(jnp.bfloat16)
 
 
-def feed_forward(normed, gate_weight, up_weight, down_weight):
+def feed_forward_direct(normed, gate_weight, up_weight, down_weight):
     groups = lax.axis_size("grp")
     rows = normed.shape[0]
     arrived = [
@@ -178,6 +178,32 @@
         part = lax.ppermute(part, "grp", [(j, (j - k) % groups) for j in range(groups)])
         total = total + part.astype(jnp.float32)
     return total
+
+
+def feed_forward(normed, gate_weight, up_weight, down_weight):
+    groups = lax.axis_size("grp")
+    if groups != 4:
+        return feed_forward_direct(normed, gate_weight, up_weight, down_weight)
+    rows = normed.shape[0]
+    half = rows // 2
+    plus = [(j, (j + 1) % groups) for j in range(groups)]
+    minus = [(j, (j - 1) % groups) for j in range(groups)]
+    from_left = lax.ppermute(normed, "grp", plus)
+    from_right = lax.ppermute(normed, "grp", minus)
+    own = ffn_rows(normed, gate_weight, up_weight, down_weight)
+    own, from_left, from_right = lax.optimization_barrier((own, from_left, from_right))
+    far_first = lax.ppermute(from_left[:half], "grp", plus)
+    far_second = lax.ppermute(from_right[half:], "grp", minus)
+    near = ffn_rows(jnp.concatenate([from_left, from_right], axis=0), gate_weight, up_weight, down_weight)
+    back_from_right = lax.ppermute(near[:rows], "grp", minus)
+    back_from_left = lax.ppermute(near[rows:], "grp", plus)
+    near, far_first, far_second = lax.optimization_barrier((near, far_first, far_second))
+    far = ffn_rows(jnp.concatenate([far_first, far_second], axis=0), gate_weight, up_weight, down_weight)
+    hop_first = lax.ppermute(lax.ppermute(far[:half], "grp", plus), "grp", plus)
+    hop_second = lax.ppermute(lax.ppermute(far[half:], "grp", minus), "grp", minus)
+    total = own.astype(jnp.float32) + back_from_right.astype(jnp.float32)
+    total = total + back_from_left.astype(jnp.float32)
+    return total + jnp.concatenate([hop_first, hop_second], axis=0).astype(jnp.float32)
 
 
 def take_rows(table, index, valid):

time: 215 us -> 215 us (level)
  waiting for transfers between devices: 94.5 us -> 78.9 us
  starting transfers between devices: 37.6 us -> 45.1 us
  matrix products: 25.6 us -> 30.4 us
  local copies, waits for them, and re-layouts: 13.2 us -> 16.3 us
    ppermute x6 -> x10, waiting for transfers between devices: 26.6 us -> 11 us  [the longest x2 5.24 us: feed_forward(): hop_first = lax.ppermute(lax.ppermute(far[:half], 'grp', plus), 'grp', plus)]
    ppermute x6 -> x10, starting transfers between devices: 5.66 us -> 11.2 us  [the longest x1 2.76 us: feed_forward(): lax.ppermute(lax.ppermute(far[half:], 'grp', minus), 'grp', minus)]
    slice x2 -> x5, local copies, waits for them, and re-layouts: 2.25 us -> 4.91 us  [the longest x1 1.97 us: feed_forward(): back_from_right = lax.ppermute(near[:rows], 'grp', minus)]
    dot_general x2 -> x3, matrix products: 5.19 us -> 7.63 us  [ffn_rows(): gate = jnp.dot(rows, gate_weight, preferred_element_type=jnp.float32)]
    dot_general x2 -> x3, matrix products: 9.04 us -> 11.4 us  [ffn_rows(): jnp.dot(hidden, down_weight, preferred_element_type=jnp.float32)]
  transfers between devices with their start and end apart: 9 -> 13, of which waited for: 7 -> 6; matrix products, arithmetic and copies ran while one was open for 7% -> 16% of each run, Pallas kernels for 17% -> 17%
where the time goes in v8:
time: 215 us; the launch traced here: 214 us
  waiting for transfers between devices  78.9 us (37%)
  starting transfers between devices  45.1 us (21%)
  Pallas kernels  35.7 us (17%)
  matrix products  30.4 us (14%)
  local copies, waits for them, and re-layouts  16.3 us (8%)
  other arithmetic  4.39 us (2%)
  between operations  3.15 us (1%)
    pallas_call x1, Pallas kernels, attend(): pl.pallas_call(attention_kernel, grid=(tiles,), in_specs=[pl.BlockSpec((s...  35.7 us
    all_to_all x1, waiting for transfers between devices, on_device(): lax.all_to_all(outgoing.reshape(request_owners, block_rows, -1), 'req', 0...  34 us
    all_to_all x1, waiting for transfers between devices, on_device(): lax.all_to_all(outbound.reshape(request_owners, block_rows, -1), 'req', 0...  33.9 us
    all_to_all x1, starting transfers between devices, on_device(): lax.all_to_all(jnp.broadcast_to(live_rows.reshape(1, 1), (request_owners,...  13.1 us
    dot_general x3, matrix products, ffn_rows(): jnp.dot(hidden, down_weight, preferred_element_type=jnp.float32)  11.4 us
    dot_general x4, matrix products, take_rows(): jnp.dot(chosen.astype(table.dtype), table, preferred_element_type=jnp.flo...  11.4 us
    all_to_all x1, starting transfers between devices, on_device(): lax.all_to_all(outbound.reshape(request_owners, block_rows, -1), 'req', 0...  10.6 us
    all_to_all x1, starting transfers between devices, on_device(): lax.all_to_all(outgoing.reshape(request_owners, block_rows, -1), 'req', 0...  10.1 us
  transfers between devices with their start and end apart: 13, of which 6 were waited for; matrix products, arithmetic and copies ran while one was open for 16% of the time, Pallas kernels for 17%

profile of v8, /device:TPU:1, one launch (start us, length us, event | category | flops | bytes accessed | tf_op | source)
XLA Modules:
  0.0 214.0 jit_solution(3176563110687657418)
XLA Ops:
  0.8 0.6 broadcast_in_dim.52
  1.4 13.1 %all-to-all-start = ((s32[64,1,128]{2,1,0:T(1,128)}), s32[64,1,128]{2,1,0:T(1,128)S(1)}, u32[]{:S(2)}, u32[]{:S(2)}) async-start(s32[64,1,128]{2,1,0:T(1,128)} %broadcast_in_dim.52), calls=%async_computation | async-start | bytes 65536 | tf_op jit(solution)/shard_map/all_to_all | solution.py:239
  14.6 0.8 compare_reduce_fusion
  15.6 0.3 reduce-window.19
  16.2 0.6 iota_subtract_fusion.posr_ref
  16.8 0.3 multiply_sine_fusion
  17.1 0.8 copy.34.sin_ref
  18.0 0.9 copy.33.cos_ref
  18.8 1.5 copy.35.segc_ref
  20.4 1.1 copy.31.k_ref
  21.5 1.0 broadcast_in_dim.60
  22.5 1.1 copy.32.v_ref
  23.6 0.6 select_convert_fusion.turn_ref
  24.2 35.7 %shard_map.109 = bf16[512,1280]{1,0:T(8,128)(2,1)} custom-call(bf16[512,1280]{1,0:T(8,128)(2,1)} %q_ref.1, bf16[512,640]{1,0:T(8,128)(2,1)} %copy.31.k_ref, bf16[512,640]{1,0:T(8,128)(2,1)} %copy.32.v_ref, f32[512,128]{1,0:T(8,128)} %copy.33.cos_ref, f32[512,128]{1,0:T(8,128)} %copy.34.sin_ref, bf16[128,128]{1,0:T(8,128)(2,1)} %select_convert_fusion.turn_ref, ...), custom_call_target="tpu_custom_call" | custom-call | tf_op jit(solution)/shard_map/pallas_call | solution.py:115
  60.3 0.7 fusion.53
  63.3 3.3 %fusion = bf16[64,8,1280]{2,1,0:T(8,128)(2,1)} fusion(bf16[512,1280]{1,0:T(8,128)(2,1)} %shard_map.109, s32[512]{0:T(512)S(1)} %add.262, pred[512]{0:T(512)(128)(4,1)S(1)} %broadcast_compare_fusion), kind=kOutput, calls=%fused_computation.3 | convolution fusion | flops 672268288 | bytes 2624000 | tf_op jit(solution)/shard_map/dot_general | solution.py:212
  66.7 10.6 %all-to-all-start.1 = ((bf16[64,8,1280]{2,1,0:T(8,128)(2,1)}), bf16[64,8,1280]{2,1,0:T(8,128)(2,1)}, u32[]{:S(2)}, u32[]{:S(2)}) async-start(bf16[64,8,1280]{2,1,0:T(8,128)(2,1)} %fusion), calls=%async_computation.1 | async-start | bytes 2621440 | tf_op jit(solution)/shard_map/all_to_all | solution.py:258
  77.5 33.9 %all-to-all-done.1 = bf16[64,8,1280]{2,1,0:T(8,128)(2,1)} async-done(((bf16[64,8,1280]{2,1,0:T(8,128)(2,1)}), bf16[64,8,1280]{2,1,0:T(8,128)(2,1)}, u32[]{:S(2)}, u32[]{:S(2)}) %all-to-all-start.1) | async-done | bytes 1310752 | tf_op jit(solution)/shard_map/all_to_all | solution.py:258
  111.4 1.9 multiply_reduce_fusion
  113.3 0.1 multiply_convert_fusion
  113.5 2.5 %collective-permute-start.1 = (bf16[128,1280]{1,0:T(8,128)(2,1)S(1)}, bf16[128,1280]{1,0:T(8,128)(2,1)}, u32[]{:S(2)}, u32[]{:S(2)}) collective-permute-start(bf16[128,1280]{1,0:T(8,128)(2,1)S(1)} %multiply_convert_fusion), channel_id=1, source_target_pairs={{0,3},{1,0},{2,1},{3,2},{4,7},{5,4},{6,5},{7,6},{8,11},{9,8},{10,9... | collective-permute-start | bytes 983048 | tf_op jit(solution)/shard_map/ppermute | solution.py:192
  116.0 1.3 fusion.64
  117.3 3.4 %convolution_convert_fusion.5 = bf16[128,1280]{1,0:T(8,128)(2,1)} fusion(bf16[896,1280]{1,0:T(8,128)(2,1)S(1)} %copy-done, bf16[128,1280]{1,0:T(8,128)(2,1)S(1)} %multiply_convert_fusion, bf16[1280,896]{1,0:T(8,128)(2,1)} %param.20, f32[128,896]{1,0:T(8,128)} %fusion.64), kind=kOutput, calls=%fused_computation.7 | convolution fusion | flops 588054528 | bytes 5701632 | tf_op jit(solution)/shard_map/dot_general | solution.py:162
  120.7 2.5 %collective-permute-done.1 = bf16[128,1280]{1,0:T(8,128)(2,1)} collective-permute-done((bf16[128,1280]{1,0:T(8,128)(2,1)S(1)}, bf16[128,1280]{1,0:T(8,128)(2,1)}, u32[]{:S(2)}, u32[]{:S(2)}) %collective-permute-start.1) | collective-permute-done | bytes 327712 | tf_op jit(solution)/shard_map/ppermute | solution.py:192
  123.3 3.2 %collective-permute-done = bf16[128,1280]{1,0:T(8,128)(2,1)} collective-permute-done((bf16[128,1280]{1,0:T(8,128)(2,1)S(1)}, bf16[128,1280]{1,0:T(8,128)(2,1)}, u32[]{:S(2)}, u32[]{:S(2)}) %collective-permute-start) | collective-permute-done | bytes 327712 | tf_op jit(solution)/shard_map/ppermute | solution.py:191
  126.5 0.9 slice.43
  127.4 1.0 constant_dynamic-update-slice_fusion.1
  128.4 0.9 slice.44
  129.4 0.4 collective-permute-start.5
  129.7 1.2 collective-permute-start.4
  130.9 1.0 constant_dynamic-update-slice_fusion
  131.9 0.8 copy-done.3
  132.8 3.4 %fusion.65 = f32[256,896]{1,0:T(8,128)} fusion(bf16[256,1280]{1,0:T(8,128)(2,1)S(1)} %constant_dynamic-update-slice_fusion, bf16[1280,896]{1,0:T(8,128)(2,1)} %param.19), kind=kOutput, calls=%fused_computation.136 | convolution fusion | flops 587202560 | bytes 3866624 | tf_op jit(solution)/shard_map/dot_general | solution.py:159
  136.2 4.6 %convolution_convert_fusion.3 = bf16[256,1280]{1,0:T(8,128)(2,1)} fusion(bf16[896,1280]{1,0:T(8,128)(2,1)S(1)} %copy-done, bf16[256,1280]{1,0:T(8,128)(2,1)} %copy-done.3, bf16[1280,896]{1,0:T(8,128)(2,1)} %param.20, f32[256,896]{1,0:T(8,128)} %fusion.65), kind=kOutput, calls=%fused_computation.5 | convolution fusion | flops 1176109056 | bytes 6815744 | tf_op jit(solution)/shard_map/dot_general | solution.py:162
  140.7 2.0 fusion.62
  142.7 1.5 collective-permute-start.2
  144.2 0.9 constant_dynamic-update-slice_fusion.3
  145.2 2.9 %fusion.66 = f32[128,896]{1,0:T(8,128)} fusion(bf16[128,1280]{1,0:T(8,128)(2,1)S(1)} %constant_dynamic-update-slice_fusion.2, bf16[1280,896]{1,0:T(8,128)(2,1)} %param.19), kind=kOutput, calls=%fused_computation.137 | convolution fusion | flops 293601280 | bytes 3080192 | tf_op jit(solution)/shard_map/dot_general | solution.py:159
  148.1 3.4 %convolution_convert_fusion.4 = bf16[128,1280]{1,0:T(8,128)(2,1)} fusion(bf16[896,1280]{1,0:T(8,128)(2,1)S(1)} %copy-done, bf16[128,1280]{1,0:T(8,128)(2,1)S(1)} %constant_dynamic-update-slice_fusion.2, bf16[1280,896]{1,0:T(8,128)(2,1)} %param.20, f32[128,896]{1,0:T(8,128)} %fusion.66), kind=kOutput, calls=%fused_computation.6 | convolution fusion | flops 588054528 | bytes 5701632 | tf_op jit(solution)/shard_map/dot_general | solution.py:162
  151.5 1.0 fusion.63
  152.6 2.8 %collective-permute-start.8 = (bf16[64,1280]{1,0:T(8,128)(2,1)S(1)}, bf16[64,1280]{1,0:T(8,128)(2,1)}, u32[]{:S(2)}, u32[]{:S(2)}) collective-permute-start(bf16[64,1280]{1,0:T(8,128)(2,1)S(1)} %get-tuple-element.24), channel_id=1, source_target_pairs={{0,3},{1,0},{2,1},{3,2},{4,7},{5,4},{6,5},{7,6},{8,11},{9,8},{10,9... | collective-permute-start | bytes 491528 | tf_op jit(solution)/shard_map/ppermute | solution.py:203
  155.6 2.4 %collective-permute-done.6 = bf16[64,1280]{1,0:T(8,128)(2,1)} collective-permute-done((bf16[64,1280]{1,0:T(8,128)(2,1)S(1)}, bf16[64,1280]{1,0:T(8,128)(2,1)}, u32[]{:S(2)}, u32[]{:S(2)}) %collective-permute-start.6) | collective-permute-done | bytes 163872 | tf_op jit(solution)/shard_map/ppermute | solution.py:202
  158.1 2.8 %collective-permute-start.9 = (bf16[64,1280]{1,0:T(8,128)(2,1)}, bf16[64,1280]{1,0:T(8,128)(2,1)S(1)}, u32[]{:S(2)}, u32[]{:S(2)}) collective-permute-start(bf16[64,1280]{1,0:T(8,128)(2,1)} %collective-permute-done.8), channel_id=1, source_target_pairs={{0,3},{1,0},{2,1},{3,2},{4,7},{5,4},{6,5},{7,6},{8,11},{9,8},{10,9... | collective-permute-start | bytes 491528 | tf_op jit(solution)/shard_map/ppermute | solution.py:203
  160.9 2.8 %collective-permute-done.7 = bf16[64,1280]{1,0:T(8,128)(2,1)S(1)} collective-permute-done((bf16[64,1280]{1,0:T(8,128)(2,1)}, bf16[64,1280]{1,0:T(8,128)(2,1)S(1)}, u32[]{:S(2)}, u32[]{:S(2)}) %collective-permute-start.7) | collective-permute-done | bytes 163872 | tf_op jit(solution)/shard_map/ppermute | solution.py:202
  163.7 2.8 %fusion.1 = bf16[64,8,1280]{2,1,0:T(8,128)(2,1)} fusion(f32[128,1280]{1,0:T(8,128)S(1)} %get-tuple-element.32, bf16[128,1280]{1,0:T(8,128)(2,1)} %collective-permute-done.3, bf16[128,1280]{1,0:T(8,128)(2,1)} %collective-permute-done.2, bf16[128,1280]{1,0:T(8,128)(2,1)} %convolution_convert_fusion.5, bf16[64,1280]{1,0:T(8,128)(2,1)S(1)} %collective-permute-done.9, ...), kind=kOutput, calls=%fused_computation.4 | convolution fusion | flops 170524672 | bytes 3279360 | tf_op jit(solution)/shard_map/dot_general | solution.py:212
  166.5 10.1 %all-to-all-start.2 = ((bf16[64,8,1280]{2,1,0:T(8,128)(2,1)}), bf16[64,8,1280]{2,1,0:T(8,128)(2,1)}, u32[]{:S(2)}, u32[]{:S(2)}) async-start(bf16[64,8,1280]{2,1,0:T(8,128)(2,1)} %fusion.1), calls=%async_computation.2 | async-start | bytes 2621440 | tf_op jit(solution)/shard_map/all_to_all | solution.py:271
  176.7 34.0 %all-to-all-done.2 = bf16[64,8,1280]{2,1,0:T(8,128)(2,1)} async-done(((bf16[64,8,1280]{2,1,0:T(8,128)(2,1)}), bf16[64,8,1280]{2,1,0:T(8,128)(2,1)}, u32[]{:S(2)}, u32[]{:S(2)}) %all-to-all-start.2) | async-done | bytes 1310752 | tf_op jit(solution)/shard_map/all_to_all | solution.py:271
  210.7 3.3 %convolution_convert_fusion = bf16[512,1280]{1,0:T(8,128)(2,1)} fusion(bf16[64,8,1280]{2,1,0:T(8,128)(2,1)} %all-to-all-done.2, s32[512]{0:T(512)S(1)} %fusion.43, pred[512]{0:T(512)(128)(4,1)S(1)} %broadcast_compare_fusion.1), kind=kOutput, calls=%fused_computation | convolution fusion | flops 672268288 | bytes 2624000 | tf_op jit(solution)/shard_map/dot_general | solution.py:212
  (52 shorter events, 1.7 us)
Async XLA Ops:
  0.0 117.3 %copy-start = (bf16[896,1280]{1,0:T(8,128)(2,1)S(1)}, bf16[896,1280]{1,0:T(8,128)(2,1)}, u32[]{:S(2)}) copy-start(bf16[896,1280]{1,0:T(8,128)(2,1)} %param.21) | copy-start | bytes 6881284
  0.0 20.4 %copy-start.2 = (bf16[512,320]{0,1:T(8,128)(2,1)S(1)}, bf16[512,320]{0,1:T(8,128)(2,1)}, u32[]{:S(2)}) copy-start(bf16[512,320]{0,1:T(8,128)(2,1)} %param.13) | copy-start | bytes 983044
  1.4 58.5 %all-to-all-start = ((s32[64,1,128]{2,1,0:T(1,128)}), s32[64,1,128]{2,1,0:T(1,128)S(1)}, u32[]{:S(2)}, u32[]{:S(2)}) async-start(s32[64,1,128]{2,1,0:T(1,128)} %broadcast_in_dim.52), calls=%async_computation | async-start | bytes 65536 | tf_op jit(solution)/shard_map/all_to_all | solution.py:239
  66.7 46.7 %copy-start.4 = (f32[1280]{0:T(1024)S(1)}, f32[1280]{0:T(1024)}, u32[]{:S(2)}) copy-start(f32[1280]{0:T(1024)} %param.18) | copy-start | bytes 15364
  66.7 44.7 %all-to-all-start.1 = ((bf16[64,8,1280]{2,1,0:T(8,128)(2,1)}), bf16[64,8,1280]{2,1,0:T(8,128)(2,1)}, u32[]{:S(2)}, u32[]{:S(2)}) async-start(bf16[64,8,1280]{2,1,0:T(8,128)(2,1)} %fusion), calls=%async_computation.1 | async-start | bytes 2621440 | tf_op jit(solution)/shard_map/all_to_all | solution.py:258
  111.4 4.6 %copy-start.1 = (bf16[1280,896]{1,0:T(8,128)(2,1)S(1)}, bf16[1280,896]{1,0:T(8,128)(2,1)}, u32[]{:S(2)}) copy-start(bf16[1280,896]{1,0:T(8,128)(2,1)} %param.19) | copy-start | bytes 6881284
  113.5 9.8 %collective-permute-start.1 = (bf16[128,1280]{1,0:T(8,128)(2,1)S(1)}, bf16[128,1280]{1,0:T(8,128)(2,1)}, u32[]{:S(2)}, u32[]{:S(2)}) collective-permute-start(bf16[128,1280]{1,0:T(8,128)(2,1)S(1)} %multiply_convert_fusion), channel_id=1, source_target_pairs={{0,3},{1,0},{2,1},{3,2},{4,7},{5,4},{6,5},{7,6},{8,11},{9,8},{10,9... | collective-permute-start | bytes 983048 | tf_op jit(solution)/shard_map/ppermute | solution.py:192
  116.0 10.5 %collective-permute-start = (bf16[128,1280]{1,0:T(8,128)(2,1)S(1)}, bf16[128,1280]{1,0:T(8,128)(2,1)}, u32[]{:S(2)}, u32[]{:S(2)}) collective-permute-start(bf16[128,1280]{1,0:T(8,128)(2,1)S(1)} %multiply_convert_fusion), channel_id=1, source_target_pairs={{0,1},{1,2},{2,3},{3,0},{4,5},{5,6},{6,7},{7,4},{8,9},{9,10},{10,1... | collective-permute-start | bytes 983048 | tf_op jit(solution)/shard_map/ppermute | solution.py:191
  129.4 14.8 %collective-permute-start.5 = (bf16[64,1280]{1,0:T(8,128)(2,1)S(1)}, bf16[64,1280]{1,0:T(8,128)(2,1)S(1)}, u32[]{:S(2)}, u32[]{:S(2)}) collective-permute-start(bf16[64,1280]{1,0:T(8,128)(2,1)S(1)} %slice.44), channel_id=1, source_target_pairs={{0,3},{1,0},{2,1},{3,2},{4,7},{5,4},{6,5},{7,6},{8,11},{9,8},{10,9... | collective-permute-start | bytes 491528 | tf_op jit(solution)/shard_map/ppermute | solution.py:196
  129.7 14.5 %collective-permute-start.4 = (bf16[64,1280]{1,0:T(8,128)(2,1)S(1)}, bf16[64,1280]{1,0:T(8,128)(2,1)}, u32[]{:S(2)}, u32[]{:S(2)}) collective-permute-start(bf16[64,1280]{1,0:T(8,128)(2,1)S(1)} %slice.43), channel_id=1, source_target_pairs={{0,1},{1,2},{2,3},{3,0},{4,5},{5,6},{6,7},{7,4},{8,9},{9,10},{10,1... | collective-permute-start | bytes 491528 | tf_op jit(solution)/shard_map/ppermute | solution.py:195
  131.9 0.9 copy-start.3
  142.7 18.2 %collective-permute-start.2 = (bf16[128,1280]{1,0:T(8,128)(2,1)}, bf16[128,1280]{1,0:T(8,128)(2,1)}, u32[]{:S(2)}, u32[]{:S(2)}) collective-permute-start(bf16[128,1280]{1,0:T(8,128)(2,1)} %get-tuple-element.21), channel_id=1, source_target_pairs={{0,3},{1,0},{2,1},{3,2},{4,7},{5,4},{6,5},{7,6},{8,11},{9,8},{10,9... | collective-permute-start | bytes 983048 | tf_op jit(solution)/shard_map/ppermute | solution.py:198
  144.2 16.7 %collective-permute-start.3 = (bf16[128,1280]{1,0:T(8,128)(2,1)}, bf16[128,1280]{1,0:T(8,128)(2,1)}, u32[]{:S(2)}, u32[]{:S(2)}) collective-permute-start(bf16[128,1280]{1,0:T(8,128)(2,1)} %get-tuple-element.22), channel_id=1, source_target_pairs={{0,1},{1,2},{2,3},{3,0},{4,5},{5,6},{6,7},{7,4},{8,9},{9,10},{10,1... | collective-permute-start | bytes 983048 | tf_op jit(solution)/shard_map/ppermute | solution.py:199
  152.5 5.6 %collective-permute-start.6 = (bf16[64,1280]{1,0:T(8,128)(2,1)S(1)}, bf16[64,1280]{1,0:T(8,128)(2,1)}, u32[]{:S(2)}, u32[]{:S(2)}) collective-permute-start(bf16[64,1280]{1,0:T(8,128)(2,1)S(1)} %get-tuple-element.23), channel_id=1, source_target_pairs={{0,1},{1,2},{2,3},{3,0},{4,5},{5,6},{6,7},{7,4},{8,9},{9,10},{10,1... | collective-permute-start | bytes 491528 | tf_op jit(solution)/shard_map/ppermute | solution.py:202
  152.6 5.5 %collective-permute-start.8 = (bf16[64,1280]{1,0:T(8,128)(2,1)S(1)}, bf16[64,1280]{1,0:T(8,128)(2,1)}, u32[]{:S(2)}, u32[]{:S(2)}) collective-permute-start(bf16[64,1280]{1,0:T(8,128)(2,1)S(1)} %get-tuple-element.24), channel_id=1, source_target_pairs={{0,3},{1,0},{2,1},{3,2},{4,7},{5,4},{6,5},{7,6},{8,11},{9,8},{10,9... | collective-permute-start | bytes 491528 | tf_op jit(solution)/shard_map/ppermute | solution.py:203
  158.1 5.6 %collective-permute-start.7 = (bf16[64,1280]{1,0:T(8,128)(2,1)}, bf16[64,1280]{1,0:T(8,128)(2,1)S(1)}, u32[]{:S(2)}, u32[]{:S(2)}) collective-permute-start(bf16[64,1280]{1,0:T(8,128)(2,1)} %collective-permute-done.6), channel_id=1, source_target_pairs={{0,1},{1,2},{2,3},{3,0},{4,5},{5,6},{6,7},{7,4},{8,9},{9,10},{10,1... | collective-permute-start | bytes 491528 | tf_op jit(solution)/shard_map/ppermute | solution.py:202
  158.1 5.6 %collective-permute-start.9 = (bf16[64,1280]{1,0:T(8,128)(2,1)}, bf16[64,1280]{1,0:T(8,128)(2,1)S(1)}, u32[]{:S(2)}, u32[]{:S(2)}) collective-permute-start(bf16[64,1280]{1,0:T(8,128)(2,1)} %collective-permute-done.8), channel_id=1, source_target_pairs={{0,3},{1,0},{2,1},{3,2},{4,7},{5,4},{6,5},{7,6},{8,11},{9,8},{10,9... | collective-permute-start | bytes 491528 | tf_op jit(solution)/shard_map/ppermute | solution.py:203
  166.5 44.2 %all-to-all-start.2 = ((bf16[64,8,1280]{2,1,0:T(8,128)(2,1)}), bf16[64,8,1280]{2,1,0:T(8,128)(2,1)}, u32[]{:S(2)}, u32[]{:S(2)}) async-start(bf16[64,8,1280]{2,1,0:T(8,128)(2,1)} %fusion.1), calls=%async_computation.2 | async-start | bytes 2621440 | tf_op jit(solution)/shard_map/all_to_all | solution.py:271

commit v9 on v7

--- a/solution.py
+++ b/solution.py
@@ -155,11 +155,45 @@
     ).astype(jnp.bfloat16)
 
 
+def ffn_kernel(x_ref, g_ref, u_ref, d_ref, o_ref, acc_ref):
+    step = pl.program_id(0)
+
+    @pl.when(step == 0)
+    def _():
+        acc_ref[...] = jnp.zeros_like(acc_ref)
+
+    x = x_ref[...]
+    gate = jnp.dot(x, g_ref[...], preferred_element_type=jnp.float32)
+    upward = jnp.dot(x, u_ref[...], preferred_element_type=jnp.float32)
+    hidden = (gate / (1.0 + jnp.exp(-gate)) * upward).astype(jnp.bfloat16)
+    acc_ref[...] += jnp.dot(hidden, d_ref[...], preferred_element_type=jnp.float32)
+
+    @pl.when(step == pl.num_programs(0) - 1)
+    def _():
+        o_ref[...] = acc_ref[...].astype(o_ref.dtype)
+
+
 def ffn_rows(rows, gate_weight, up_weight, down_weight):
-    gate = jnp.dot(rows, gate_weight, preferred_element_type=jnp.float32)
-    upward = jnp.dot(rows, up_weight, preferred_element_type=jnp.float32)
-    hidden = (jax.nn.silu(gate) * upward).astype(jnp.bfloat16)
-    return jnp.dot(hidden, down_weight, preferred_element_type=jnp.float32).astype(jnp.bfloat16)
+    count, width = rows.shape
+    units = gate_weight.shape[1]
+    chunk = LANES
+    flops = 6 * count * width * units
+    moved = 2 * (3 * width * units + 2 * count * width)
+    return pl.pallas_call(
+        ffn_kernel,
+        grid=(units // chunk,),
+        in_specs=[
+            pl.BlockSpec((count, width), lambda j: (0, 0)),
+            pl.BlockSpec((width, chunk), lambda j: (0, j)),
+            pl.BlockSpec((width, chunk), lambda j: (0, j)),
+            pl.BlockSpec((chunk, width), lambda j: (j, 0)),
+        ],
+        out_specs=pl.BlockSpec((count, width), lambda j: (0, 0)),
+        out_shape=jax.ShapeDtypeStruct((count, width), jnp.bfloat16),
+        scratch_shapes=[pltpu.VMEM((count, width), jnp.float32)],
+        compiler_params=pltpu.CompilerParams(dimension_semantics=("arbitrary",)),
+        cost_estimate=pl.CostEstimate(flops=flops, transcendentals=count * units, bytes_accessed=moved),
+    )(rows, gate_weight, up_weight, down_weight)
 
 
 def feed_forward(normed, gate_weight, up_weight, down_weight):

time: 215 us -> 205 us (0.953)
  Pallas kernels: 35.7 us -> 54.6 us
  matrix products: 25.6 us -> 7.42 us
  waiting for transfers between devices: 94.5 us -> 87.1 us
  local copies, waits for them, and re-layouts: 13.2 us -> 8.34 us
    pallas_call x0 -> x2, Pallas kernels: none -> 18.9 us  [ffn_rows(): pl.pallas_call(ffn_kernel, grid=(units // chunk,), in_specs=[pl.BlockSpec...]
    dot_general x4 -> x0, matrix products: 14.2 us -> none  [the longest x2 9.04 us: ffn_rows(): jnp.dot(hidden, down_weight, preferred_element_type=jnp.float32)]
    ppermute x3, waiting for transfers between devices: 12.4 us -> 5.79 us  [feed_forward(): lax.ppermute(normed, 'grp', [(j, (j + k) % groups) for j in range(groups)])]
    dot_general x4, matrix products: 11.4 us -> 7.42 us  [take_rows(): jnp.dot(chosen.astype(table.dtype), table, preferred_element_type=jnp.flo...]
    unnamed x16 -> x10, local copies, waits for them, and re-layouts: 2.95 us -> 0.02 us
    ppermute x3, starting transfers between devices: 1.99 us -> 4.25 us  [feed_forward(): lax.ppermute(part, 'grp', [(j, (j - k) % groups) for j in range(groups)])]
  transfers between devices with their start and end apart: 9 -> 9, of which waited for: 7 -> 5; matrix products, arithmetic and copies ran while one was open for 7% -> 4% of each run, Pallas kernels for 17% -> 21%
where the time goes in v9:
time: 205 us
  waiting for transfers between devices  87.1 us (42%)
  Pallas kernels  54.6 us (27%)
  starting transfers between devices  39.7 us (19%)
  local copies, waits for them, and re-layouts  8.34 us (4%)
  matrix products  7.42 us (4%)
  other arithmetic  4.65 us (2%)
  between operations  3 us (1%)
    pallas_call x1, Pallas kernels, attend(): pl.pallas_call(attention_kernel, grid=(tiles,), in_specs=[pl.BlockSpec((s...  35.7 us
    all_to_all x1, waiting for transfers between devices, on_device(): lax.all_to_all(outgoing.reshape(request_owners, block_rows, -1), 'req', 0...  34.1 us
    all_to_all x1, waiting for transfers between devices, on_device(): lax.all_to_all(outbound.reshape(request_owners, block_rows, -1), 'req', 0...  33.9 us
    pallas_call x2, Pallas kernels, ffn_rows(): pl.pallas_call(ffn_kernel, grid=(units // chunk,), in_specs=[pl.BlockSpec...  18.9 us
    ppermute x3, waiting for transfers between devices, feed_forward(): lax.ppermute(part, 'grp', [(j, (j - k) % groups) for j in range(groups)])  13.3 us
    all_to_all x1, starting transfers between devices, on_device(): lax.all_to_all(jnp.broadcast_to(live_rows.reshape(1, 1), (request_owners,...  13.1 us
    all_to_all x1, starting transfers between devices, on_device(): lax.all_to_all(outbound.reshape(request_owners, block_rows, -1), 'req', 0...  10.3 us
    dot_general x4, matrix products, take_rows(): jnp.dot(chosen.astype(table.dtype), table, preferred_element_type=jnp.flo...  7.42 us
  transfers between devices with their start and end apart: 9, of which 5 were waited for; matrix products, arithmetic and copies ran while one was open for 4% of the time, Pallas kernels for 21%

profile of v9, /device:TPU:1, one launch (start us, length us, event | category | flops | bytes accessed | tf_op | source)
XLA Modules:
  0.0 204.7 jit_solution(18261754657291053760)
XLA Ops:
  0.7 0.6 broadcast_in_dim.52
  1.3 13.1 %all-to-all-start = ((s32[64,1,128]{2,1,0:T(1,128)}), s32[64,1,128]{2,1,0:T(1,128)S(1)}, u32[]{:S(2)}, u32[]{:S(2)}) async-start(s32[64,1,128]{2,1,0:T(1,128)} %broadcast_in_dim.52), calls=%async_computation | async-start | bytes 65536 | tf_op jit(solution)/shard_map/all_to_all | solution.py:247
  14.5 1.0 broadcast_in_dim.58
  15.5 1.1 copy.31.k_ref
  16.7 1.1 copy.32.v_ref
  17.8 0.1 compare_reduce_fusion
  18.0 0.3 reduce-window.19
  18.4 0.1 slice_reduce_fusion
  18.6 0.3 multiply_sine_fusion
  18.9 0.9 copy.33.cos_ref
  19.8 0.8 copy.34.sin_ref
  20.6 0.9 copy.35.segc_ref
  21.5 0.6 iota_subtract_fusion.posr_ref
  22.1 0.6 select_convert_fusion.turn_ref
  22.7 35.7 %shard_map.109 = bf16[512,1280]{1,0:T(8,128)(2,1)} custom-call(bf16[512,1280]{1,0:T(8,128)(2,1)} %q_ref.1, bf16[512,640]{1,0:T(8,128)(2,1)} %copy.31.k_ref, bf16[512,640]{1,0:T(8,128)(2,1)} %copy.32.v_ref, f32[512,128]{1,0:T(8,128)} %copy.33.cos_ref, f32[512,128]{1,0:T(8,128)} %copy.34.sin_ref, bf16[128,128]{1,0:T(8,128)(2,1)} %select_convert_fusion.turn_ref, ...), custom_call_target="tpu_custom_call" | custom-call | tf_op jit(solution)/shard_map/pallas_call | solution.py:115
  58.4 0.1 slice_reduce_fusion.1
  58.5 0.1 reduce-window.18
  58.6 0.1 reduce
  58.8 0.7 fusion.34
  61.6 0.1 add_add_fusion
  61.7 0.1 add.251
  61.8 3.3 %fusion = bf16[64,8,1280]{2,1,0:T(8,128)(2,1)} fusion(bf16[512,1280]{1,0:T(8,128)(2,1)} %shard_map.109, s32[512]{0:T(512)S(1)} %add.251, pred[512]{0:T(512)(128)(4,1)S(1)} %broadcast_compare_fusion), kind=kOutput, calls=%fused_computation.3 | convolution fusion | flops 672268288 | bytes 2624000 | tf_op jit(solution)/shard_map/dot_general | solution.py:220
  65.1 10.3 %all-to-all-start.1 = ((bf16[64,8,1280]{2,1,0:T(8,128)(2,1)}), bf16[64,8,1280]{2,1,0:T(8,128)(2,1)S(1)}, u32[]{:S(2)}, u32[]{:S(2)}) async-start(bf16[64,8,1280]{2,1,0:T(8,128)(2,1)} %fusion), calls=%async_computation.1 | async-start | bytes 2621440 | tf_op jit(solution)/shard_map/all_to_all | solution.py:266
  75.5 0.1 convert_reduce_fusion
  75.6 0.1 select_reduce_fusion
  75.7 33.9 %all-to-all-done.1 = bf16[64,8,1280]{2,1,0:T(8,128)(2,1)S(1)} async-done(((bf16[64,8,1280]{2,1,0:T(8,128)(2,1)}), bf16[64,8,1280]{2,1,0:T(8,128)(2,1)S(1)}, u32[]{:S(2)}, u32[]{:S(2)}) %all-to-all-start.1) | async-done | bytes 1310752 | tf_op jit(solution)/shard_map/all_to_all | solution.py:266
  109.6 0.5 multiply_reduce_fusion
  110.1 0.1 multiply_convert_fusion.x_ref
  110.2 1.3 collective-permute-start
  111.5 2.4 %collective-permute-start.1 = (bf16[128,1280]{1,0:T(8,128)(2,1)S(1)}, bf16[128,1280]{1,0:T(8,128)(2,1)S(1)}, u32[]{:S(2)}, u32[]{:S(2)}) collective-permute-start(bf16[128,1280]{1,0:T(8,128)(2,1)S(1)} %multiply_convert_fusion.x_ref), channel_id=1, source_target_pairs={{0,2},{1,3},{2,0},{3,1},{4,6},{5,7},{6,4},{7,5},{8,10},{9,11},{10,... | collective-permute-start | bytes 983048 | tf_op jit(solution)/shard_map/ppermute | solution.py:203
  113.9 1.2 collective-permute-start.2
  115.1 8.1 %shard_map.110 = bf16[128,1280]{1,0:T(8,128)(2,1)} custom-call(bf16[128,1280]{1,0:T(8,128)(2,1)} %copy-done.1, bf16[1280,896]{1,0:T(8,128)(2,1)} %g_ref.3, bf16[1280,896]{1,0:T(8,128)(2,1)} %u_ref.3, bf16[896,1280]{1,0:T(8,128)(2,1)} %d_ref.3), custom_call_target="tpu_custom_call" | custom-call | flops 880803840 | bytes 7536640 | tf_op jit(solution)/shard_map/pallas_call | solution.py:182
  123.2 5.8 %collective-permute-done.1 = bf16[128,1280]{1,0:T(8,128)(2,1)S(1)} collective-permute-done((bf16[128,1280]{1,0:T(8,128)(2,1)S(1)}, bf16[128,1280]{1,0:T(8,128)(2,1)S(1)}, u32[]{:S(2)}, u32[]{:S(2)}) %collective-permute-start.1) | collective-permute-done | bytes 327712 | tf_op jit(solution)/shard_map/ppermute | solution.py:203
  129.0 1.0 pad_maximum_fusion.x_ref
  130.0 10.8 %shard_map.111 = bf16[384,1280]{1,0:T(8,128)(2,1)} custom-call(bf16[384,1280]{1,0:T(8,128)(2,1)} %pad_maximum_fusion.x_ref, bf16[1280,896]{1,0:T(8,128)(2,1)} %g_ref.3, bf16[1280,896]{1,0:T(8,128)(2,1)} %u_ref.3, bf16[896,1280]{1,0:T(8,128)(2,1)} %d_ref.3), custom_call_target="tpu_custom_call" | custom-call | flops 2642411520 | bytes 8847360 | tf_op jit(solution)/shard_map/pallas_call | solution.py:182
  140.8 1.3 fusion.39
  142.0 0.7 collective-permute-start.5
  142.7 2.8 %collective-permute-start.4 = (bf16[128,1280]{1,0:T(8,128)(2,1)S(1)}, bf16[128,1280]{1,0:T(8,128)(2,1)S(1)}, u32[]{:S(2)}, u32[]{:S(2)}) collective-permute-start(bf16[128,1280]{1,0:T(8,128)(2,1)S(1)} %get-tuple-element.21), channel_id=1, source_target_pairs={{0,2},{1,3},{2,0},{3,1},{4,6},{5,7},{6,4},{7,5},{8,10},{9,11},{10,... | collective-permute-start | bytes 983048 | tf_op jit(solution)/shard_map/ppermute | solution.py:212
  145.5 0.8 collective-permute-start.3
  146.3 0.1 add_compare_fusion
  146.4 0.1 lt.81
  146.5 0.1 add.244
  146.6 5.3 %collective-permute-done.5 = bf16[128,1280]{1,0:T(8,128)(2,1)S(1)} collective-permute-done((bf16[128,1280]{1,0:T(8,128)(2,1)S(1)}, bf16[128,1280]{1,0:T(8,128)(2,1)S(1)}, u32[]{:S(2)}, u32[]{:S(2)}) %collective-permute-start.5) | collective-permute-done | bytes 327712 | tf_op jit(solution)/shard_map/ppermute | solution.py:212
  151.9 7.9 %collective-permute-done.4 = bf16[128,1280]{1,0:T(8,128)(2,1)S(1)} collective-permute-done((bf16[128,1280]{1,0:T(8,128)(2,1)S(1)}, bf16[128,1280]{1,0:T(8,128)(2,1)S(1)}, u32[]{:S(2)}, u32[]{:S(2)}) %collective-permute-start.4) | collective-permute-done | bytes 327712 | tf_op jit(solution)/shard_map/ppermute | solution.py:212
  159.9 1.7 fusion.1
  161.5 7.1 %all-to-all-start.2 = ((bf16[64,8,1280]{2,1,0:T(8,128)(2,1)}), bf16[64,8,1280]{2,1,0:T(8,128)(2,1)S(1)}, u32[]{:S(2)}, u32[]{:S(2)}) async-start(bf16[64,8,1280]{2,1,0:T(8,128)(2,1)} %fusion.1), calls=%async_computation.2 | async-start | bytes 2621440 | tf_op jit(solution)/shard_map/all_to_all | solution.py:279
  168.6 34.1 %all-to-all-done.2 = bf16[64,8,1280]{2,1,0:T(8,128)(2,1)S(1)} async-done(((bf16[64,8,1280]{2,1,0:T(8,128)(2,1)}), bf16[64,8,1280]{2,1,0:T(8,128)(2,1)S(1)}, u32[]{:S(2)}, u32[]{:S(2)}) %all-to-all-start.2) | async-done | bytes 1310752 | tf_op jit(solution)/shard_map/all_to_all | solution.py:279
  202.7 2.0 convolution_convert_fusion
  (34 shorter events, 0.5 us)
Async XLA Ops:
  0.0 16.6 %copy-start.2 = (bf16[512,320]{0,1:T(8,128)(2,1)S(1)}, bf16[512,320]{0,1:T(8,128)(2,1)}, u32[]{:S(2)}) copy-start(bf16[512,320]{0,1:T(8,128)(2,1)} %param.14) | copy-start | bytes 983044
  1.3 57.1 %all-to-all-start = ((s32[64,1,128]{2,1,0:T(1,128)}), s32[64,1,128]{2,1,0:T(1,128)S(1)}, u32[]{:S(2)}, u32[]{:S(2)}) async-start(s32[64,1,128]{2,1,0:T(1,128)} %broadcast_in_dim.52), calls=%async_computation | async-start | bytes 65536 | tf_op jit(solution)/shard_map/all_to_all | solution.py:247
  16.6 1.2 copy-start.3
  65.1 44.5 %all-to-all-start.1 = ((bf16[64,8,1280]{2,1,0:T(8,128)(2,1)}), bf16[64,8,1280]{2,1,0:T(8,128)(2,1)S(1)}, u32[]{:S(2)}, u32[]{:S(2)}) async-start(bf16[64,8,1280]{2,1,0:T(8,128)(2,1)} %fusion), calls=%async_computation.1 | async-start | bytes 2621440 | tf_op jit(solution)/shard_map/all_to_all | solution.py:266
  75.4 34.6 %copy-start.4 = (f32[1280]{0:T(1024)S(1)}, f32[1280]{0:T(1024)}, u32[]{:S(2)}) copy-start(f32[1280]{0:T(1024)} %param.18) | copy-start | bytes 15364
  110.2 4.9 %copy-start.1 = (bf16[128,1280]{1,0:T(8,128)(2,1)}, bf16[128,1280]{1,0:T(8,128)(2,1)S(1)}, u32[]{:S(2)}) copy-start(bf16[128,1280]{1,0:T(8,128)(2,1)S(1)} %multiply_convert_fusion.x_ref) | copy-start | bytes 983044
  110.2 13.0 %collective-permute-start = (bf16[128,1280]{1,0:T(8,128)(2,1)S(1)}, bf16[128,1280]{1,0:T(8,128)(2,1)S(1)}, u32[]{:S(2)}, u32[]{:S(2)}) collective-permute-start(bf16[128,1280]{1,0:T(8,128)(2,1)S(1)} %multiply_convert_fusion.x_ref), channel_id=1, source_target_pairs={{0,1},{1,2},{2,3},{3,0},{4,5},{5,6},{6,7},{7,4},{8,9},{9,10},{10,1... | collective-permute-start | bytes 983048 | tf_op jit(solution)/shard_map/ppermute | solution.py:203
  111.5 17.5 %collective-permute-start.1 = (bf16[128,1280]{1,0:T(8,128)(2,1)S(1)}, bf16[128,1280]{1,0:T(8,128)(2,1)S(1)}, u32[]{:S(2)}, u32[]{:S(2)}) collective-permute-start(bf16[128,1280]{1,0:T(8,128)(2,1)S(1)} %multiply_convert_fusion.x_ref), channel_id=1, source_target_pairs={{0,2},{1,3},{2,0},{3,1},{4,6},{5,7},{6,4},{7,5},{8,10},{9,11},{10,... | collective-permute-start | bytes 983048 | tf_op jit(solution)/shard_map/ppermute | solution.py:203
  113.9 15.0 %collective-permute-start.2 = (bf16[128,1280]{1,0:T(8,128)(2,1)S(1)}, bf16[128,1280]{1,0:T(8,128)(2,1)S(1)}, u32[]{:S(2)}, u32[]{:S(2)}) collective-permute-start(bf16[128,1280]{1,0:T(8,128)(2,1)S(1)} %multiply_convert_fusion.x_ref), channel_id=1, source_target_pairs={{0,3},{1,0},{2,1},{3,2},{4,7},{5,4},{6,5},{7,6},{8,11},{9,8},{10,9... | collective-permute-start | bytes 983048 | tf_op jit(solution)/shard_map/ppermute | solution.py:203
  140.8 19.1 %copy-start = (bf16[128,1280]{1,0:T(8,128)(2,1)S(1)}, bf16[128,1280]{1,0:T(8,128)(2,1)}, u32[]{:S(2)}) copy-start(bf16[128,1280]{1,0:T(8,128)(2,1)} %shard_map.110) | copy-start | bytes 983044
  142.0 9.9 %collective-permute-start.5 = (bf16[128,1280]{1,0:T(8,128)(2,1)S(1)}, bf16[128,1280]{1,0:T(8,128)(2,1)S(1)}, u32[]{:S(2)}, u32[]{:S(2)}) collective-permute-start(bf16[128,1280]{1,0:T(8,128)(2,1)S(1)} %get-tuple-element.20), channel_id=1, source_target_pairs={{0,1},{1,2},{2,3},{3,0},{4,5},{5,6},{6,7},{7,4},{8,9},{9,10},{10,1... | collective-permute-start | bytes 983048 | tf_op jit(solution)/shard_map/ppermute | solution.py:212
  142.7 17.1 %collective-permute-start.4 = (bf16[128,1280]{1,0:T(8,128)(2,1)S(1)}, bf16[128,1280]{1,0:T(8,128)(2,1)S(1)}, u32[]{:S(2)}, u32[]{:S(2)}) collective-permute-start(bf16[128,1280]{1,0:T(8,128)(2,1)S(1)} %get-tuple-element.21), channel_id=1, source_target_pairs={{0,2},{1,3},{2,0},{3,1},{4,6},{5,7},{6,4},{7,5},{8,10},{9,11},{10,... | collective-permute-start | bytes 983048 | tf_op jit(solution)/shard_map/ppermute | solution.py:212
  145.5 14.4 %collective-permute-start.3 = (bf16[128,1280]{1,0:T(8,128)(2,1)S(1)}, bf16[128,1280]{1,0:T(8,128)(2,1)S(1)}, u32[]{:S(2)}, u32[]{:S(2)}) collective-permute-start(bf16[128,1280]{1,0:T(8,128)(2,1)S(1)} %get-tuple-element.19), channel_id=1, source_target_pairs={{0,3},{1,0},{2,1},{3,2},{4,7},{5,4},{6,5},{7,6},{8,11},{9,8},{10,9... | collective-permute-start | bytes 983048 | tf_op jit(solution)/shard_map/ppermute | solution.py:212
  161.5 41.2 %all-to-all-start.2 = ((bf16[64,8,1280]{2,1,0:T(8,128)(2,1)}), bf16[64,8,1280]{2,1,0:T(8,128)(2,1)S(1)}, u32[]{:S(2)}, u32[]{:S(2)}) async-start(bf16[64,8,1280]{2,1,0:T(8,128)(2,1)} %fusion.1), calls=%async_computation.2 | async-start | bytes 2621440 | tf_op jit(solution)/shard_map/all_to_all | solution.py:279

commit v10 on v9

--- a/solution.py
+++ b/solution.py
@@ -38,7 +38,7 @@
     return turn.astype(jnp.bfloat16)
 
 
-def attention_kernel(q_ref, k_ref, v_ref, cos_ref, sin_ref, turn_ref, segc_ref, segr_ref, posr_ref, w_ref, h_ref, out_ref, bias_ref, acc_ref):
+def attention_kernel(q_ref, k_ref, v_ref, cos_ref, sin_ref, turn_ref, segc_ref, segr_ref, posr_ref, w_ref, h_ref, out_ref, bias_ref, ctx_ref):
     slots = q_ref.shape[0]
     block = LANES
 
@@ -49,7 +49,6 @@
         allowed = (segc_ref[...] == segr_ref[...]) & (ki <= qi)
         allowed = allowed & ((qi - ki < WINDOW) | (posr_ref[...] < SINK))
         bias_ref[...] = jnp.where(allowed, 0.0, -jnp.inf).astype(jnp.float32)
-        acc_ref[...] = h_ref[...].astype(jnp.float32)
 
     cosine = cos_ref[...]
     sine = sin_ref[...]
@@ -85,13 +84,15 @@
             weights = (raised * (1.0 / total)).astype(jnp.bfloat16)
             parts.append(jnp.dot(weights, v_part, preferred_element_type=jnp.float32))
         context = jnp.where(low, parts[0], parts[1]).astype(jnp.bfloat16)
-        acc_ref[i * block:(i + 1) * block, :] += jnp.dot(
-            context, w_ref[...], preferred_element_type=jnp.float32
-        )
+        ctx_ref[pl.program_id(0), i * block:(i + 1) * block, :] = context
 
     @pl.when(pl.program_id(0) == pl.num_programs(0) - 1)
     def _():
-        out_ref[...] = acc_ref[...].astype(out_ref.dtype)
+        heads = jnp.concatenate([ctx_ref[t] for t in range(ctx_ref.shape[0])], axis=1)
+        mixed = h_ref[...].astype(jnp.float32) + jnp.dot(
+            heads, w_ref[...], preferred_element_type=jnp.float32
+        )
+        out_ref[...] = mixed.astype(out_ref.dtype)
 
 
 def attend(queries, projected_keys, projected_values, segment, out_weight, hidden_in):
@@ -125,14 +126,14 @@
             pl.BlockSpec((slot_capacity, 1), full),
             pl.BlockSpec((1, slot_capacity), full),
             pl.BlockSpec((1, slot_capacity), full),
-            pl.BlockSpec((LANES, width), lambda t: (t, 0)),
+            pl.BlockSpec((width, width), full),
             pl.BlockSpec((slot_capacity, width), full),
         ],
         out_specs=pl.BlockSpec((slot_capacity, width), full),
         out_shape=jax.ShapeDtypeStruct((slot_capacity, width), jnp.bfloat16),
         scratch_shapes=[
             pltpu.VMEM((slot_capacity, slot_capacity), jnp.float32),
-            pltpu.VMEM((slot_capacity, width), jnp.float32),
+            pltpu.VMEM((tiles, slot_capacity, LANES), jnp.bfloat16),
         ],
         compiler_params=pltpu.CompilerParams(dimension_semantics=("arbitrary",)),
     )(
@@ -176,7 +177,7 @@
 def ffn_rows(rows, gate_weight, up_weight, down_weight):
     count, width = rows.shape
     units = gate_weight.shape[1]
-    chunk = LANES
+    chunk = units
     flops = 6 * count * width * units
     moved = 2 * (3 * width * units + 2 * count * width)
     return pl.pallas_call(

time: 205 us -> 199 us (0.971)
  Pallas kernels: 54.6 us -> 45.9 us
  waiting for transfers between devices: 87.1 us -> 89.9 us
    pallas_call x2, Pallas kernels: 18.9 us -> 12.8 us  [ffn_rows(): pl.pallas_call(ffn_kernel, grid=(units // chunk,), in_specs=[pl.BlockSpec...]
    ppermute x3, waiting for transfers between devices: 5.79 us -> 8.67 us  [feed_forward(): lax.ppermute(normed, 'grp', [(j, (j + k) % groups) for j in range(groups)])]
    pallas_call x1, Pallas kernels: 35.7 us -> 33.1 us  [attend(): pl.pallas_call(attention_kernel, grid=(tiles,), in_specs=[pl.BlockSpec((s...]
  transfers between devices with their start and end apart: 9 -> 9, of which waited for: 5 -> 6; matrix products, arithmetic and copies ran while one was open for 4% -> 4% of each run, Pallas kernels for 21% -> 19%
where the time goes in v10:
time: 199 us
  waiting for transfers between devices  89.9 us (45%)
  Pallas kernels  45.9 us (23%)
  starting transfers between devices  39.7 us (20%)
  local copies, waits for them, and re-layouts  8.34 us (4%)
  matrix products  7.42 us (4%)
  other arithmetic  4.65 us (2%)
  between operations  3 us (2%)
    all_to_all x1, waiting for transfers between devices, on_device(): lax.all_to_all(outgoing.reshape(request_owners, block_rows, -1), 'req', 0...  34.1 us
    all_to_all x1, waiting for transfers between devices, on_device(): lax.all_to_all(outbound.reshape(request_owners, block_rows, -1), 'req', 0...  33.9 us
    pallas_call x1, Pallas kernels, attend(): pl.pallas_call(attention_kernel, grid=(tiles,), in_specs=[pl.BlockSpec((s...  33.1 us
    ppermute x3, waiting for transfers between devices, feed_forward(): lax.ppermute(part, 'grp', [(j, (j - k) % groups) for j in range(groups)])  13.2 us
    all_to_all x1, starting transfers between devices, on_device(): lax.all_to_all(jnp.broadcast_to(live_rows.reshape(1, 1), (request_owners,...  13.1 us
    pallas_call x2, Pallas kernels, ffn_rows(): pl.pallas_call(ffn_kernel, grid=(units // chunk,), in_specs=[pl.BlockSpec...  12.8 us
    all_to_all x1, starting transfers between devices, on_device(): lax.all_to_all(outbound.reshape(request_owners, block_rows, -1), 'req', 0...  10.3 us
    ppermute x3, waiting for transfers between devices, feed_forward(): lax.ppermute(normed, 'grp', [(j, (j + k) % groups) for j in range(groups)])  8.67 us
  transfers between devices with their start and end apart: 9, of which 6 were waited for; matrix products, arithmetic and copies ran while one was open for 4% of the time, Pallas kernels for 19%

profile of v10, /device:TPU:1, one launch (start us, length us, event | category | flops | bytes accessed | tf_op | source)
XLA Modules:
  0.0 198.9 jit_solution(12934105324765753178)
XLA Ops:
  0.7 0.6 broadcast_in_dim.52
  1.3 13.1 %all-to-all-start = ((s32[64,1,128]{2,1,0:T(1,128)}), s32[64,1,128]{2,1,0:T(1,128)S(1)}, u32[]{:S(2)}, u32[]{:S(2)}) async-start(s32[64,1,128]{2,1,0:T(1,128)} %broadcast_in_dim.52), calls=%async_computation | async-start | bytes 65536 | tf_op jit(solution)/shard_map/all_to_all | solution.py:248
  14.5 1.0 broadcast_in_dim.58
  15.5 1.1 copy.31.k_ref
  16.7 1.1 copy.32.v_ref
  17.8 0.1 compare_reduce_fusion
  18.0 0.3 reduce-window.19
  18.4 0.1 slice_reduce_fusion
  18.6 0.3 multiply_sine_fusion
  18.9 0.9 copy.33.cos_ref
  19.8 0.8 copy.34.sin_ref
  20.6 0.9 copy.35.segc_ref
  21.5 0.6 iota_subtract_fusion.posr_ref
  22.1 0.6 select_convert_fusion.turn_ref
  22.7 33.1 %shard_map.109 = bf16[512,1280]{1,0:T(8,128)(2,1)} custom-call(bf16[512,1280]{1,0:T(8,128)(2,1)} %q_ref.1, bf16[512,640]{1,0:T(8,128)(2,1)} %copy.31.k_ref, bf16[512,640]{1,0:T(8,128)(2,1)} %copy.32.v_ref, f32[512,128]{1,0:T(8,128)} %copy.33.cos_ref, f32[512,128]{1,0:T(8,128)} %copy.34.sin_ref, bf16[128,128]{1,0:T(8,128)(2,1)} %select_convert_fusion.turn_ref, ...), custom_call_target="tpu_custom_call" | custom-call | tf_op jit(solution)/shard_map/pallas_call | solution.py:116
  55.8 0.1 slice_reduce_fusion.1
  55.9 0.1 reduce-window.18
  56.0 0.1 reduce
  56.1 0.7 fusion.34
  59.0 0.1 add_add_fusion
  59.1 0.1 add.251
  59.2 3.3 %fusion = bf16[64,8,1280]{2,1,0:T(8,128)(2,1)} fusion(bf16[512,1280]{1,0:T(8,128)(2,1)} %shard_map.109, s32[512]{0:T(512)S(1)} %add.251, pred[512]{0:T(512)(128)(4,1)S(1)} %broadcast_compare_fusion), kind=kOutput, calls=%fused_computation.3 | convolution fusion | flops 672268288 | bytes 2624000 | tf_op jit(solution)/shard_map/dot_general | solution.py:221
  62.5 10.3 %all-to-all-start.1 = ((bf16[64,8,1280]{2,1,0:T(8,128)(2,1)}), bf16[64,8,1280]{2,1,0:T(8,128)(2,1)S(1)}, u32[]{:S(2)}, u32[]{:S(2)}) async-start(bf16[64,8,1280]{2,1,0:T(8,128)(2,1)} %fusion), calls=%async_computation.1 | async-start | bytes 2621440 | tf_op jit(solution)/shard_map/all_to_all | solution.py:267
  72.8 0.1 convert_reduce_fusion
  72.9 0.1 select_reduce_fusion
  73.0 33.9 %all-to-all-done.1 = bf16[64,8,1280]{2,1,0:T(8,128)(2,1)S(1)} async-done(((bf16[64,8,1280]{2,1,0:T(8,128)(2,1)}), bf16[64,8,1280]{2,1,0:T(8,128)(2,1)S(1)}, u32[]{:S(2)}, u32[]{:S(2)}) %all-to-all-start.1) | async-done | bytes 1310752 | tf_op jit(solution)/shard_map/all_to_all | solution.py:267
  106.9 0.5 multiply_reduce_fusion
  107.4 0.1 multiply_convert_fusion.x_ref
  107.6 1.3 collective-permute-start
  108.9 2.4 %collective-permute-start.1 = (bf16[128,1280]{1,0:T(8,128)(2,1)S(1)}, bf16[128,1280]{1,0:T(8,128)(2,1)S(1)}, u32[]{:S(2)}, u32[]{:S(2)}) collective-permute-start(bf16[128,1280]{1,0:T(8,128)(2,1)S(1)} %multiply_convert_fusion.x_ref), channel_id=1, source_target_pairs={{0,2},{1,3},{2,0},{3,1},{4,6},{5,7},{6,4},{7,5},{8,10},{9,11},{10,... | collective-permute-start | bytes 983048 | tf_op jit(solution)/shard_map/ppermute | solution.py:204
  111.3 1.2 collective-permute-start.2
  112.5 5.2 %shard_map.110 = bf16[128,1280]{1,0:T(8,128)(2,1)} custom-call(bf16[128,1280]{1,0:T(8,128)(2,1)} %copy-done.1, bf16[1280,896]{1,0:T(8,128)(2,1)} %g_ref.3, bf16[1280,896]{1,0:T(8,128)(2,1)} %u_ref.3, bf16[896,1280]{1,0:T(8,128)(2,1)} %d_ref.3), custom_call_target="tpu_custom_call" | custom-call | flops 880803840 | bytes 7536640 | tf_op jit(solution)/shard_map/pallas_call | solution.py:183
  117.7 0.7 collective-permute-done
  118.3 8.0 %collective-permute-done.1 = bf16[128,1280]{1,0:T(8,128)(2,1)S(1)} collective-permute-done((bf16[128,1280]{1,0:T(8,128)(2,1)S(1)}, bf16[128,1280]{1,0:T(8,128)(2,1)S(1)}, u32[]{:S(2)}, u32[]{:S(2)}) %collective-permute-start.1) | collective-permute-done | bytes 327712 | tf_op jit(solution)/shard_map/ppermute | solution.py:204
  126.3 1.0 pad_maximum_fusion.x_ref
  127.3 7.6 %shard_map.111 = bf16[384,1280]{1,0:T(8,128)(2,1)} custom-call(bf16[384,1280]{1,0:T(8,128)(2,1)} %pad_maximum_fusion.x_ref, bf16[1280,896]{1,0:T(8,128)(2,1)} %g_ref.3, bf16[1280,896]{1,0:T(8,128)(2,1)} %u_ref.3, bf16[896,1280]{1,0:T(8,128)(2,1)} %d_ref.3), custom_call_target="tpu_custom_call" | custom-call | flops 2642411520 | bytes 8847360 | tf_op jit(solution)/shard_map/pallas_call | solution.py:183
  135.0 1.3 fusion.39
  136.2 0.6 collective-permute-start.5
  136.9 2.8 %collective-permute-start.4 = (bf16[128,1280]{1,0:T(8,128)(2,1)S(1)}, bf16[128,1280]{1,0:T(8,128)(2,1)S(1)}, u32[]{:S(2)}, u32[]{:S(2)}) collective-permute-start(bf16[128,1280]{1,0:T(8,128)(2,1)S(1)} %get-tuple-element.21), channel_id=1, source_target_pairs={{0,2},{1,3},{2,0},{3,1},{4,6},{5,7},{6,4},{7,5},{8,10},{9,11},{10,... | collective-permute-start | bytes 983048 | tf_op jit(solution)/shard_map/ppermute | solution.py:213
  139.7 0.8 collective-permute-start.3
  140.6 0.1 lt.81
  140.7 0.1 add.244
  140.8 5.3 %collective-permute-done.5 = bf16[128,1280]{1,0:T(8,128)(2,1)S(1)} collective-permute-done((bf16[128,1280]{1,0:T(8,128)(2,1)S(1)}, bf16[128,1280]{1,0:T(8,128)(2,1)S(1)}, u32[]{:S(2)}, u32[]{:S(2)}) %collective-permute-start.5) | collective-permute-done | bytes 327712 | tf_op jit(solution)/shard_map/ppermute | solution.py:213
  146.1 7.9 %collective-permute-done.4 = bf16[128,1280]{1,0:T(8,128)(2,1)S(1)} collective-permute-done((bf16[128,1280]{1,0:T(8,128)(2,1)S(1)}, bf16[128,1280]{1,0:T(8,128)(2,1)S(1)}, u32[]{:S(2)}, u32[]{:S(2)}) %collective-permute-start.4) | collective-permute-done | bytes 327712 | tf_op jit(solution)/shard_map/ppermute | solution.py:213
  154.0 1.7 fusion.1
  155.7 7.1 %all-to-all-start.2 = ((bf16[64,8,1280]{2,1,0:T(8,128)(2,1)}), bf16[64,8,1280]{2,1,0:T(8,128)(2,1)S(1)}, u32[]{:S(2)}, u32[]{:S(2)}) async-start(bf16[64,8,1280]{2,1,0:T(8,128)(2,1)} %fusion.1), calls=%async_computation.2 | async-start | bytes 2621440 | tf_op jit(solution)/shard_map/all_to_all | solution.py:280
  162.8 34.1 %all-to-all-done.2 = bf16[64,8,1280]{2,1,0:T(8,128)(2,1)S(1)} async-done(((bf16[64,8,1280]{2,1,0:T(8,128)(2,1)}), bf16[64,8,1280]{2,1,0:T(8,128)(2,1)S(1)}, u32[]{:S(2)}, u32[]{:S(2)}) %all-to-all-start.2) | async-done | bytes 1310752 | tf_op jit(solution)/shard_map/all_to_all | solution.py:280
  196.9 2.0 %convolution_convert_fusion = bf16[512,1280]{1,0:T(8,128)(2,1)} fusion(bf16[64,8,1280]{2,1,0:T(8,128)(2,1)S(1)} %all-to-all-done.2, s32[512]{0:T(512)S(1)} %fusion.24, pred[512]{0:T(512)(128)(4,1)S(1)} %broadcast_compare_fusion.1), kind=kOutput, calls=%fused_computation | convolution fusion | flops 672268288 | bytes 2624000 | tf_op jit(solution)/shard_map/dot_general | solution.py:221
  (34 shorter events, 0.6 us)
Async XLA Ops:
  0.0 16.6 %copy-start.2 = (bf16[512,320]{0,1:T(8,128)(2,1)S(1)}, bf16[512,320]{0,1:T(8,128)(2,1)}, u32[]{:S(2)}) copy-start(bf16[512,320]{0,1:T(8,128)(2,1)} %param.14) | copy-start | bytes 983044
  1.3 54.5 %all-to-all-start = ((s32[64,1,128]{2,1,0:T(1,128)}), s32[64,1,128]{2,1,0:T(1,128)S(1)}, u32[]{:S(2)}, u32[]{:S(2)}) async-start(s32[64,1,128]{2,1,0:T(1,128)} %broadcast_in_dim.52), calls=%async_computation | async-start | bytes 65536 | tf_op jit(solution)/shard_map/all_to_all | solution.py:248
  16.6 1.2 copy-start.3
  62.5 44.5 %all-to-all-start.1 = ((bf16[64,8,1280]{2,1,0:T(8,128)(2,1)}), bf16[64,8,1280]{2,1,0:T(8,128)(2,1)S(1)}, u32[]{:S(2)}, u32[]{:S(2)}) async-start(bf16[64,8,1280]{2,1,0:T(8,128)(2,1)} %fusion), calls=%async_computation.1 | async-start | bytes 2621440 | tf_op jit(solution)/shard_map/all_to_all | solution.py:267
  72.8 34.6 %copy-start.4 = (f32[1280]{0:T(1024)S(1)}, f32[1280]{0:T(1024)}, u32[]{:S(2)}) copy-start(f32[1280]{0:T(1024)} %param.18) | copy-start | bytes 15364
  107.6 4.9 %copy-start.1 = (bf16[128,1280]{1,0:T(8,128)(2,1)}, bf16[128,1280]{1,0:T(8,128)(2,1)S(1)}, u32[]{:S(2)}) copy-start(bf16[128,1280]{1,0:T(8,128)(2,1)S(1)} %multiply_convert_fusion.x_ref) | copy-start | bytes 983044
  107.6 10.8 %collective-permute-start = (bf16[128,1280]{1,0:T(8,128)(2,1)S(1)}, bf16[128,1280]{1,0:T(8,128)(2,1)S(1)}, u32[]{:S(2)}, u32[]{:S(2)}) collective-permute-start(bf16[128,1280]{1,0:T(8,128)(2,1)S(1)} %multiply_convert_fusion.x_ref), channel_id=1, source_target_pairs={{0,1},{1,2},{2,3},{3,0},{4,5},{5,6},{6,7},{7,4},{8,9},{9,10},{10,1... | collective-permute-start | bytes 983048 | tf_op jit(solution)/shard_map/ppermute | solution.py:204
  108.9 17.5 %collective-permute-start.1 = (bf16[128,1280]{1,0:T(8,128)(2,1)S(1)}, bf16[128,1280]{1,0:T(8,128)(2,1)S(1)}, u32[]{:S(2)}, u32[]{:S(2)}) collective-permute-start(bf16[128,1280]{1,0:T(8,128)(2,1)S(1)} %multiply_convert_fusion.x_ref), channel_id=1, source_target_pairs={{0,2},{1,3},{2,0},{3,1},{4,6},{5,7},{6,4},{7,5},{8,10},{9,11},{10,... | collective-permute-start | bytes 983048 | tf_op jit(solution)/shard_map/ppermute | solution.py:204
  111.3 15.0 %collective-permute-start.2 = (bf16[128,1280]{1,0:T(8,128)(2,1)S(1)}, bf16[128,1280]{1,0:T(8,128)(2,1)S(1)}, u32[]{:S(2)}, u32[]{:S(2)}) collective-permute-start(bf16[128,1280]{1,0:T(8,128)(2,1)S(1)} %multiply_convert_fusion.x_ref), channel_id=1, source_target_pairs={{0,3},{1,0},{2,1},{3,2},{4,7},{5,4},{6,5},{7,6},{8,11},{9,8},{10,9... | collective-permute-start | bytes 983048 | tf_op jit(solution)/shard_map/ppermute | solution.py:204
  135.0 19.1 %copy-start = (bf16[128,1280]{1,0:T(8,128)(2,1)S(1)}, bf16[128,1280]{1,0:T(8,128)(2,1)}, u32[]{:S(2)}) copy-start(bf16[128,1280]{1,0:T(8,128)(2,1)} %shard_map.110) | copy-start | bytes 983044
  136.2 9.9 %collective-permute-start.5 = (bf16[128,1280]{1,0:T(8,128)(2,1)S(1)}, bf16[128,1280]{1,0:T(8,128)(2,1)S(1)}, u32[]{:S(2)}, u32[]{:S(2)}) collective-permute-start(bf16[128,1280]{1,0:T(8,128)(2,1)S(1)} %get-tuple-element.20), channel_id=1, source_target_pairs={{0,1},{1,2},{2,3},{3,0},{4,5},{5,6},{6,7},{7,4},{8,9},{9,10},{10,1... | collective-permute-start | bytes 983048 | tf_op jit(solution)/shard_map/ppermute | solution.py:213
  136.9 17.2 %collective-permute-start.4 = (bf16[128,1280]{1,0:T(8,128)(2,1)S(1)}, bf16[128,1280]{1,0:T(8,128)(2,1)S(1)}, u32[]{:S(2)}, u32[]{:S(2)}) collective-permute-start(bf16[128,1280]{1,0:T(8,128)(2,1)S(1)} %get-tuple-element.21), channel_id=1, source_target_pairs={{0,2},{1,3},{2,0},{3,1},{4,6},{5,7},{6,4},{7,5},{8,10},{9,11},{10,... | collective-permute-start | bytes 983048 | tf_op jit(solution)/shard_map/ppermute | solution.py:213
  139.7 14.4 %collective-permute-start.3 = (bf16[128,1280]{1,0:T(8,128)(2,1)S(1)}, bf16[128,1280]{1,0:T(8,128)(2,1)S(1)}, u32[]{:S(2)}, u32[]{:S(2)}) collective-permute-start(bf16[128,1280]{1,0:T(8,128)(2,1)S(1)} %get-tuple-element.19), channel_id=1, source_target_pairs={{0,3},{1,0},{2,1},{3,2},{4,7},{5,4},{6,5},{7,6},{8,11},{9,8},{10,9... | collective-permute-start | bytes 983048 | tf_op jit(solution)/shard_map/ppermute | solution.py:213
  155.7 41.2 %all-to-all-start.2 = ((bf16[64,8,1280]{2,1,0:T(8,128)(2,1)}), bf16[64,8,1280]{2,1,0:T(8,128)(2,1)S(1)}, u32[]{:S(2)}, u32[]{:S(2)}) async-start(bf16[64,8,1280]{2,1,0:T(8,128)(2,1)} %fusion.1), calls=%async_computation.2 | async-start | bytes 2621440 | tf_op jit(solution)/shard_map/all_to_all | solution.py:280

commit v11 on v10

--- a/solution.py
+++ b/solution.py
@@ -38,7 +38,7 @@
     return turn.astype(jnp.bfloat16)
 
 
-def attention_kernel(q_ref, k_ref, v_ref, cos_ref, sin_ref, turn_ref, segc_ref, segr_ref, posr_ref, w_ref, h_ref, out_ref, bias_ref, ctx_ref):
+def attention_kernel(q_ref, k_ref, v_ref, pick_ref, cos_ref, sin_ref, turn_ref, segc_ref, segr_ref, posr_ref, w_ref, h_ref, out_ref, bias_ref, ctx_ref):
     slots = q_ref.shape[0]
     block = LANES
 
@@ -59,8 +59,9 @@
         return (x.astype(jnp.float32) * cosine + turned * sine).astype(jnp.bfloat16)
 
     q_rot = rotate(q_ref[...]) * jnp.bfloat16(1.0 / math.sqrt(HEAD_SIZE))
-    k_rot = rotate(k_ref[...])
-    v = v_ref[...]
+    pick = pick_ref[...]
+    k_rot = rotate(jnp.dot(k_ref[...], pick, preferred_element_type=jnp.float32).astype(jnp.bfloat16))
+    v = jnp.dot(v_ref[...], pick, preferred_element_type=jnp.float32).astype(jnp.bfloat16)
     lane = lax.broadcasted_iota(jnp.int32, (1, LANES), 1)
     low = lane < HEAD_SIZE
     zero = jnp.zeros((), jnp.bfloat16)
@@ -103,12 +104,13 @@
     token_position = slots - starts
     cosine, sine = rotation_tables(token_position)
     turn = half_turn_matrix()
-    def doubled(x):
-        x = x.reshape(slot_capacity, KEY_VALUE_HEADS, 1, HEAD_SIZE)
-        x = jnp.broadcast_to(x, (slot_capacity, KEY_VALUE_HEADS, 2, HEAD_SIZE))
-        return x.reshape(slot_capacity, KEY_VALUE_HEADS * 2 * HEAD_SIZE)
-    keys2 = doubled(projected_keys)
-    values2 = doubled(projected_values)
+    padded = -projected_keys.shape[1] % LANES
+    keys2 = jnp.pad(projected_keys, ((0, 0), (0, padded)))
+    values2 = jnp.pad(projected_values, ((0, 0), (0, padded)))
+    lane = jnp.arange(LANES, dtype=jnp.int32)
+    halves = jnp.arange(LANES // HEAD_SIZE, dtype=jnp.int32)[:, None, None]
+    picks = (lane[None, :, None] == halves * HEAD_SIZE + lane[None, None, :] % HEAD_SIZE)
+    picks = picks.astype(jnp.bfloat16)
     tiles = QUERY_HEADS * HEAD_SIZE // LANES
     per_kv = tiles // KEY_VALUE_HEADS
     full = lambda t: (0, 0)
@@ -118,8 +120,9 @@
         grid=(tiles,),
         in_specs=[
             pl.BlockSpec((slot_capacity, LANES), lambda t: (0, t)),
-            pl.BlockSpec((slot_capacity, LANES), lambda t: (0, t // per_kv)),
-            pl.BlockSpec((slot_capacity, LANES), lambda t: (0, t // per_kv)),
+            pl.BlockSpec((slot_capacity, LANES), lambda t: (0, t // per_kv // 2)),
+            pl.BlockSpec((slot_capacity, LANES), lambda t: (0, t // per_kv // 2)),
+            pl.BlockSpec((None, LANES, LANES), lambda t: (t // per_kv % 2, 0, 0)),
             pl.BlockSpec((slot_capacity, LANES), full),
             pl.BlockSpec((slot_capacity, LANES), full),
             pl.BlockSpec((LANES, LANES), full),
@@ -137,7 +140,7 @@
         ],
         compiler_params=pltpu.CompilerParams(dimension_semantics=("arbitrary",)),
     )(
-        queries, keys2, values2, cosine, sine, turn,
+        queries, keys2, values2, picks, cosine, sine, turn,
         segment.reshape(slot_capacity, 1), segment.reshape(1, slot_capacity),
         token_position.reshape(1, slot_capacity), out_weight, hidden_in,
     )

time: 199 us -> 203 us (1.020)
  waiting for transfers between devices: 89.9 us -> 93.5 us
    ppermute x3, waiting for transfers between devices: 13.2 us -> 16.8 us  [feed_forward(): lax.ppermute(part, 'grp', [(j, (j - k) % groups) for j in range(groups)])]
    reshape x2 -> x0, local copies, waits for them, and re-layouts: 2.17 us -> none  [doubled(): return x.reshape(slot_capacity, KEY_VALUE_HEADS * 2 * HEAD_SIZE)]
  transfers between devices with their start and end apart: 9 -> 9, of which waited for: 6 -> 7; matrix products, arithmetic and copies ran while one was open for 4% -> 4% of each run, Pallas kernels for 19% -> 20%
where the time goes in v11:
time: 203 us; the launch traced here: 202 us
  waiting for transfers between devices  93.5 us (46%)
  Pallas kernels  47.4 us (23%)
  starting transfers between devices  37.8 us (19%)
  matrix products  7.42 us (4%)
  local copies, waits for them, and re-layouts  7.11 us (4%)
  other arithmetic  6.11 us (3%)
  between operations  3.04 us (1%)
    pallas_call x1, Pallas kernels, attend(): pl.pallas_call(attention_kernel, grid=(tiles,), in_specs=[pl.BlockSpec((s...  34.6 us
    all_to_all x1, waiting for transfers between devices, on_device(): lax.all_to_all(outgoing.reshape(request_owners, block_rows, -1), 'req', 0...  34.1 us
    all_to_all x1, waiting for transfers between devices, on_device(): lax.all_to_all(outbound.reshape(request_owners, block_rows, -1), 'req', 0...  33.9 us
    ppermute x3, waiting for transfers between devices, feed_forward(): lax.ppermute(part, 'grp', [(j, (j - k) % groups) for j in range(groups)])  16.8 us
    all_to_all x1, starting transfers between devices, on_device(): lax.all_to_all(jnp.broadcast_to(live_rows.reshape(1, 1), (request_owners,...  13.1 us
    pallas_call x2, Pallas kernels, ffn_rows(): pl.pallas_call(ffn_kernel, grid=(units // chunk,), in_specs=[pl.BlockSpec...  12.8 us
    all_to_all x1, starting transfers between devices, on_device(): lax.all_to_all(outbound.reshape(request_owners, block_rows, -1), 'req', 0...  10.3 us
    ppermute x3, waiting for transfers between devices, feed_forward(): lax.ppermute(normed, 'grp', [(j, (j + k) % groups) for j in range(groups)])  8.66 us
  transfers between devices with their start and end apart: 9, of which 7 were waited for; matrix products, arithmetic and copies ran while one was open for 4% of the time, Pallas kernels for 20%

profile of v11, /device:TPU:1, one launch (start us, length us, event | category | flops | bytes accessed | tf_op | source)
XLA Modules:
  0.0 202.4 jit_solution(3555544184437144589)
XLA Ops:
  0.7 0.6 broadcast_in_dim.44
  1.3 13.1 %all-to-all-start = ((s32[64,1,128]{2,1,0:T(1,128)}), s32[64,1,128]{2,1,0:T(1,128)S(1)}, u32[]{:S(2)}, u32[]{:S(2)}) async-start(s32[64,1,128]{2,1,0:T(1,128)} %broadcast_in_dim.44), calls=%async_computation | async-start | bytes 65536 | tf_op jit(solution)/shard_map/all_to_all | solution.py:251
  14.6 0.8 compare_reduce_fusion
  15.5 0.3 reduce-window.19
  15.9 0.1 slice_reduce_fusion
  16.1 0.3 multiply_sine_fusion
  16.4 0.8 copy.33.cos_ref
  17.3 0.9 copy.34.sin_ref
  18.2 0.6 iota_subtract_fusion.posr_ref
  18.7 0.2 copy.31
  19.0 0.2 copy.32
  19.2 0.8 pad.7.k_ref
  20.0 0.8 pad.8.v_ref
  20.8 0.9 copy.35.segc_ref
  21.7 0.6 fusion.21.pick_ref
  22.4 0.6 select_convert_fusion.turn_ref
  23.0 34.6 %shard_map.109 = bf16[512,1280]{1,0:T(8,128)(2,1)} custom-call(bf16[512,1280]{1,0:T(8,128)(2,1)} %q_ref.1, bf16[512,384]{1,0:T(8,128)(2,1)} %pad.7.k_ref, bf16[512,384]{1,0:T(8,128)(2,1)} %pad.8.v_ref, bf16[2,128,128]{2,1,0:T(8,128)(2,1)} %fusion.21.pick_ref, f32[512,128]{1,0:T(8,128)} %copy.33.cos_ref, f32[512,128]{1,0:T(8,128)} %copy.34.sin_ref, ...), custom_call_target="tpu_custom_call" | custom-call | tf_op jit(solution)/shard_map/pallas_call | solution.py:118
  57.6 0.1 slice_reduce_fusion.1
  57.7 0.1 reduce-window.18
  57.8 0.1 reduce
  57.9 0.7 fusion.35
  61.0 3.3 %fusion = bf16[64,8,1280]{2,1,0:T(8,128)(2,1)} fusion(bf16[512,1280]{1,0:T(8,128)(2,1)} %shard_map.109, s32[512]{0:T(512)S(1)} %add.284, pred[512]{0:T(512)(128)(4,1)S(1)} %broadcast_compare_fusion), kind=kOutput, calls=%fused_computation.3 | convolution fusion | flops 672268288 | bytes 2624000 | tf_op jit(solution)/shard_map/dot_general | solution.py:224
  64.3 10.3 %all-to-all-start.1 = ((bf16[64,8,1280]{2,1,0:T(8,128)(2,1)}), bf16[64,8,1280]{2,1,0:T(8,128)(2,1)S(1)}, u32[]{:S(2)}, u32[]{:S(2)}) async-start(bf16[64,8,1280]{2,1,0:T(8,128)(2,1)} %fusion), calls=%async_computation.1 | async-start | bytes 2621440 | tf_op jit(solution)/shard_map/all_to_all | solution.py:270
  74.6 0.1 convert_reduce_fusion
  74.7 0.1 select_reduce_fusion
  74.8 33.9 %all-to-all-done.1 = bf16[64,8,1280]{2,1,0:T(8,128)(2,1)S(1)} async-done(((bf16[64,8,1280]{2,1,0:T(8,128)(2,1)}), bf16[64,8,1280]{2,1,0:T(8,128)(2,1)S(1)}, u32[]{:S(2)}, u32[]{:S(2)}) %all-to-all-start.1) | async-done | bytes 1310752 | tf_op jit(solution)/shard_map/all_to_all | solution.py:270
  108.7 0.5 multiply_reduce_fusion
  109.2 0.1 multiply_convert_fusion.x_ref
  109.4 1.3 collective-permute-start
  110.7 2.4 %collective-permute-start.1 = (bf16[128,1280]{1,0:T(8,128)(2,1)S(1)}, bf16[128,1280]{1,0:T(8,128)(2,1)S(1)}, u32[]{:S(2)}, u32[]{:S(2)}) collective-permute-start(bf16[128,1280]{1,0:T(8,128)(2,1)S(1)} %multiply_convert_fusion.x_ref), channel_id=1, source_target_pairs={{0,2},{1,3},{2,0},{3,1},{4,6},{5,7},{6,4},{7,5},{8,10},{9,11},{10,... | collective-permute-start | bytes 983048 | tf_op jit(solution)/shard_map/ppermute | solution.py:207
  113.1 1.2 collective-permute-start.2
  114.3 5.2 %shard_map.110 = bf16[128,1280]{1,0:T(8,128)(2,1)} custom-call(bf16[128,1280]{1,0:T(8,128)(2,1)} %copy-done.1, bf16[1280,896]{1,0:T(8,128)(2,1)} %g_ref.3, bf16[1280,896]{1,0:T(8,128)(2,1)} %u_ref.3, bf16[896,1280]{1,0:T(8,128)(2,1)} %d_ref.3), custom_call_target="tpu_custom_call" | custom-call | flops 880803840 | bytes 7536640 | tf_op jit(solution)/shard_map/pallas_call | solution.py:186
  119.5 0.7 collective-permute-done
  120.1 8.0 %collective-permute-done.1 = bf16[128,1280]{1,0:T(8,128)(2,1)S(1)} collective-permute-done((bf16[128,1280]{1,0:T(8,128)(2,1)S(1)}, bf16[128,1280]{1,0:T(8,128)(2,1)S(1)}, u32[]{:S(2)}, u32[]{:S(2)}) %collective-permute-start.1) | collective-permute-done | bytes 327712 | tf_op jit(solution)/shard_map/ppermute | solution.py:207
  128.1 1.0 pad_maximum_fusion.x_ref
  129.1 7.6 %shard_map.111 = bf16[384,1280]{1,0:T(8,128)(2,1)} custom-call(bf16[384,1280]{1,0:T(8,128)(2,1)} %pad_maximum_fusion.x_ref, bf16[1280,896]{1,0:T(8,128)(2,1)} %g_ref.3, bf16[1280,896]{1,0:T(8,128)(2,1)} %u_ref.3, bf16[896,1280]{1,0:T(8,128)(2,1)} %d_ref.3), custom_call_target="tpu_custom_call" | custom-call | flops 2642411520 | bytes 8847360 | tf_op jit(solution)/shard_map/pallas_call | solution.py:186
  136.7 1.3 fusion.40
  138.0 2.2 %collective-permute-start.3 = (bf16[128,1280]{1,0:T(8,128)(2,1)S(1)}, bf16[128,1280]{1,0:T(8,128)(2,1)S(1)}, u32[]{:S(2)}, u32[]{:S(2)}) collective-permute-start(bf16[128,1280]{1,0:T(8,128)(2,1)S(1)} %get-tuple-element.19), channel_id=1, source_target_pairs={{0,3},{1,0},{2,1},{3,2},{4,7},{5,4},{6,5},{7,6},{8,11},{9,8},{10,9... | collective-permute-start | bytes 983048 | tf_op jit(solution)/shard_map/ppermute | solution.py:216
  140.3 0.2 collective-permute-start.4
  140.4 0.6 collective-permute-start.5
  141.3 0.1 lt.87
  141.4 6.2 %collective-permute-done.3 = bf16[128,1280]{1,0:T(8,128)(2,1)S(1)} collective-permute-done((bf16[128,1280]{1,0:T(8,128)(2,1)S(1)}, bf16[128,1280]{1,0:T(8,128)(2,1)S(1)}, u32[]{:S(2)}, u32[]{:S(2)}) %collective-permute-start.3) | collective-permute-done | bytes 327712 | tf_op jit(solution)/shard_map/ppermute | solution.py:216
  147.6 2.8 %collective-permute-done.4 = bf16[128,1280]{1,0:T(8,128)(2,1)S(1)} collective-permute-done((bf16[128,1280]{1,0:T(8,128)(2,1)S(1)}, bf16[128,1280]{1,0:T(8,128)(2,1)S(1)}, u32[]{:S(2)}, u32[]{:S(2)}) %collective-permute-start.4) | collective-permute-done | bytes 327712 | tf_op jit(solution)/shard_map/ppermute | solution.py:216
  150.4 7.8 %collective-permute-done.5 = bf16[128,1280]{1,0:T(8,128)(2,1)S(1)} collective-permute-done((bf16[128,1280]{1,0:T(8,128)(2,1)S(1)}, bf16[128,1280]{1,0:T(8,128)(2,1)S(1)}, u32[]{:S(2)}, u32[]{:S(2)}) %collective-permute-start.5) | collective-permute-done | bytes 327712 | tf_op jit(solution)/shard_map/ppermute | solution.py:216
  158.2 1.6 fusion.1
  159.8 6.4 %all-to-all-start.2 = ((bf16[64,8,1280]{2,1,0:T(8,128)(2,1)}), bf16[64,8,1280]{2,1,0:T(8,128)(2,1)S(1)}, u32[]{:S(2)}, u32[]{:S(2)}) async-start(bf16[64,8,1280]{2,1,0:T(8,128)(2,1)} %fusion.1), calls=%async_computation.2 | async-start | bytes 2621440 | tf_op jit(solution)/shard_map/all_to_all | solution.py:283
  166.3 34.1 %all-to-all-done.2 = bf16[64,8,1280]{2,1,0:T(8,128)(2,1)S(1)} async-done(((bf16[64,8,1280]{2,1,0:T(8,128)(2,1)}), bf16[64,8,1280]{2,1,0:T(8,128)(2,1)S(1)}, u32[]{:S(2)}, u32[]{:S(2)}) %all-to-all-start.2) | async-done | bytes 1310752 | tf_op jit(solution)/shard_map/all_to_all | solution.py:283
  200.4 2.0 convolution_convert_fusion
  (40 shorter events, 0.9 us)
Async XLA Ops:
  0.0 18.7 %copy-start.2 = (bf16[512,320]{0,1:T(8,128)(2,1)S(1)}, bf16[512,320]{0,1:T(8,128)(2,1)}, u32[]{:S(2)}) copy-start(bf16[512,320]{0,1:T(8,128)(2,1)} %param.13) | copy-start | bytes 983044
  1.3 56.3 %all-to-all-start = ((s32[64,1,128]{2,1,0:T(1,128)}), s32[64,1,128]{2,1,0:T(1,128)S(1)}, u32[]{:S(2)}, u32[]{:S(2)}) async-start(s32[64,1,128]{2,1,0:T(1,128)} %broadcast_in_dim.44), calls=%async_computation | async-start | bytes 65536 | tf_op jit(solution)/shard_map/all_to_all | solution.py:251
  14.5 4.5 %copy-start.3 = (bf16[512,320]{0,1:T(8,128)(2,1)S(1)}, bf16[512,320]{0,1:T(8,128)(2,1)}, u32[]{:S(2)}) copy-start(bf16[512,320]{0,1:T(8,128)(2,1)} %param.14) | copy-start | bytes 983044
  19.0 1.8 copy-start.4
  64.3 44.5 %all-to-all-start.1 = ((bf16[64,8,1280]{2,1,0:T(8,128)(2,1)}), bf16[64,8,1280]{2,1,0:T(8,128)(2,1)S(1)}, u32[]{:S(2)}, u32[]{:S(2)}) async-start(bf16[64,8,1280]{2,1,0:T(8,128)(2,1)} %fusion), calls=%async_computation.1 | async-start | bytes 2621440 | tf_op jit(solution)/shard_map/all_to_all | solution.py:270
  74.6 34.6 %copy-start.5 = (f32[1280]{0:T(1024)S(1)}, f32[1280]{0:T(1024)}, u32[]{:S(2)}) copy-start(f32[1280]{0:T(1024)} %param.18) | copy-start | bytes 15364
  109.3 4.9 %copy-start.1 = (bf16[128,1280]{1,0:T(8,128)(2,1)}, bf16[128,1280]{1,0:T(8,128)(2,1)S(1)}, u32[]{:S(2)}) copy-start(bf16[128,1280]{1,0:T(8,128)(2,1)S(1)} %multiply_convert_fusion.x_ref) | copy-start | bytes 983044
  109.4 10.8 %collective-permute-start = (bf16[128,1280]{1,0:T(8,128)(2,1)S(1)}, bf16[128,1280]{1,0:T(8,128)(2,1)S(1)}, u32[]{:S(2)}, u32[]{:S(2)}) collective-permute-start(bf16[128,1280]{1,0:T(8,128)(2,1)S(1)} %multiply_convert_fusion.x_ref), channel_id=1, source_target_pairs={{0,1},{1,2},{2,3},{3,0},{4,5},{5,6},{6,7},{7,4},{8,9},{9,10},{10,1... | collective-permute-start | bytes 983048 | tf_op jit(solution)/shard_map/ppermute | solution.py:207
  110.7 17.5 %collective-permute-start.1 = (bf16[128,1280]{1,0:T(8,128)(2,1)S(1)}, bf16[128,1280]{1,0:T(8,128)(2,1)S(1)}, u32[]{:S(2)}, u32[]{:S(2)}) collective-permute-start(bf16[128,1280]{1,0:T(8,128)(2,1)S(1)} %multiply_convert_fusion.x_ref), channel_id=1, source_target_pairs={{0,2},{1,3},{2,0},{3,1},{4,6},{5,7},{6,4},{7,5},{8,10},{9,11},{10,... | collective-permute-start | bytes 983048 | tf_op jit(solution)/shard_map/ppermute | solution.py:207
  113.1 15.0 %collective-permute-start.2 = (bf16[128,1280]{1,0:T(8,128)(2,1)S(1)}, bf16[128,1280]{1,0:T(8,128)(2,1)S(1)}, u32[]{:S(2)}, u32[]{:S(2)}) collective-permute-start(bf16[128,1280]{1,0:T(8,128)(2,1)S(1)} %multiply_convert_fusion.x_ref), channel_id=1, source_target_pairs={{0,3},{1,0},{2,1},{3,2},{4,7},{5,4},{6,5},{7,6},{8,11},{9,8},{10,9... | collective-permute-start | bytes 983048 | tf_op jit(solution)/shard_map/ppermute | solution.py:207
  136.7 21.4 %copy-start = (bf16[128,1280]{1,0:T(8,128)(2,1)S(1)}, bf16[128,1280]{1,0:T(8,128)(2,1)}, u32[]{:S(2)}) copy-start(bf16[128,1280]{1,0:T(8,128)(2,1)} %shard_map.110) | copy-start | bytes 983044
  138.0 9.5 %collective-permute-start.3 = (bf16[128,1280]{1,0:T(8,128)(2,1)S(1)}, bf16[128,1280]{1,0:T(8,128)(2,1)S(1)}, u32[]{:S(2)}, u32[]{:S(2)}) collective-permute-start(bf16[128,1280]{1,0:T(8,128)(2,1)S(1)} %get-tuple-element.19), channel_id=1, source_target_pairs={{0,3},{1,0},{2,1},{3,2},{4,7},{5,4},{6,5},{7,6},{8,11},{9,8},{10,9... | collective-permute-start | bytes 983048 | tf_op jit(solution)/shard_map/ppermute | solution.py:216
  140.3 10.1 %collective-permute-start.4 = (bf16[128,1280]{1,0:T(8,128)(2,1)S(1)}, bf16[128,1280]{1,0:T(8,128)(2,1)S(1)}, u32[]{:S(2)}, u32[]{:S(2)}) collective-permute-start(bf16[128,1280]{1,0:T(8,128)(2,1)S(1)} %get-tuple-element.21), channel_id=1, source_target_pairs={{0,2},{1,3},{2,0},{3,1},{4,6},{5,7},{6,4},{7,5},{8,10},{9,11},{10,... | collective-permute-start | bytes 983048 | tf_op jit(solution)/shard_map/ppermute | solution.py:216
  140.4 17.7 %collective-permute-start.5 = (bf16[128,1280]{1,0:T(8,128)(2,1)S(1)}, bf16[128,1280]{1,0:T(8,128)(2,1)S(1)}, u32[]{:S(2)}, u32[]{:S(2)}) collective-permute-start(bf16[128,1280]{1,0:T(8,128)(2,1)S(1)} %get-tuple-element.20), channel_id=1, source_target_pairs={{0,1},{1,2},{2,3},{3,0},{4,5},{5,6},{6,7},{7,4},{8,9},{9,10},{10,1... | collective-permute-start | bytes 983048 | tf_op jit(solution)/shard_map/ppermute | solution.py:216
  159.8 40.6 %all-to-all-start.2 = ((bf16[64,8,1280]{2,1,0:T(8,128)(2,1)}), bf16[64,8,1280]{2,1,0:T(8,128)(2,1)S(1)}, u32[]{:S(2)}, u32[]{:S(2)}) async-start(bf16[64,8,1280]{2,1,0:T(8,128)(2,1)} %fusion.1), calls=%async_computation.2 | async-start | bytes 2621440 | tf_op jit(solution)/shard_map/all_to_all | solution.py:283

commit v12 on v10

--- a/solution.py
+++ b/solution.py
@@ -38,7 +38,7 @@
     return turn.astype(jnp.bfloat16)
 
 
-def attention_kernel(q_ref, k_ref, v_ref, cos_ref, sin_ref, turn_ref, segc_ref, segr_ref, posr_ref, w_ref, h_ref, out_ref, bias_ref, ctx_ref):
+def attention_kernel(q_ref, k_ref, v_ref, cos_ref, sin_ref, segc_ref, segr_ref, posr_ref, w_ref, h_ref, out_ref, bias_ref, ctx_ref):
     slots = q_ref.shape[0]
     block = LANES
 
@@ -52,7 +52,12 @@
 
     cosine = cos_ref[...]
     sine = sin_ref[...]
-    turn = turn_ref[...]
+    src = lax.broadcasted_iota(jnp.int32, (LANES, LANES), 0)
+    dst = lax.broadcasted_iota(jnp.int32, (LANES, LANES), 1)
+    first = dst % HEAD_SIZE < HEAD_SIZE // 2
+    turn = jnp.where(
+        first & (src == dst + HEAD_SIZE // 2), -1.0, jnp.where(~first & (src == dst - HEAD_SIZE // 2), 1.0, 0.0)
+    ).astype(jnp.bfloat16)
 
     def rotate(x):
         turned = jnp.dot(x, turn, preferred_element_type=jnp.float32)
@@ -102,7 +107,6 @@
     starts = lax.cummax(jnp.where(begins, slots, 0), axis=0)
     token_position = slots - starts
     cosine, sine = rotation_tables(token_position)
-    turn = half_turn_matrix()
     def doubled(x):
         x = x.reshape(slot_capacity, KEY_VALUE_HEADS, 1, HEAD_SIZE)
         x = jnp.broadcast_to(x, (slot_capacity, KEY_VALUE_HEADS, 2, HEAD_SIZE))
@@ -122,7 +126,6 @@
             pl.BlockSpec((slot_capacity, LANES), lambda t: (0, t // per_kv)),
             pl.BlockSpec((slot_capacity, LANES), full),
             pl.BlockSpec((slot_capacity, LANES), full),
-            pl.BlockSpec((LANES, LANES), full),
             pl.BlockSpec((slot_capacity, 1), full),
             pl.BlockSpec((1, slot_capacity), full),
             pl.BlockSpec((1, slot_capacity), full),
@@ -137,7 +140,7 @@
         ],
         compiler_params=pltpu.CompilerParams(dimension_semantics=("arbitrary",)),
     )(
-        queries, keys2, values2, cosine, sine, turn,
+        queries, keys2, values2, cosine, sine,
         segment.reshape(slot_capacity, 1), segment.reshape(1, slot_capacity),
         token_position.reshape(1, slot_capacity), out_weight, hidden_in,
     )
@@ -156,45 +159,34 @@
     ).astype(jnp.bfloat16)
 
 
-def ffn_kernel(x_ref, g_ref, u_ref, d_ref, o_ref, acc_ref):
-    step = pl.program_id(0)
-
-    @pl.when(step == 0)
-    def _():
-        acc_ref[...] = jnp.zeros_like(acc_ref)
-
-    x = x_ref[...]
+def ffn_kernel(*refs):
+    *x_refs, g_ref, u_ref, d_ref, o_ref = refs
+    x = jnp.concatenate([r[...] for r in x_refs], axis=0) if len(x_refs) > 1 else x_refs[0][...]
     gate = jnp.dot(x, g_ref[...], preferred_element_type=jnp.float32)
     upward = jnp.dot(x, u_ref[...], preferred_element_type=jnp.float32)
     hidden = (gate / (1.0 + jnp.exp(-gate)) * upward).astype(jnp.bfloat16)
-    acc_ref[...] += jnp.dot(hidden, d_ref[...], preferred_element_type=jnp.float32)
-
-    @pl.when(step == pl.num_programs(0) - 1)
-    def _():
-        o_ref[...] = acc_ref[...].astype(o_ref.dtype)
-
-
-def ffn_rows(rows, gate_weight, up_weight, down_weight):
-    count, width = rows.shape
+    o_ref[...] = jnp.dot(hidden, d_ref[...], preferred_element_type=jnp.float32).astype(o_ref.dtype)
+
+
+def ffn_rows(blocks, gate_weight, up_weight, down_weight):
+    width = blocks[0].shape[1]
+    count = sum(b.shape[0] for b in blocks)
     units = gate_weight.shape[1]
-    chunk = units
     flops = 6 * count * width * units
     moved = 2 * (3 * width * units + 2 * count * width)
     return pl.pallas_call(
         ffn_kernel,
-        grid=(units // chunk,),
-        in_specs=[
-            pl.BlockSpec((count, width), lambda j: (0, 0)),
-            pl.BlockSpec((width, chunk), lambda j: (0, j)),
-            pl.BlockSpec((width, chunk), lambda j: (0, j)),
-            pl.BlockSpec((chunk, width), lambda j: (j, 0)),
+        grid=(1,),
+        in_specs=[pl.BlockSpec(b.shape, lambda j: (0, 0)) for b in blocks] + [
+            pl.BlockSpec((width, units), lambda j: (0, 0)),
+            pl.BlockSpec((width, units), lambda j: (0, 0)),
+            pl.BlockSpec((units, width), lambda j: (0, 0)),
         ],
         out_specs=pl.BlockSpec((count, width), lambda j: (0, 0)),
         out_shape=jax.ShapeDtypeStruct((count, width), jnp.bfloat16),
-        scratch_shapes=[pltpu.VMEM((count, width), jnp.float32)],
         compiler_params=pltpu.CompilerParams(dimension_semantics=("arbitrary",)),
         cost_estimate=pl.CostEstimate(flops=flops, transcendentals=count * units, bytes_accessed=moved),
-    )(rows, gate_weight, up_weight, down_weight)
+    )(*blocks, gate_weight, up_weight, down_weight)
 
 
 def feed_forward(normed, gate_weight, up_weight, down_weight):
@@ -204,9 +196,9 @@
         lax.ppermute(normed, "grp", [(j, (j + k) % groups) for j in range(groups)])
         for k in range(1, groups)
     ]
-    own = ffn_rows(normed, gate_weight, up_weight, down_weight)
+    own = ffn_rows([normed], gate_weight, up_weight, down_weight)
     own, *arrived = lax.optimization_barrier((own, *arrived))
-    others = ffn_rows(jnp.concatenate(arrived, axis=0), gate_weight, up_weight, down_weight)
+    others = ffn_rows(arrived, gate_weight, up_weight, down_weight)
     total = own.astype(jnp.float32)
     for k in range(1, groups):
         part = others[(k - 1) * rows:k * rows]

time: 199 us -> 199 us (level)
  transfers between devices with their start and end apart: 9 -> 9, of which waited for: 6 -> 7; matrix products, arithmetic and copies ran while one was open for 4% -> 4% of each run, Pallas kernels for 19% -> 19%
where the time goes in v12:
time: 199 us
  waiting for transfers between devices  90.3 us (45%)
  Pallas kernels  45.9 us (23%)
  starting transfers between devices  39.3 us (20%)
  local copies, waits for them, and re-layouts  9.8 us (5%)
  matrix products  7.41 us (4%)
  other arithmetic  3.02 us (2%)
  between operations  2.99 us (2%)
    all_to_all x1, waiting for transfers between devices, on_device(): lax.all_to_all(outgoing.reshape(request_owners, block_rows, -1), 'req', 0...  34.1 us
    all_to_all x1, waiting for transfers between devices, on_device(): lax.all_to_all(outbound.reshape(request_owners, block_rows, -1), 'req', 0...  33.9 us
    pallas_call x1, Pallas kernels, attend(): pl.pallas_call(attention_kernel, grid=(tiles,), in_specs=[pl.BlockSpec((s...  33.1 us
    ppermute x3, waiting for transfers between devices, feed_forward(): lax.ppermute(part, 'grp', [(j, (j - k) % groups) for j in range(groups)])  13.6 us
    all_to_all x1, starting transfers between devices, on_device(): lax.all_to_all(jnp.broadcast_to(live_rows.reshape(1, 1), (request_owners,...  13.1 us
    pallas_call x2, Pallas kernels, ffn_rows(): pl.pallas_call(ffn_kernel, grid=(1,), in_specs=[pl.BlockSpec(b.shape, lam...  12.8 us
    all_to_all x1, starting transfers between devices, on_device(): lax.all_to_all(outbound.reshape(request_owners, block_rows, -1), 'req', 0...  10.3 us
    ppermute x3, waiting for transfers between devices, feed_forward(): lax.ppermute(normed, 'grp', [(j, (j + k) % groups) for j in range(groups)])  8.66 us
  transfers between devices with their start and end apart: 9, of which 7 were waited for; matrix products, arithmetic and copies ran while one was open for 4% of the time, Pallas kernels for 19%

profile of v12, /device:TPU:1, one launch (start us, length us, event | category | flops | bytes accessed | tf_op | source)
XLA Modules:
  0.0 198.7 jit_solution(7378693987295122603)
XLA Ops:
  0.7 0.6 broadcast_in_dim.32
  1.3 13.1 %all-to-all-start = ((s32[64,1,128]{2,1,0:T(1,128)}), s32[64,1,128]{2,1,0:T(1,128)S(1)}, u32[]{:S(2)}, u32[]{:S(2)}) async-start(s32[64,1,128]{2,1,0:T(1,128)} %broadcast_in_dim.32), calls=%async_computation | async-start | bytes 65536 | tf_op jit(solution)/shard_map/all_to_all | solution.py:240
  14.5 1.0 broadcast_in_dim.37
  15.5 1.1 copy.31.k_ref
  16.7 1.1 copy.32.v_ref
  17.8 0.1 compare_reduce_fusion
  17.9 0.3 reduce-window.19
  18.4 0.1 slice_reduce_fusion
  18.6 0.3 multiply_sine_fusion
  18.9 0.9 copy.33.cos_ref
  19.8 0.8 copy.34.sin_ref
  20.6 0.9 copy.35.segc_ref
  21.5 0.6 iota_subtract_fusion.posr_ref
  22.1 33.1 %shard_map.109 = bf16[512,1280]{1,0:T(8,128)(2,1)} custom-call(bf16[512,1280]{1,0:T(8,128)(2,1)} %q_ref.1, bf16[512,640]{1,0:T(8,128)(2,1)} %copy.31.k_ref, bf16[512,640]{1,0:T(8,128)(2,1)} %copy.32.v_ref, f32[512,128]{1,0:T(8,128)} %copy.33.cos_ref, f32[512,128]{1,0:T(8,128)} %copy.34.sin_ref, s32[512,1]{1,0:T(8,128)} %copy.35.segc_ref, s32[1,512]{1,0:T(1,128)} %bitcast.41, ...), custom_call_target="tpu_custom_call" | custom-call | tf_op jit(solution)/shard_map/pallas_call | solution.py:120
  55.2 0.1 slice_reduce_fusion.1
  55.3 0.1 reduce-window.18
  55.4 0.1 reduce
  55.6 0.7 fusion.34
  58.4 0.1 add_add_fusion
  58.5 0.1 add.226
  58.6 3.3 %fusion = bf16[64,8,1280]{2,1,0:T(8,128)(2,1)} fusion(bf16[512,1280]{1,0:T(8,128)(2,1)} %shard_map.109, s32[512]{0:T(512)S(1)} %add.226, pred[512]{0:T(512)(128)(4,1)S(1)} %broadcast_compare_fusion), kind=kOutput, calls=%fused_computation.3 | convolution fusion | flops 672268288 | bytes 2624000 | tf_op jit(solution)/shard_map/dot_general | solution.py:213
  61.9 10.3 %all-to-all-start.1 = ((bf16[64,8,1280]{2,1,0:T(8,128)(2,1)}), bf16[64,8,1280]{2,1,0:T(8,128)(2,1)S(1)}, u32[]{:S(2)}, u32[]{:S(2)}) async-start(bf16[64,8,1280]{2,1,0:T(8,128)(2,1)} %fusion), calls=%async_computation.1 | async-start | bytes 2621440 | tf_op jit(solution)/shard_map/all_to_all | solution.py:259
  72.2 0.1 convert_reduce_fusion
  72.3 0.1 select_reduce_fusion
  72.4 33.9 %all-to-all-done.1 = bf16[64,8,1280]{2,1,0:T(8,128)(2,1)S(1)} async-done(((bf16[64,8,1280]{2,1,0:T(8,128)(2,1)}), bf16[64,8,1280]{2,1,0:T(8,128)(2,1)S(1)}, u32[]{:S(2)}, u32[]{:S(2)}) %all-to-all-start.1) | async-done | bytes 1310752 | tf_op jit(solution)/shard_map/all_to_all | solution.py:259
  106.4 0.5 multiply_reduce_fusion
  106.8 0.1 multiply_convert_fusion.refs_0_
  107.0 1.3 collective-permute-start
  108.2 2.5 %collective-permute-start.1 = (bf16[128,1280]{1,0:T(8,128)(2,1)S(1)}, bf16[128,1280]{1,0:T(8,128)(2,1)S(1)}, u32[]{:S(2)}, u32[]{:S(2)}) collective-permute-start(bf16[128,1280]{1,0:T(8,128)(2,1)S(1)} %multiply_convert_fusion.refs_0_), channel_id=1, source_target_pairs={{0,2},{1,3},{2,0},{3,1},{4,6},{5,7},{6,4},{7,5},{8,10},{9,11},{10,... | collective-permute-start | bytes 983048 | tf_op jit(solution)/shard_map/ppermute | solution.py:196
  110.7 1.2 collective-permute-start.2
  111.9 5.2 %shard_map.110 = bf16[128,1280]{1,0:T(8,128)(2,1)} custom-call(bf16[128,1280]{1,0:T(8,128)(2,1)} %copy-done.1, bf16[1280,896]{1,0:T(8,128)(2,1)} %refs_3_.3, bf16[1280,896]{1,0:T(8,128)(2,1)} %refs_4_.1, bf16[896,1280]{1,0:T(8,128)(2,1)} %refs_5_.1), custom_call_target="tpu_custom_call" | custom-call | flops 880803840 | bytes 7536640 | tf_op jit(solution)/shard_map/pallas_call | solution.py:177
  117.0 0.7 collective-permute-done.refs_0_
  117.7 8.0 %collective-permute-done.1.refs_1_ = bf16[128,1280]{1,0:T(8,128)(2,1)S(1)} collective-permute-done((bf16[128,1280]{1,0:T(8,128)(2,1)S(1)}, bf16[128,1280]{1,0:T(8,128)(2,1)S(1)}, u32[]{:S(2)}, u32[]{:S(2)}) %collective-permute-start.1) | collective-permute-done | bytes 327712 | tf_op jit(solution)/shard_map/ppermute | solution.py:196
  125.7 0.7 copy-done.6
  126.4 0.7 copy-done.7
  127.2 7.6 %shard_map.111 = bf16[384,1280]{1,0:T(8,128)(2,1)} custom-call(bf16[128,1280]{1,0:T(8,128)(2,1)} %copy-done.5, bf16[128,1280]{1,0:T(8,128)(2,1)} %copy-done.6, bf16[128,1280]{1,0:T(8,128)(2,1)} %copy-done.7, bf16[1280,896]{1,0:T(8,128)(2,1)} %refs_3_.3, bf16[1280,896]{1,0:T(8,128)(2,1)} %refs_4_.1, bf16[896,1280]{1,0:T(8,128)(2,1)} %refs_5_.1), custom_call_target="tpu_custom_call" | custom-call | flops 2642411520 | bytes 8847360 | tf_op jit(solution)/shard_map/pallas_call | solution.py:177
  134.8 1.3 fusion.39
  136.2 2.6 %collective-permute-start.4 = (bf16[128,1280]{1,0:T(8,128)(2,1)S(1)}, bf16[128,1280]{1,0:T(8,128)(2,1)S(1)}, u32[]{:S(2)}, u32[]{:S(2)}) collective-permute-start(bf16[128,1280]{1,0:T(8,128)(2,1)S(1)} %get-tuple-element.21), channel_id=1, source_target_pairs={{0,2},{1,3},{2,0},{3,1},{4,6},{5,7},{6,4},{7,5},{8,10},{9,11},{10,... | collective-permute-start | bytes 983048 | tf_op jit(solution)/shard_map/ppermute | solution.py:205
  138.8 0.8 collective-permute-start.3
  139.7 0.1 lt.64
  139.8 0.1 add.219
  139.9 6.0 %collective-permute-done.5 = bf16[128,1280]{1,0:T(8,128)(2,1)S(1)} collective-permute-done((bf16[128,1280]{1,0:T(8,128)(2,1)S(1)}, bf16[128,1280]{1,0:T(8,128)(2,1)S(1)}, u32[]{:S(2)}, u32[]{:S(2)}) %collective-permute-start.5) | collective-permute-done | bytes 327712 | tf_op jit(solution)/shard_map/ppermute | solution.py:205
  146.0 7.2 %collective-permute-done.4 = bf16[128,1280]{1,0:T(8,128)(2,1)S(1)} collective-permute-done((bf16[128,1280]{1,0:T(8,128)(2,1)S(1)}, bf16[128,1280]{1,0:T(8,128)(2,1)S(1)}, u32[]{:S(2)}, u32[]{:S(2)}) %collective-permute-start.4) | collective-permute-done | bytes 327712 | tf_op jit(solution)/shard_map/ppermute | solution.py:205
  153.2 0.4 collective-permute-done.3
  153.6 1.6 fusion.1
  155.2 7.4 %all-to-all-start.2 = ((bf16[64,8,1280]{2,1,0:T(8,128)(2,1)}), bf16[64,8,1280]{2,1,0:T(8,128)(2,1)S(1)}, u32[]{:S(2)}, u32[]{:S(2)}) async-start(bf16[64,8,1280]{2,1,0:T(8,128)(2,1)} %fusion.1), calls=%async_computation.2 | async-start | bytes 2621440 | tf_op jit(solution)/shard_map/all_to_all | solution.py:272
  162.6 34.1 %all-to-all-done.2 = bf16[64,8,1280]{2,1,0:T(8,128)(2,1)S(1)} async-done(((bf16[64,8,1280]{2,1,0:T(8,128)(2,1)}), bf16[64,8,1280]{2,1,0:T(8,128)(2,1)S(1)}, u32[]{:S(2)}, u32[]{:S(2)}) %all-to-all-start.2) | async-done | bytes 1310752 | tf_op jit(solution)/shard_map/all_to_all | solution.py:272
  196.8 2.0 %convolution_convert_fusion = bf16[512,1280]{1,0:T(8,128)(2,1)} fusion(bf16[64,8,1280]{2,1,0:T(8,128)(2,1)S(1)} %all-to-all-done.2, s32[512]{0:T(512)S(1)} %fusion.24, pred[512]{0:T(512)(128)(4,1)S(1)} %broadcast_compare_fusion.1), kind=kOutput, calls=%fused_computation | convolution fusion | flops 672268288 | bytes 2624000 | tf_op jit(solution)/shard_map/dot_general | solution.py:213
  (36 shorter events, 0.7 us)
Async XLA Ops:
  0.0 16.6 %copy-start.2 = (bf16[512,320]{0,1:T(8,128)(2,1)S(1)}, bf16[512,320]{0,1:T(8,128)(2,1)}, u32[]{:S(2)}) copy-start(bf16[512,320]{0,1:T(8,128)(2,1)} %param.14) | copy-start | bytes 983044
  1.3 53.9 %all-to-all-start = ((s32[64,1,128]{2,1,0:T(1,128)}), s32[64,1,128]{2,1,0:T(1,128)S(1)}, u32[]{:S(2)}, u32[]{:S(2)}) async-start(s32[64,1,128]{2,1,0:T(1,128)} %broadcast_in_dim.32), calls=%async_computation | async-start | bytes 65536 | tf_op jit(solution)/shard_map/all_to_all | solution.py:240
  16.6 1.2 copy-start.3
  61.9 44.5 %all-to-all-start.1 = ((bf16[64,8,1280]{2,1,0:T(8,128)(2,1)}), bf16[64,8,1280]{2,1,0:T(8,128)(2,1)S(1)}, u32[]{:S(2)}, u32[]{:S(2)}) async-start(bf16[64,8,1280]{2,1,0:T(8,128)(2,1)} %fusion), calls=%async_computation.1 | async-start | bytes 2621440 | tf_op jit(solution)/shard_map/all_to_all | solution.py:259
  72.2 34.6 %copy-start.4 = (f32[1280]{0:T(1024)S(1)}, f32[1280]{0:T(1024)}, u32[]{:S(2)}) copy-start(f32[1280]{0:T(1024)} %param.18) | copy-start | bytes 15364
  107.0 4.9 %copy-start.1 = (bf16[128,1280]{1,0:T(8,128)(2,1)}, bf16[128,1280]{1,0:T(8,128)(2,1)S(1)}, u32[]{:S(2)}) copy-start(bf16[128,1280]{1,0:T(8,128)(2,1)S(1)} %multiply_convert_fusion.refs_0_) | copy-start | bytes 983044
  107.0 10.7 %collective-permute-start = (bf16[128,1280]{1,0:T(8,128)(2,1)S(1)}, bf16[128,1280]{1,0:T(8,128)(2,1)S(1)}, u32[]{:S(2)}, u32[]{:S(2)}) collective-permute-start(bf16[128,1280]{1,0:T(8,128)(2,1)S(1)} %multiply_convert_fusion.refs_0_), channel_id=1, source_target_pairs={{0,1},{1,2},{2,3},{3,0},{4,5},{5,6},{6,7},{7,4},{8,9},{9,10},{10,1... | collective-permute-start | bytes 983048 | tf_op jit(solution)/shard_map/ppermute | solution.py:196
  108.2 17.5 %collective-permute-start.1 = (bf16[128,1280]{1,0:T(8,128)(2,1)S(1)}, bf16[128,1280]{1,0:T(8,128)(2,1)S(1)}, u32[]{:S(2)}, u32[]{:S(2)}) collective-permute-start(bf16[128,1280]{1,0:T(8,128)(2,1)S(1)} %multiply_convert_fusion.refs_0_), channel_id=1, source_target_pairs={{0,2},{1,3},{2,0},{3,1},{4,6},{5,7},{6,4},{7,5},{8,10},{9,11},{10,... | collective-permute-start | bytes 983048 | tf_op jit(solution)/shard_map/ppermute | solution.py:196
  110.7 15.0 %collective-permute-start.2 = (bf16[128,1280]{1,0:T(8,128)(2,1)S(1)}, bf16[128,1280]{1,0:T(8,128)(2,1)S(1)}, u32[]{:S(2)}, u32[]{:S(2)}) collective-permute-start(bf16[128,1280]{1,0:T(8,128)(2,1)S(1)} %multiply_convert_fusion.refs_0_), channel_id=1, source_target_pairs={{0,3},{1,0},{2,1},{3,2},{4,7},{5,4},{6,5},{7,6},{8,11},{9,8},{10,9... | collective-permute-start | bytes 983048 | tf_op jit(solution)/shard_map/ppermute | solution.py:196
  117.7 8.0 %copy-start.5 = (bf16[128,1280]{1,0:T(8,128)(2,1)}, bf16[128,1280]{1,0:T(8,128)(2,1)S(1)}, u32[]{:S(2)}) copy-start(bf16[128,1280]{1,0:T(8,128)(2,1)S(1)} %collective-permute-done.refs_0_) | copy-start | bytes 983044
  125.7 0.7 copy-start.6
  126.4 0.7 copy-start.7
  134.8 18.8 %copy-start = (bf16[128,1280]{1,0:T(8,128)(2,1)S(1)}, bf16[128,1280]{1,0:T(8,128)(2,1)}, u32[]{:S(2)}) copy-start(bf16[128,1280]{1,0:T(8,128)(2,1)} %shard_map.110) | copy-start | bytes 983044
  136.1 9.9 %collective-permute-start.5 = (bf16[128,1280]{1,0:T(8,128)(2,1)S(1)}, bf16[128,1280]{1,0:T(8,128)(2,1)S(1)}, u32[]{:S(2)}, u32[]{:S(2)}) collective-permute-start(bf16[128,1280]{1,0:T(8,128)(2,1)S(1)} %get-tuple-element.20), channel_id=1, source_target_pairs={{0,1},{1,2},{2,3},{3,0},{4,5},{5,6},{6,7},{7,4},{8,9},{9,10},{10,1... | collective-permute-start | bytes 983048 | tf_op jit(solution)/shard_map/ppermute | solution.py:205
  136.2 17.0 %collective-permute-start.4 = (bf16[128,1280]{1,0:T(8,128)(2,1)S(1)}, bf16[128,1280]{1,0:T(8,128)(2,1)S(1)}, u32[]{:S(2)}, u32[]{:S(2)}) collective-permute-start(bf16[128,1280]{1,0:T(8,128)(2,1)S(1)} %get-tuple-element.21), channel_id=1, source_target_pairs={{0,2},{1,3},{2,0},{3,1},{4,6},{5,7},{6,4},{7,5},{8,10},{9,11},{10,... | collective-permute-start | bytes 983048 | tf_op jit(solution)/shard_map/ppermute | solution.py:205
  138.8 14.8 %collective-permute-start.3 = (bf16[128,1280]{1,0:T(8,128)(2,1)S(1)}, bf16[128,1280]{1,0:T(8,128)(2,1)S(1)}, u32[]{:S(2)}, u32[]{:S(2)}) collective-permute-start(bf16[128,1280]{1,0:T(8,128)(2,1)S(1)} %get-tuple-element.19), channel_id=1, source_target_pairs={{0,3},{1,0},{2,1},{3,2},{4,7},{5,4},{6,5},{7,6},{8,11},{9,8},{10,9... | collective-permute-start | bytes 983048 | tf_op jit(solution)/shard_map/ppermute | solution.py:205
  155.2 41.5 %all-to-all-start.2 = ((bf16[64,8,1280]{2,1,0:T(8,128)(2,1)}), bf16[64,8,1280]{2,1,0:T(8,128)(2,1)S(1)}, u32[]{:S(2)}, u32[]{:S(2)}) async-start(bf16[64,8,1280]{2,1,0:T(8,128)(2,1)} %fusion.1), calls=%async_computation.2 | async-start | bytes 2621440 | tf_op jit(solution)/shard_map/all_to_all | solution.py:272

commit v13 on v12

--- a/solution.py
+++ b/solution.py
@@ -23,9 +23,9 @@
 def rotation_tables(token_position):
     half = HEAD_SIZE // 2
     inverse = rope_base ** (-(2.0 * jnp.arange(half, dtype=jnp.float32)) / HEAD_SIZE)
+    inverse = jnp.tile(inverse, LANES // half)
     angle = token_position.astype(jnp.float32)[:, None] * inverse[None, :]
-    reps = LANES // half
-    return jnp.tile(jnp.cos(angle), (1, reps)), jnp.tile(jnp.sin(angle), (1, reps))
+    return jnp.cos(angle), jnp.sin(angle)
 
 
 def half_turn_matrix():

time: 199 us -> 199 us (level)
  no operation moved by 1% of the time
where the time goes in v13:
time: 199 us
  waiting for transfers between devices  90.4 us (45%)
  Pallas kernels  45.9 us (23%)
  starting transfers between devices  39.2 us (20%)
  local copies, waits for them, and re-layouts  8.16 us (4%)
  matrix products  7.42 us (4%)
  other arithmetic  4.52 us (2%)
  between operations  2.97 us (1%)
    all_to_all x1, waiting for transfers between devices, on_device(): lax.all_to_all(outgoing.reshape(request_owners, block_rows, -1), 'req', 0...  34.1 us
    all_to_all x1, waiting for transfers between devices, on_device(): lax.all_to_all(outbound.reshape(request_owners, block_rows, -1), 'req', 0...  33.9 us
    pallas_call x1, Pallas kernels, attend(): pl.pallas_call(attention_kernel, grid=(tiles,), in_specs=[pl.BlockSpec((s...  33.1 us
    ppermute x3, waiting for transfers between devices, feed_forward(): lax.ppermute(part, 'grp', [(j, (j - k) % groups) for j in range(groups)])  13.7 us
    all_to_all x1, starting transfers between devices, on_device(): lax.all_to_all(jnp.broadcast_to(live_rows.reshape(1, 1), (request_owners,...  13.1 us
    pallas_call x2, Pallas kernels, ffn_rows(): pl.pallas_call(ffn_kernel, grid=(1,), in_specs=[pl.BlockSpec(b.shape, lam...  12.8 us
    all_to_all x1, starting transfers between devices, on_device(): lax.all_to_all(outbound.reshape(request_owners, block_rows, -1), 'req', 0...  10.3 us
    ppermute x3, waiting for transfers between devices, feed_forward(): lax.ppermute(normed, 'grp', [(j, (j + k) % groups) for j in range(groups)])  8.71 us
  transfers between devices with their start and end apart: 9, of which 7 were waited for; matrix products, arithmetic and copies ran while one was open for 4% of the time, Pallas kernels for 19%

profile of v13, /device:TPU:1, one launch (start us, length us, event | category | flops | bytes accessed | tf_op | source)
XLA Modules:
  0.0 198.6 jit_solution(8440258925520042177)
XLA Ops:
  0.7 0.6 broadcast_in_dim.32
  1.3 13.1 %all-to-all-start = ((s32[64,1,128]{2,1,0:T(1,128)}), s32[64,1,128]{2,1,0:T(1,128)S(1)}, u32[]{:S(2)}, u32[]{:S(2)}) async-start(s32[64,1,128]{2,1,0:T(1,128)} %broadcast_in_dim.32), calls=%async_computation | async-start | bytes 65536 | tf_op jit(solution)/shard_map/all_to_all | solution.py:240
  14.5 1.0 broadcast_in_dim.37
  15.5 1.1 copy.25.k_ref
  16.7 1.1 copy.26.v_ref
  17.8 0.1 mul.112
  17.9 0.1 compare_reduce_fusion
  18.0 0.3 reduce-window.19
  18.4 0.1 slice_reduce_fusion
  18.6 0.9 copy.27.segc_ref
  19.5 0.6 iota_subtract_fusion.posr_ref
  20.1 1.8 multiply_sine_fusion
  21.9 33.1 %shard_map.109 = bf16[512,1280]{1,0:T(8,128)(2,1)} custom-call(bf16[512,1280]{1,0:T(8,128)(2,1)} %q_ref.1, bf16[512,640]{1,0:T(8,128)(2,1)} %copy.25.k_ref, bf16[512,640]{1,0:T(8,128)(2,1)} %copy.26.v_ref, f32[512,128]{1,0:T(8,128)} %get-tuple-element.25.cos_ref, f32[512,128]{1,0:T(8,128)} %get-tuple-element.24.sin_ref, s32[512,1]{1,0:T(8,128)} %copy.27.segc_ref, ...), custom_call_target="tpu_custom_call" | custom-call | tf_op jit(solution)/shard_map/pallas_call | solution.py:120
  55.0 0.1 slice_reduce_fusion.1
  55.1 0.1 reduce-window.18
  55.2 0.1 reduce
  55.4 0.7 fusion.34
  58.2 0.1 add_add_fusion
  58.3 0.1 add.226
  58.4 3.3 %fusion = bf16[64,8,1280]{2,1,0:T(8,128)(2,1)} fusion(bf16[512,1280]{1,0:T(8,128)(2,1)} %shard_map.109, s32[512]{0:T(512)S(1)} %add.226, pred[512]{0:T(512)(128)(4,1)S(1)} %broadcast_compare_fusion), kind=kOutput, calls=%fused_computation.3 | convolution fusion | flops 672268288 | bytes 2624000 | tf_op jit(solution)/shard_map/dot_general | solution.py:213
  61.7 10.3 %all-to-all-start.1 = ((bf16[64,8,1280]{2,1,0:T(8,128)(2,1)}), bf16[64,8,1280]{2,1,0:T(8,128)(2,1)S(1)}, u32[]{:S(2)}, u32[]{:S(2)}) async-start(bf16[64,8,1280]{2,1,0:T(8,128)(2,1)} %fusion), calls=%async_computation.1 | async-start | bytes 2621440 | tf_op jit(solution)/shard_map/all_to_all | solution.py:259
  72.0 0.1 convert_reduce_fusion
  72.1 0.1 select_reduce_fusion
  72.3 33.9 %all-to-all-done.1 = bf16[64,8,1280]{2,1,0:T(8,128)(2,1)S(1)} async-done(((bf16[64,8,1280]{2,1,0:T(8,128)(2,1)}), bf16[64,8,1280]{2,1,0:T(8,128)(2,1)S(1)}, u32[]{:S(2)}, u32[]{:S(2)}) %all-to-all-start.1) | async-done | bytes 1310752 | tf_op jit(solution)/shard_map/all_to_all | solution.py:259
  106.2 0.5 multiply_reduce_fusion
  106.6 0.1 multiply_convert_fusion.refs_0_
  106.8 1.3 collective-permute-start
  108.1 2.4 %collective-permute-start.1 = (bf16[128,1280]{1,0:T(8,128)(2,1)S(1)}, bf16[128,1280]{1,0:T(8,128)(2,1)S(1)}, u32[]{:S(2)}, u32[]{:S(2)}) collective-permute-start(bf16[128,1280]{1,0:T(8,128)(2,1)S(1)} %multiply_convert_fusion.refs_0_), channel_id=1, source_target_pairs={{0,2},{1,3},{2,0},{3,1},{4,6},{5,7},{6,4},{7,5},{8,10},{9,11},{10,... | collective-permute-start | bytes 983048 | tf_op jit(solution)/shard_map/ppermute | solution.py:196
  110.6 1.1 collective-permute-start.2
  111.7 5.2 %shard_map.110 = bf16[128,1280]{1,0:T(8,128)(2,1)} custom-call(bf16[128,1280]{1,0:T(8,128)(2,1)} %copy-done.1, bf16[1280,896]{1,0:T(8,128)(2,1)} %refs_3_.3, bf16[1280,896]{1,0:T(8,128)(2,1)} %refs_4_.1, bf16[896,1280]{1,0:T(8,128)(2,1)} %refs_5_.1), custom_call_target="tpu_custom_call" | custom-call | flops 880803840 | bytes 7536640 | tf_op jit(solution)/shard_map/pallas_call | solution.py:177
  116.9 0.7 collective-permute-done.refs_0_
  117.5 8.0 %collective-permute-done.1.refs_1_ = bf16[128,1280]{1,0:T(8,128)(2,1)S(1)} collective-permute-done((bf16[128,1280]{1,0:T(8,128)(2,1)S(1)}, bf16[128,1280]{1,0:T(8,128)(2,1)S(1)}, u32[]{:S(2)}, u32[]{:S(2)}) %collective-permute-start.1) | collective-permute-done | bytes 327712 | tf_op jit(solution)/shard_map/ppermute | solution.py:196
  125.6 0.7 copy-done.6
  126.3 0.7 copy-done.7
  127.0 7.6 %shard_map.111 = bf16[384,1280]{1,0:T(8,128)(2,1)} custom-call(bf16[128,1280]{1,0:T(8,128)(2,1)} %copy-done.5, bf16[128,1280]{1,0:T(8,128)(2,1)} %copy-done.6, bf16[128,1280]{1,0:T(8,128)(2,1)} %copy-done.7, bf16[1280,896]{1,0:T(8,128)(2,1)} %refs_3_.3, bf16[1280,896]{1,0:T(8,128)(2,1)} %refs_4_.1, bf16[896,1280]{1,0:T(8,128)(2,1)} %refs_5_.1), custom_call_target="tpu_custom_call" | custom-call | flops 2642411520 | bytes 8847360 | tf_op jit(solution)/shard_map/pallas_call | solution.py:177
  134.7 1.3 fusion.39
  135.9 0.1 collective-permute-start.5
  136.0 2.6 %collective-permute-start.4 = (bf16[128,1280]{1,0:T(8,128)(2,1)S(1)}, bf16[128,1280]{1,0:T(8,128)(2,1)S(1)}, u32[]{:S(2)}, u32[]{:S(2)}) collective-permute-start(bf16[128,1280]{1,0:T(8,128)(2,1)S(1)} %get-tuple-element.21), channel_id=1, source_target_pairs={{0,2},{1,3},{2,0},{3,1},{4,6},{5,7},{6,4},{7,5},{8,10},{9,11},{10,... | collective-permute-start | bytes 983048 | tf_op jit(solution)/shard_map/ppermute | solution.py:205
  138.6 0.8 collective-permute-start.3
  139.5 0.1 lt.64
  139.6 0.1 add.219
  139.8 6.1 %collective-permute-done.5 = bf16[128,1280]{1,0:T(8,128)(2,1)S(1)} collective-permute-done((bf16[128,1280]{1,0:T(8,128)(2,1)S(1)}, bf16[128,1280]{1,0:T(8,128)(2,1)S(1)}, u32[]{:S(2)}, u32[]{:S(2)}) %collective-permute-start.5) | collective-permute-done | bytes 327712 | tf_op jit(solution)/shard_map/ppermute | solution.py:205
  145.8 7.2 %collective-permute-done.4 = bf16[128,1280]{1,0:T(8,128)(2,1)S(1)} collective-permute-done((bf16[128,1280]{1,0:T(8,128)(2,1)S(1)}, bf16[128,1280]{1,0:T(8,128)(2,1)S(1)}, u32[]{:S(2)}, u32[]{:S(2)}) %collective-permute-start.4) | collective-permute-done | bytes 327712 | tf_op jit(solution)/shard_map/ppermute | solution.py:205
  153.0 0.4 collective-permute-done.3
  153.4 1.6 fusion.1
  155.1 7.4 %all-to-all-start.2 = ((bf16[64,8,1280]{2,1,0:T(8,128)(2,1)}), bf16[64,8,1280]{2,1,0:T(8,128)(2,1)S(1)}, u32[]{:S(2)}, u32[]{:S(2)}) async-start(bf16[64,8,1280]{2,1,0:T(8,128)(2,1)} %fusion.1), calls=%async_computation.2 | async-start | bytes 2621440 | tf_op jit(solution)/shard_map/all_to_all | solution.py:272
  162.5 34.1 %all-to-all-done.2 = bf16[64,8,1280]{2,1,0:T(8,128)(2,1)S(1)} async-done(((bf16[64,8,1280]{2,1,0:T(8,128)(2,1)}), bf16[64,8,1280]{2,1,0:T(8,128)(2,1)S(1)}, u32[]{:S(2)}, u32[]{:S(2)}) %all-to-all-start.2) | async-done | bytes 1310752 | tf_op jit(solution)/shard_map/all_to_all | solution.py:272
  196.6 2.0 %convolution_convert_fusion = bf16[512,1280]{1,0:T(8,128)(2,1)} fusion(bf16[64,8,1280]{2,1,0:T(8,128)(2,1)S(1)} %all-to-all-done.2, s32[512]{0:T(512)S(1)} %fusion.24, pred[512]{0:T(512)(128)(4,1)S(1)} %broadcast_compare_fusion.1), kind=kOutput, calls=%fused_computation | convolution fusion | flops 672268288 | bytes 2624000 | tf_op jit(solution)/shard_map/dot_general | solution.py:213
  (34 shorter events, 0.6 us)
Async XLA Ops:
  0.0 16.6 %copy-start.2 = (bf16[512,320]{0,1:T(8,128)(2,1)S(1)}, bf16[512,320]{0,1:T(8,128)(2,1)}, u32[]{:S(2)}) copy-start(bf16[512,320]{0,1:T(8,128)(2,1)} %param.14) | copy-start | bytes 983044
  1.3 53.7 %all-to-all-start = ((s32[64,1,128]{2,1,0:T(1,128)}), s32[64,1,128]{2,1,0:T(1,128)S(1)}, u32[]{:S(2)}, u32[]{:S(2)}) async-start(s32[64,1,128]{2,1,0:T(1,128)} %broadcast_in_dim.32), calls=%async_computation | async-start | bytes 65536 | tf_op jit(solution)/shard_map/all_to_all | solution.py:240
  16.6 1.3 copy-start.3
  61.7 44.5 %all-to-all-start.1 = ((bf16[64,8,1280]{2,1,0:T(8,128)(2,1)}), bf16[64,8,1280]{2,1,0:T(8,128)(2,1)S(1)}, u32[]{:S(2)}, u32[]{:S(2)}) async-start(bf16[64,8,1280]{2,1,0:T(8,128)(2,1)} %fusion), calls=%async_computation.1 | async-start | bytes 2621440 | tf_op jit(solution)/shard_map/all_to_all | solution.py:259
  72.0 34.6 %copy-start.4 = (f32[1280]{0:T(1024)S(1)}, f32[1280]{0:T(1024)}, u32[]{:S(2)}) copy-start(f32[1280]{0:T(1024)} %param.18) | copy-start | bytes 15364
  106.8 4.9 %copy-start.1 = (bf16[128,1280]{1,0:T(8,128)(2,1)}, bf16[128,1280]{1,0:T(8,128)(2,1)S(1)}, u32[]{:S(2)}) copy-start(bf16[128,1280]{1,0:T(8,128)(2,1)S(1)} %multiply_convert_fusion.refs_0_) | copy-start | bytes 983044
  106.8 10.8 %collective-permute-start = (bf16[128,1280]{1,0:T(8,128)(2,1)S(1)}, bf16[128,1280]{1,0:T(8,128)(2,1)S(1)}, u32[]{:S(2)}, u32[]{:S(2)}) collective-permute-start(bf16[128,1280]{1,0:T(8,128)(2,1)S(1)} %multiply_convert_fusion.refs_0_), channel_id=1, source_target_pairs={{0,1},{1,2},{2,3},{3,0},{4,5},{5,6},{6,7},{7,4},{8,9},{9,10},{10,1... | collective-permute-start | bytes 983048 | tf_op jit(solution)/shard_map/ppermute | solution.py:196
  108.1 17.5 %collective-permute-start.1 = (bf16[128,1280]{1,0:T(8,128)(2,1)S(1)}, bf16[128,1280]{1,0:T(8,128)(2,1)S(1)}, u32[]{:S(2)}, u32[]{:S(2)}) collective-permute-start(bf16[128,1280]{1,0:T(8,128)(2,1)S(1)} %multiply_convert_fusion.refs_0_), channel_id=1, source_target_pairs={{0,2},{1,3},{2,0},{3,1},{4,6},{5,7},{6,4},{7,5},{8,10},{9,11},{10,... | collective-permute-start | bytes 983048 | tf_op jit(solution)/shard_map/ppermute | solution.py:196
  110.6 15.0 %collective-permute-start.2 = (bf16[128,1280]{1,0:T(8,128)(2,1)S(1)}, bf16[128,1280]{1,0:T(8,128)(2,1)S(1)}, u32[]{:S(2)}, u32[]{:S(2)}) collective-permute-start(bf16[128,1280]{1,0:T(8,128)(2,1)S(1)} %multiply_convert_fusion.refs_0_), channel_id=1, source_target_pairs={{0,3},{1,0},{2,1},{3,2},{4,7},{5,4},{6,5},{7,6},{8,11},{9,8},{10,9... | collective-permute-start | bytes 983048 | tf_op jit(solution)/shard_map/ppermute | solution.py:196
  117.5 8.0 %copy-start.5 = (bf16[128,1280]{1,0:T(8,128)(2,1)}, bf16[128,1280]{1,0:T(8,128)(2,1)S(1)}, u32[]{:S(2)}) copy-start(bf16[128,1280]{1,0:T(8,128)(2,1)S(1)} %collective-permute-done.refs_0_) | copy-start | bytes 983044
  125.6 0.7 copy-start.6
  126.3 0.7 copy-start.7
  134.7 18.8 %copy-start = (bf16[128,1280]{1,0:T(8,128)(2,1)S(1)}, bf16[128,1280]{1,0:T(8,128)(2,1)}, u32[]{:S(2)}) copy-start(bf16[128,1280]{1,0:T(8,128)(2,1)} %shard_map.110) | copy-start | bytes 983044
  135.9 9.9 %collective-permute-start.5 = (bf16[128,1280]{1,0:T(8,128)(2,1)S(1)}, bf16[128,1280]{1,0:T(8,128)(2,1)S(1)}, u32[]{:S(2)}, u32[]{:S(2)}) collective-permute-start(bf16[128,1280]{1,0:T(8,128)(2,1)S(1)} %get-tuple-element.20), channel_id=1, source_target_pairs={{0,1},{1,2},{2,3},{3,0},{4,5},{5,6},{6,7},{7,4},{8,9},{9,10},{10,1... | collective-permute-start | bytes 983048 | tf_op jit(solution)/shard_map/ppermute | solution.py:205
  136.0 17.0 %collective-permute-start.4 = (bf16[128,1280]{1,0:T(8,128)(2,1)S(1)}, bf16[128,1280]{1,0:T(8,128)(2,1)S(1)}, u32[]{:S(2)}, u32[]{:S(2)}) collective-permute-start(bf16[128,1280]{1,0:T(8,128)(2,1)S(1)} %get-tuple-element.21), channel_id=1, source_target_pairs={{0,2},{1,3},{2,0},{3,1},{4,6},{5,7},{6,4},{7,5},{8,10},{9,11},{10,... | collective-permute-start | bytes 983048 | tf_op jit(solution)/shard_map/ppermute | solution.py:205
  138.6 14.8 %collective-permute-start.3 = (bf16[128,1280]{1,0:T(8,128)(2,1)S(1)}, bf16[128,1280]{1,0:T(8,128)(2,1)S(1)}, u32[]{:S(2)}, u32[]{:S(2)}) collective-permute-start(bf16[128,1280]{1,0:T(8,128)(2,1)S(1)} %get-tuple-element.19), channel_id=1, source_target_pairs={{0,3},{1,0},{2,1},{3,2},{4,7},{5,4},{6,5},{7,6},{8,11},{9,8},{10,9... | collective-permute-start | bytes 983048 | tf_op jit(solution)/shard_map/ppermute | solution.py:205
  155.1 41.5 %all-to-all-start.2 = ((bf16[64,8,1280]{2,1,0:T(8,128)(2,1)}), bf16[64,8,1280]{2,1,0:T(8,128)(2,1)S(1)}, u32[]{:S(2)}, u32[]{:S(2)}) async-start(bf16[64,8,1280]{2,1,0:T(8,128)(2,1)} %fusion.1), calls=%async_computation.2 | async-start | bytes 2621440 | tf_op jit(solution)/shard_map/all_to_all | solution.py:272

commit v14 on v12

--- a/solution.py
+++ b/solution.py
@@ -238,7 +238,7 @@
     own_index = lax.axis_index("req")
     block_rows = slot_capacity // request_owners
     counts = lax.all_to_all(
-        jnp.broadcast_to(live_rows.reshape(1, 1), (request_owners, LANES)), "req", 0, 0, tiled=True
+        jnp.broadcast_to(live_rows.reshape(1, 1), (request_owners, 8)), "req", 0, 0, tiled=True
     )[:, 0]
     ends = jnp.cumsum(counts)
     firsts = ends - counts

time: 199 us -> 200 us (level)
  no operation moved by 1% of the time
where the time goes in v14:
time: 200 us
  waiting for transfers between devices  90.4 us (45%)
  Pallas kernels  45.9 us (23%)
  starting transfers between devices  39.2 us (20%)
  local copies, waits for them, and re-layouts  9.8 us (5%)
  matrix products  7.42 us (4%)
  other arithmetic  3.78 us (2%)
  between operations  3 us (2%)
    all_to_all x1, waiting for transfers between devices, on_device(): lax.all_to_all(outgoing.reshape(request_owners, block_rows, -1), 'req', 0...  34.1 us
    all_to_all x1, waiting for transfers between devices, on_device(): lax.all_to_all(outbound.reshape(request_owners, block_rows, -1), 'req', 0...  33.9 us
    pallas_call x1, Pallas kernels, attend(): pl.pallas_call(attention_kernel, grid=(tiles,), in_specs=[pl.BlockSpec((s...  33.1 us
    ppermute x3, waiting for transfers between devices, feed_forward(): lax.ppermute(part, 'grp', [(j, (j - k) % groups) for j in range(groups)])  13.7 us
    all_to_all x1, starting transfers between devices, on_device(): lax.all_to_all(jnp.broadcast_to(live_rows.reshape(1, 1), (request_owners,...  13.1 us
    pallas_call x2, Pallas kernels, ffn_rows(): pl.pallas_call(ffn_kernel, grid=(1,), in_specs=[pl.BlockSpec(b.shape, lam...  12.8 us
    all_to_all x1, starting transfers between devices, on_device(): lax.all_to_all(outbound.reshape(request_owners, block_rows, -1), 'req', 0...  10.3 us
    ppermute x3, waiting for transfers between devices, feed_forward(): lax.ppermute(normed, 'grp', [(j, (j + k) % groups) for j in range(groups)])  8.69 us
  transfers between devices with their start and end apart: 9, of which 7 were waited for; matrix products, arithmetic and copies ran while one was open for 4% of the time, Pallas kernels for 19%

profile of v14, /device:TPU:1, one launch (start us, length us, event | category | flops | bytes accessed | tf_op | source)
XLA Modules:
  0.0 199.5 jit_solution(4476997011179635497)
XLA Ops:
  0.7 0.6 broadcast_in_dim.32
  1.3 13.1 %all-to-all-start = ((s32[64,1,8]{2,1,0:T(1,128)}), s32[64,1,8]{2,1,0:T(1,128)S(1)}, u32[]{:S(2)}, u32[]{:S(2)}) async-start(s32[64,1,8]{2,1,0:T(1,128)} %broadcast_in_dim.32), calls=%async_computation | async-start | bytes 65536 | tf_op jit(solution)/shard_map/all_to_all | solution.py:240
  14.5 0.8 compare_reduce_fusion
  15.4 0.3 reduce-window.19
  15.8 0.1 slice_reduce_fusion
  16.0 0.6 iota_subtract_fusion.posr_ref
  16.6 0.3 multiply_sine_fusion
  17.0 1.0 broadcast_in_dim.37
  18.0 1.1 copy.31.k_ref
  19.1 1.1 copy.32.v_ref
  20.3 0.9 copy.33.cos_ref
  21.1 0.8 copy.34.sin_ref
  22.0 0.9 copy.35.segc_ref
  22.8 33.1 %shard_map.109 = bf16[512,1280]{1,0:T(8,128)(2,1)} custom-call(bf16[512,1280]{1,0:T(8,128)(2,1)} %q_ref.1, bf16[512,640]{1,0:T(8,128)(2,1)} %copy.31.k_ref, bf16[512,640]{1,0:T(8,128)(2,1)} %copy.32.v_ref, f32[512,128]{1,0:T(8,128)} %copy.33.cos_ref, f32[512,128]{1,0:T(8,128)} %copy.34.sin_ref, s32[512,1]{1,0:T(8,128)} %copy.35.segc_ref, s32[1,512]{1,0:T(1,128)} %bitcast.41, ...), custom_call_target="tpu_custom_call" | custom-call | tf_op jit(solution)/shard_map/pallas_call | solution.py:120
  56.0 0.1 slice_reduce_fusion.1
  56.1 0.1 reduce-window.18
  56.2 0.1 reduce
  56.3 0.7 fusion.34
  59.1 0.1 add_add_fusion
  59.2 0.1 add.226
  59.3 3.3 %fusion = bf16[64,8,1280]{2,1,0:T(8,128)(2,1)} fusion(bf16[512,1280]{1,0:T(8,128)(2,1)} %shard_map.109, s32[512]{0:T(512)S(1)} %add.226, pred[512]{0:T(512)(128)(4,1)S(1)} %broadcast_compare_fusion), kind=kOutput, calls=%fused_computation.3 | convolution fusion | flops 672268288 | bytes 2624000 | tf_op jit(solution)/shard_map/dot_general | solution.py:213
  62.6 10.3 %all-to-all-start.1 = ((bf16[64,8,1280]{2,1,0:T(8,128)(2,1)}), bf16[64,8,1280]{2,1,0:T(8,128)(2,1)S(1)}, u32[]{:S(2)}, u32[]{:S(2)}) async-start(bf16[64,8,1280]{2,1,0:T(8,128)(2,1)} %fusion), calls=%async_computation.1 | async-start | bytes 2621440 | tf_op jit(solution)/shard_map/all_to_all | solution.py:259
  73.0 0.1 convert_reduce_fusion
  73.1 0.1 select_reduce_fusion
  73.2 33.9 %all-to-all-done.1 = bf16[64,8,1280]{2,1,0:T(8,128)(2,1)S(1)} async-done(((bf16[64,8,1280]{2,1,0:T(8,128)(2,1)}), bf16[64,8,1280]{2,1,0:T(8,128)(2,1)S(1)}, u32[]{:S(2)}, u32[]{:S(2)}) %all-to-all-start.1) | async-done | bytes 1310752 | tf_op jit(solution)/shard_map/all_to_all | solution.py:259
  107.1 0.5 multiply_reduce_fusion
  107.6 0.1 multiply_convert_fusion.refs_0_
  107.7 1.3 collective-permute-start
  109.0 2.4 %collective-permute-start.1 = (bf16[128,1280]{1,0:T(8,128)(2,1)S(1)}, bf16[128,1280]{1,0:T(8,128)(2,1)S(1)}, u32[]{:S(2)}, u32[]{:S(2)}) collective-permute-start(bf16[128,1280]{1,0:T(8,128)(2,1)S(1)} %multiply_convert_fusion.refs_0_), channel_id=1, source_target_pairs={{0,2},{1,3},{2,0},{3,1},{4,6},{5,7},{6,4},{7,5},{8,10},{9,11},{10,... | collective-permute-start | bytes 983048 | tf_op jit(solution)/shard_map/ppermute | solution.py:196
  111.5 1.1 collective-permute-start.2
  112.6 5.2 %shard_map.110 = bf16[128,1280]{1,0:T(8,128)(2,1)} custom-call(bf16[128,1280]{1,0:T(8,128)(2,1)} %copy-done.1, bf16[1280,896]{1,0:T(8,128)(2,1)} %refs_3_.3, bf16[1280,896]{1,0:T(8,128)(2,1)} %refs_4_.1, bf16[896,1280]{1,0:T(8,128)(2,1)} %refs_5_.1), custom_call_target="tpu_custom_call" | custom-call | flops 880803840 | bytes 7536640 | tf_op jit(solution)/shard_map/pallas_call | solution.py:177
  117.8 0.7 collective-permute-done.refs_0_
  118.5 8.0 %collective-permute-done.1.refs_1_ = bf16[128,1280]{1,0:T(8,128)(2,1)S(1)} collective-permute-done((bf16[128,1280]{1,0:T(8,128)(2,1)S(1)}, bf16[128,1280]{1,0:T(8,128)(2,1)S(1)}, u32[]{:S(2)}, u32[]{:S(2)}) %collective-permute-start.1) | collective-permute-done | bytes 327712 | tf_op jit(solution)/shard_map/ppermute | solution.py:196
  126.5 0.7 copy-done.6
  127.2 0.7 copy-done.7
  127.9 7.6 %shard_map.111 = bf16[384,1280]{1,0:T(8,128)(2,1)} custom-call(bf16[128,1280]{1,0:T(8,128)(2,1)} %copy-done.5, bf16[128,1280]{1,0:T(8,128)(2,1)} %copy-done.6, bf16[128,1280]{1,0:T(8,128)(2,1)} %copy-done.7, bf16[1280,896]{1,0:T(8,128)(2,1)} %refs_3_.3, bf16[1280,896]{1,0:T(8,128)(2,1)} %refs_4_.1, bf16[896,1280]{1,0:T(8,128)(2,1)} %refs_5_.1), custom_call_target="tpu_custom_call" | custom-call | flops 2642411520 | bytes 8847360 | tf_op jit(solution)/shard_map/pallas_call | solution.py:177
  135.6 1.3 fusion.39
  136.9 2.6 %collective-permute-start.4 = (bf16[128,1280]{1,0:T(8,128)(2,1)S(1)}, bf16[128,1280]{1,0:T(8,128)(2,1)S(1)}, u32[]{:S(2)}, u32[]{:S(2)}) collective-permute-start(bf16[128,1280]{1,0:T(8,128)(2,1)S(1)} %get-tuple-element.21), channel_id=1, source_target_pairs={{0,2},{1,3},{2,0},{3,1},{4,6},{5,7},{6,4},{7,5},{8,10},{9,11},{10,... | collective-permute-start | bytes 983048 | tf_op jit(solution)/shard_map/ppermute | solution.py:205
  139.6 0.8 collective-permute-start.3
  140.5 0.1 lt.64
  140.6 0.1 add.219
  140.7 6.1 %collective-permute-done.5 = bf16[128,1280]{1,0:T(8,128)(2,1)S(1)} collective-permute-done((bf16[128,1280]{1,0:T(8,128)(2,1)S(1)}, bf16[128,1280]{1,0:T(8,128)(2,1)S(1)}, u32[]{:S(2)}, u32[]{:S(2)}) %collective-permute-start.5) | collective-permute-done | bytes 327712 | tf_op jit(solution)/shard_map/ppermute | solution.py:205
  146.7 7.2 %collective-permute-done.4 = bf16[128,1280]{1,0:T(8,128)(2,1)S(1)} collective-permute-done((bf16[128,1280]{1,0:T(8,128)(2,1)S(1)}, bf16[128,1280]{1,0:T(8,128)(2,1)S(1)}, u32[]{:S(2)}, u32[]{:S(2)}) %collective-permute-start.4) | collective-permute-done | bytes 327712 | tf_op jit(solution)/shard_map/ppermute | solution.py:205
  153.9 0.4 collective-permute-done.3
  154.3 1.6 fusion.1
  156.0 7.4 %all-to-all-start.2 = ((bf16[64,8,1280]{2,1,0:T(8,128)(2,1)}), bf16[64,8,1280]{2,1,0:T(8,128)(2,1)S(1)}, u32[]{:S(2)}, u32[]{:S(2)}) async-start(bf16[64,8,1280]{2,1,0:T(8,128)(2,1)} %fusion.1), calls=%async_computation.2 | async-start | bytes 2621440 | tf_op jit(solution)/shard_map/all_to_all | solution.py:272
  163.4 34.1 %all-to-all-done.2 = bf16[64,8,1280]{2,1,0:T(8,128)(2,1)S(1)} async-done(((bf16[64,8,1280]{2,1,0:T(8,128)(2,1)}), bf16[64,8,1280]{2,1,0:T(8,128)(2,1)S(1)}, u32[]{:S(2)}, u32[]{:S(2)}) %all-to-all-start.2) | async-done | bytes 1310752 | tf_op jit(solution)/shard_map/all_to_all | solution.py:272
  197.5 2.0 convolution_convert_fusion
  (36 shorter events, 0.7 us)
Async XLA Ops:
  0.0 19.1 %copy-start.2 = (bf16[512,320]{0,1:T(8,128)(2,1)S(1)}, bf16[512,320]{0,1:T(8,128)(2,1)}, u32[]{:S(2)}) copy-start(bf16[512,320]{0,1:T(8,128)(2,1)} %param.14) | copy-start | bytes 983044
  1.3 54.7 %all-to-all-start = ((s32[64,1,8]{2,1,0:T(1,128)}), s32[64,1,8]{2,1,0:T(1,128)S(1)}, u32[]{:S(2)}, u32[]{:S(2)}) async-start(s32[64,1,8]{2,1,0:T(1,128)} %broadcast_in_dim.32), calls=%async_computation | async-start | bytes 65536 | tf_op jit(solution)/shard_map/all_to_all | solution.py:240
  19.1 2.9 %copy-start.3 = (s32[1,1,512]{2,1,0:T(1,128)S(1)}, s32[1,1,512]{2,1,0:T(1,128)}, u32[]{:S(2)}) copy-start(s32[1,1,512]{2,1,0:T(1,128)} %param.15) | copy-start | bytes 6148
  62.6 44.4 %all-to-all-start.1 = ((bf16[64,8,1280]{2,1,0:T(8,128)(2,1)}), bf16[64,8,1280]{2,1,0:T(8,128)(2,1)S(1)}, u32[]{:S(2)}, u32[]{:S(2)}) async-start(bf16[64,8,1280]{2,1,0:T(8,128)(2,1)} %fusion), calls=%async_computation.1 | async-start | bytes 2621440 | tf_op jit(solution)/shard_map/all_to_all | solution.py:259
  73.0 34.6 %copy-start.4 = (f32[1280]{0:T(1024)S(1)}, f32[1280]{0:T(1024)}, u32[]{:S(2)}) copy-start(f32[1280]{0:T(1024)} %param.18) | copy-start | bytes 15364
  107.7 4.9 %copy-start.1 = (bf16[128,1280]{1,0:T(8,128)(2,1)}, bf16[128,1280]{1,0:T(8,128)(2,1)S(1)}, u32[]{:S(2)}) copy-start(bf16[128,1280]{1,0:T(8,128)(2,1)S(1)} %multiply_convert_fusion.refs_0_) | copy-start | bytes 983044
  107.7 10.7 %collective-permute-start = (bf16[128,1280]{1,0:T(8,128)(2,1)S(1)}, bf16[128,1280]{1,0:T(8,128)(2,1)S(1)}, u32[]{:S(2)}, u32[]{:S(2)}) collective-permute-start(bf16[128,1280]{1,0:T(8,128)(2,1)S(1)} %multiply_convert_fusion.refs_0_), channel_id=1, source_target_pairs={{0,1},{1,2},{2,3},{3,0},{4,5},{5,6},{6,7},{7,4},{8,9},{9,10},{10,1... | collective-permute-start | bytes 983048 | tf_op jit(solution)/shard_map/ppermute | solution.py:196
  109.0 17.4 %collective-permute-start.1 = (bf16[128,1280]{1,0:T(8,128)(2,1)S(1)}, bf16[128,1280]{1,0:T(8,128)(2,1)S(1)}, u32[]{:S(2)}, u32[]{:S(2)}) collective-permute-start(bf16[128,1280]{1,0:T(8,128)(2,1)S(1)} %multiply_convert_fusion.refs_0_), channel_id=1, source_target_pairs={{0,2},{1,3},{2,0},{3,1},{4,6},{5,7},{6,4},{7,5},{8,10},{9,11},{10,... | collective-permute-start | bytes 983048 | tf_op jit(solution)/shard_map/ppermute | solution.py:196
  111.5 15.0 %collective-permute-start.2 = (bf16[128,1280]{1,0:T(8,128)(2,1)S(1)}, bf16[128,1280]{1,0:T(8,128)(2,1)S(1)}, u32[]{:S(2)}, u32[]{:S(2)}) collective-permute-start(bf16[128,1280]{1,0:T(8,128)(2,1)S(1)} %multiply_convert_fusion.refs_0_), channel_id=1, source_target_pairs={{0,3},{1,0},{2,1},{3,2},{4,7},{5,4},{6,5},{7,6},{8,11},{9,8},{10,9... | collective-permute-start | bytes 983048 | tf_op jit(solution)/shard_map/ppermute | solution.py:196
  118.5 8.0 %copy-start.5 = (bf16[128,1280]{1,0:T(8,128)(2,1)}, bf16[128,1280]{1,0:T(8,128)(2,1)S(1)}, u32[]{:S(2)}) copy-start(bf16[128,1280]{1,0:T(8,128)(2,1)S(1)} %collective-permute-done.refs_0_) | copy-start | bytes 983044
  126.5 0.7 copy-start.6
  127.2 0.7 copy-start.7
  135.6 18.8 %copy-start = (bf16[128,1280]{1,0:T(8,128)(2,1)S(1)}, bf16[128,1280]{1,0:T(8,128)(2,1)}, u32[]{:S(2)}) copy-start(bf16[128,1280]{1,0:T(8,128)(2,1)} %shard_map.110) | copy-start | bytes 983044
  136.8 9.9 %collective-permute-start.5 = (bf16[128,1280]{1,0:T(8,128)(2,1)S(1)}, bf16[128,1280]{1,0:T(8,128)(2,1)S(1)}, u32[]{:S(2)}, u32[]{:S(2)}) collective-permute-start(bf16[128,1280]{1,0:T(8,128)(2,1)S(1)} %get-tuple-element.20), channel_id=1, source_target_pairs={{0,1},{1,2},{2,3},{3,0},{4,5},{5,6},{6,7},{7,4},{8,9},{9,10},{10,1... | collective-permute-start | bytes 983048 | tf_op jit(solution)/shard_map/ppermute | solution.py:205
  136.9 17.0 %collective-permute-start.4 = (bf16[128,1280]{1,0:T(8,128)(2,1)S(1)}, bf16[128,1280]{1,0:T(8,128)(2,1)S(1)}, u32[]{:S(2)}, u32[]{:S(2)}) collective-permute-start(bf16[128,1280]{1,0:T(8,128)(2,1)S(1)} %get-tuple-element.21), channel_id=1, source_target_pairs={{0,2},{1,3},{2,0},{3,1},{4,6},{5,7},{6,4},{7,5},{8,10},{9,11},{10,... | collective-permute-start | bytes 983048 | tf_op jit(solution)/shard_map/ppermute | solution.py:205
  139.6 14.8 %collective-permute-start.3 = (bf16[128,1280]{1,0:T(8,128)(2,1)S(1)}, bf16[128,1280]{1,0:T(8,128)(2,1)S(1)}, u32[]{:S(2)}, u32[]{:S(2)}) collective-permute-start(bf16[128,1280]{1,0:T(8,128)(2,1)S(1)} %get-tuple-element.19), channel_id=1, source_target_pairs={{0,3},{1,0},{2,1},{3,2},{4,7},{5,4},{6,5},{7,6},{8,11},{9,8},{10,9... | collective-permute-start | bytes 983048 | tf_op jit(solution)/shard_map/ppermute | solution.py:205
  156.0 41.5 %all-to-all-start.2 = ((bf16[64,8,1280]{2,1,0:T(8,128)(2,1)}), bf16[64,8,1280]{2,1,0:T(8,128)(2,1)S(1)}, u32[]{:S(2)}, u32[]{:S(2)}) async-start(bf16[64,8,1280]{2,1,0:T(8,128)(2,1)} %fusion.1), calls=%async_computation.2 | async-start | bytes 2621440 | tf_op jit(solution)/shard_map/all_to_all | solution.py:272
